TPU v7x, 512 devices: a whole 4x4x16 slice. The times are simulated.
512 devices in a mesh: par: 32 (over z, core), perp: 16 (over x, y).
Axes of the slice: x: 4, y: 4, z: 16, core: 2. Of those that a mesh axis runs over, the one named last changes fastest.
Arguments:
- fields: float32 [2, 32, 8192, 256], P(None, 'par', 'perp'), may hold values from -6 to 6
- weight_bank: float32 [8, 128, 128], replicated, may hold values from -1 to 2, as said below
- dest_slab: int32 [2, 32, 128, 1], P(None, 'par', 'perp'), may hold values from 0 to 15; in each aligned block of 8 rows (0 to 7, 8 to 15, ..., all dimensions but the last counted through in order) at most 2 rows name the same one
- dest_tile: int32 [2, 32, 128], P(None, 'par', 'perp'), may hold values from 0 to 7
- tile_blocks: int32 [2, 32, 128, 2], P(None, 'par', 'perp'), may hold values from 0 to 7
- band_terms: float32 [2, 32], replicated, may hold values from 0.45 to 0.49
Outputs:
- gradient: float32 [2, 32, 8192, 256], P(None, 'par', 'perp')
Inputs may be any that keep to these rules, and one draw needn't show every extreme that they name: `dest_slab`: in each direction and plane, at most 2 of the 8 tiles of one slab name the same destination slab, and in some slab exactly 2 do. `weight_bank`: each block is a dense real matrix.
All inputs are finite; a program needn't handle non-finite values.
Results may differ from a plain program's by a relative error of at most 0.0003.
Values sent between devices are 32-bit elements; how exact they have to be, the bound alone decides.
No kernel may reach another device: no remote copies, remote signals or barrier semaphores. Data moves between devices by JAX's collectives and lax.ppermute only.
A program may use at most 64 MiB of HBM per device.

v0:
```python
import jax
import jax.numpy as jnp
from jax import lax
from jax.sharding import PartitionSpec as P

TILE = 128


PRECISE = lax.Precision.HIGHEST
KAPPA = 0.125


def extended(block, sides, width):
    for axis, dim in sides:
        count = lax.axis_size(axis)
        forward = [(i, i + 1) for i in range(count - 1)]
        backward = [(target, source) for source, target in forward]
        low = lax.ppermute(
            lax.slice_in_dim(block, block.shape[dim] - width, None, axis=dim), axis, forward
        )
        high = lax.ppermute(lax.slice_in_dim(block, 0, width, axis=dim), axis, backward)
        block = jnp.concatenate([low, block, high], axis=dim)
    return block


def split_tiles(plane_pair):
    field_count, row_count, col_count = plane_pair.shape
    shaped = plane_pair.reshape(field_count, row_count // TILE, TILE, col_count // TILE, TILE)
    return shaped.transpose(0, 1, 3, 2, 4).reshape(field_count, -1, TILE, TILE)


def join_tiles(tile_set, row_count, col_count):
    field_count = tile_set.shape[0]
    shaped = tile_set.reshape(field_count, row_count // TILE, col_count // TILE, TILE, TILE)
    return shaped.transpose(0, 1, 3, 2, 4).reshape(field_count, row_count, col_count)


def coefficients(band_terms):
    plane_total = band_terms.shape[1]
    lower, pivots, ratios = [], [], []
    previous = jnp.zeros((), jnp.float32)
    for p in range(plane_total):
        lower_now = band_terms[0, p] if p > 0 else jnp.zeros((), jnp.float32)
        upper_now = band_terms[1, p] if p < plane_total - 1 else jnp.zeros((), jnp.float32)
        pivot_now = 1.0 - lower_now * previous
        ratio_now = upper_now / pivot_now
        lower.append(lower_now)
        pivots.append(pivot_now)
        ratios.append(ratio_now)
        previous = ratio_now
    return lower, pivots, ratios


def slot_labels(dest_slabs, target, peer_count, capacity):
    tile_count = dest_slabs.shape[-1]
    position = jnp.arange(tile_count, dtype=jnp.int32)
    earlier = position[:, None] > position[None, :]
    shared = dest_slabs[..., :, None] == dest_slabs[..., None, :]
    slot_rank = jnp.sum((shared & earlier).astype(jnp.int32), axis=-1)
    peer_ids = jnp.arange(peer_count, dtype=jnp.int32)
    slot_ids = jnp.arange(capacity, dtype=jnp.int32)
    chosen = (dest_slabs[..., None, None, :] == peer_ids[:, None, None]) & (
        slot_rank[..., None, None, :] == slot_ids[None, :, None]
    )
    return chosen


def local(fields, weight_bank, dest_slab, dest_tile, tile_blocks, band_terms):
    peer_count = lax.axis_size("perp")
    plane_count = lax.axis_size("par")
    row_count = fields.shape[2]
    col_count = fields.shape[3]
    local_pair = fields[:, 0]
    tile_set = split_tiles(local_pair)
    tile_count = tile_set.shape[1]
    capacity = max(2, (tile_count + peer_count - 1) // peer_count)
    dest_slabs = dest_slab[:, 0, :, 0]
    target = dest_tile[:, 0, :]
    left_index = tile_blocks[:, 0, :, 0]
    right_index = tile_blocks[:, 0, :, 1]

    left_block = jnp.take(weight_bank, left_index, axis=0, mode="clip")
    right_block = jnp.take(weight_bank, right_index, axis=0, mode="clip")
    shifted = jnp.einsum("dsij,dsjk->dsik", left_block, tile_set, precision=PRECISE)
    moved = jnp.einsum("dsik,dslk->dsil", shifted, right_block, precision=PRECISE)

    chosen = slot_labels(dest_slabs, target, peer_count, capacity)
    picker = chosen.astype(jnp.float32)
    packed = jnp.einsum("dpcs,dsij->dpcij", picker, moved, precision=PRECISE)
    moved_tiles = lax.all_to_all(packed, "perp", split_axis=1, concat_axis=1, tiled=True)

    all_slabs = lax.all_gather(dest_slabs, "perp", axis=1, tiled=True)
    all_targets = lax.all_gather(target, "perp", axis=1, tiled=True)
    field_count = all_slabs.shape[0]
    all_slabs = all_slabs.reshape(field_count, peer_count, tile_count)
    all_targets = all_targets.reshape(field_count, peer_count, tile_count)
    source_chosen = slot_labels(all_slabs, all_targets, peer_count, capacity)
    me = lax.axis_index("perp")
    mine = source_chosen[:, :, me]
    arrived_target = (
        jnp.sum(mine.astype(jnp.int32) * (all_targets[:, :, None, :] + 1), axis=-1) - 1
    )
    position = jnp.arange(tile_count, dtype=jnp.int32)
    flattened = moved_tiles.reshape(field_count, peer_count * capacity, TILE, TILE)
    flat_target = arrived_target.reshape(field_count, peer_count * capacity)
    landing = (flat_target[:, None, :] == position[None, :, None]).astype(jnp.float32)
    summed = jnp.einsum("dts,dsij->dtij", landing, flattened, precision=PRECISE)
    deposit = join_tiles(summed, row_count, col_count)

    upward = [(i, i + 1) for i in range(plane_count - 1)]
    downward = [(i + 1, i) for i in range(plane_count - 1)]
    mapped = jnp.stack(
        (lax.ppermute(deposit[0], "par", upward), lax.ppermute(deposit[1], "par", downward))
    )
    rimmed = extended(mapped, (("perp", 1),), 1)
    padded = jnp.pad(rimmed, ((0, 0), (0, 0), (1, 1)))
    beside_all = (
        padded[:, 2:, 1:-1] + padded[:, :-2, 1:-1] + padded[:, 1:-1, 2:] + padded[:, 1:-1, :-2]
    )
    smoothed = mapped + KAPPA * (beside_all - 4.0 * mapped)
    orient = jnp.array([1.0, -1.0], jnp.float32)[:, None, None]
    right_side = orient * (local_pair - smoothed)
    lower, pivots, ratios = coefficients(band_terms)
    column_block = lax.all_to_all(
        right_side[:, None], "par", split_axis=2, concat_axis=1, tiled=True
    )
    depth_count = column_block.shape[1]
    eliminated = []
    previous = None
    for p in range(depth_count):
        current = column_block[:, p]
        if previous is not None:
            current = current - lower[p] * previous
        current = current / pivots[p]
        eliminated.append(current)
        previous = current
    solved = [None] * depth_count
    following = None
    for p in reversed(range(depth_count)):
        current = eliminated[p]
        if following is not None:
            current = current - ratios[p] * following
        solved[p] = current
        following = current
    solved = jnp.stack(solved, axis=1)
    result = lax.all_to_all(solved, "par", split_axis=1, concat_axis=2, tiled=True)
    return result


def solution(mesh):
    placed = (
        P(None, "par", "perp", None),
        P(),
        P(None, "par", "perp", None),
        P(None, "par", "perp"),
        P(None, "par", "perp", None),
        P(),
    )
    return jax.shard_map(
        local, mesh=mesh, in_specs=placed, out_specs=P(None, "par", "perp", None), check_vma=False
    )
```

profile of v0, /device:TPU:6, one launch (start us, length us, event | category | flops | bytes accessed | tf_op | source)
XLA Modules:
  0.0 322.5 jit_solution(12230348033059756992)
XLA Ops:
  0.0 0.0 copy-start
  0.0 0.8 slice_reduce_fusion
  0.8 0.1 reshape.112
  0.9 0.1 reshape.104
  1.0 1.7 reshape_squeeze.3
  2.7 0.1 copy.171
  2.8 0.0 copy-done
  2.8 0.0 copy-start.4
  2.8 0.6 gather_fusion
  3.5 1.6 gather_fusion.1
  5.1 0.0 copy-done.4
  5.1 0.1 iota_compare_fusion.2
  5.1 0.2 convert_reduce_fusion.1
  5.4 1.2 fusion.71
  6.5 2.3 convolution_bitcast_fusion
  8.8 2.1 fusion.7
  10.9 3.2 %copy.173 = f32[2,16,2,128,128]{4,3,2,0,1:T(8,128)} copy(f32[2,16,2,128,128]{4,1,3,2,0:T(8,128)S(1)} %fusion.7) | data formatting | bytes 8388608 | tf_op jit(solution)/shard_map/dpcs,dsij->dpcij/dot_general | solution.py:89
  14.2 10.3 %all-to-all-start = ((f32[2,16,2,128,128]{4,3,2,0,1:T(8,128)}), f32[2,16,2,128,128]{4,3,2,0,1:T(8,128)}, u32[]{:S(2)}, u32[]{:S(2)}) async-start(f32[2,16,2,128,128]{4,3,2,0,1:T(8,128)} %copy.173), calls=%async_computation | async-start | bytes 8388608 | tf_op jit(solution)/shard_map/all_to_all | solution.py:90
  24.5 0.1 copy.162
  24.5 0.1 copy.167
  24.6 63.9 %all-gather.1 = s32[2,1,128]{0,1,2:T(1,128)S(1)} all-gather(s32[2,1,8]{0,1,2:T(1,128)S(1)} %copy.167), channel_id=3, replica_groups=mesh['par'=32,'perp'=16] {'perp'}, dimensions={2}, use_global_device_ids=true | all-gather | bytes 1088 | tf_op jit(solution)/shard_map/all_gather | solution.py:93
  88.5 0.1 copy.168
  88.6 0.1 add.40
  88.7 0.1 copy.169
  88.8 22.1 %all-gather = s32[2,1,128,1]{0,3,1,2:T(1,128)S(1)} all-gather(s32[2,1,8,1]{0,3,1,2:T(1,128)S(1)} %copy.162), channel_id=2, replica_groups=mesh['par'=32,'perp'=16] {'perp'}, dimensions={2}, use_global_device_ids=true | all-gather | bytes 1088 | tf_op jit(solution)/shard_map/all_gather | solution.py:92
  110.9 0.1 copy.164
  111.0 0.1 convert_reduce_fusion
  111.2 0.1 copy.170
  111.3 0.1 sub.1780
  111.4 0.0 all-to-all-done
  111.4 2.5 copy.174
  113.8 3.9 %fusion = f32[2,8,128,128]{3,1,2,0:T(8,128)S(1)} fusion(f32[2,32,128,128]{3,2,1,0:T(8,128)S(1)} %bitcast.114, s32[2,32]{1,0:T(2,128)S(1)} %sub.1780), kind=kOutput, calls=%fused_computation.2 | convolution fusion | flops 100663808 | bytes 5243136 | tf_op jit(solution)/shard_map/dts,dsij->dtij/dot_general | solution.py:107
  117.7 0.4 fusion.66
  118.0 0.2 copy.176
  118.3 1.3 collective-permute-start
  119.6 0.2 copy.177
  119.8 1.3 collective-permute-start.1
  121.1 0.0 collective-permute-done
  121.2 0.4 stack.8
  121.5 16.2 %collective-permute-done.1 = f32[512,256]{1,0:T(8,128)S(1)} collective-permute-done((f32[512,256]{1,0:T(8,128)S(1)}, f32[512,256]{1,0:T(8,128)S(1)}, u32[]{:S(2)}, u32[]{:S(2)}) %collective-permute-start.1) | collective-permute-done | bytes 524320 | tf_op jit(solution)/shard_map/ppermute | solution.py:113
  137.7 0.4 stack.9
  138.1 0.0 copy-start.2
  138.1 0.0 copy-start.6
  138.1 3.8 %collective-permute-start.2 = (f32[2,1,256]{2,0,1:T(2,128)S(1)}, f32[2,1,256]{2,0,1:T(2,128)S(1)}, u32[]{:S(2)}, u32[]{:S(2)}) collective-permute-start(f32[2,1,256]{2,0,1:T(2,128)S(1)} %get-tuple-element.71), channel_id=1, source_target_pairs={{1,0},{2,1},{3,2},{4,3},{5,4},{6,5},{7,6},{8,7},{9,8},{10,9},{11,1... | collective-permute-start | bytes 6152 | tf_op jit(solution)/shard_map/ppermute | solution.py:21
  141.9 2.5 collective-permute-start.3
  144.3 0.0 collective-permute-done.2
  144.4 5.1 %collective-permute-done.3 = f32[2,1,256]{2,0,1:T(2,128)S(1)} collective-permute-done((f32[2,1,256]{2,0,1:T(2,128)S(1)}, f32[2,1,256]{2,0,1:T(2,128)S(1)}, u32[]{:S(2)}, u32[]{:S(2)}) %collective-permute-start.3) | collective-permute-done | bytes 2080 | tf_op jit(solution)/shard_map/ppermute | solution.py:18
  149.5 5.3 %select_maximum_fusion = f32[2,514,258]{2,0,1:T(2,128)S(1)} fusion(f32[2,1,256]{2,0,1:T(2,128)S(1)} %collective-permute-done.2, f32[2,1,256]{2,0,1:T(2,128)S(1)} %collective-permute-done.3, f32[1,512,256]{2,0,1:T(1,128)S(1)} %stack.9, f32[1,512,256]{2,0,1:T(1,128)S(1)} %stack.8), kind=kLoop, calls=%fused_computation.5 | loop fusion | flops 2652240 | bytes 2113568 | tf_op jit(solution)/shard_map/concatenate | solution.py:22
  154.7 0.0 copy-done.2
  154.7 0.0 copy-done.6
  154.7 6.2 %multiply_bitcast_fusion = f32[2,1,512,256]{3,0,1,2:T(2,128)} fusion(f32[2,514,258]{2,0,1:T(2,128)S(1)} %select_maximum_fusion, f32[1,512,256]{2,0,1:T(1,128)S(1)} %stack.9, f32[1,512,256]{2,0,1:T(1,128)S(1)} %stack.8, f32[2,1,256]{2,0,1:T(2,128)S(1)} %collective-permute-done.3, f32[2,1,256]{2,0,1:T(2,128)S(1)} %collective-permute-done.2, ...), kind=kLoop, calls=%fused_computation.27 | loop fusion | flops 3670016 | bytes 5246984 | tf_op jit(solution)/shard_map/broadcast_in_dim | solution.py:125
  161.0 22.1 %all-to-all-start.1 = ((f32[2,1,512,256]{3,0,1,2:T(2,128)}), f32[2,1,512,256]{3,0,1,2:T(2,128)S(1)}, u32[]{:S(2)}, u32[]{:S(2)}) async-start(f32[2,1,512,256]{3,0,1,2:T(2,128)} %multiply_bitcast_fusion), calls=%async_computation.1 | async-start | bytes 2097152 | tf_op jit(solution)/shard_map/all_to_all | solution.py:124
  183.1 0.7 fusion.70
  186.8 0.7 fusion.69
  199.0 0.7 fusion.68
  211.1 0.7 fusion.67
  224.9 14.0 %all-to-all-done.1 = f32[2,1,512,256]{3,0,1,2:T(2,128)S(1)} async-done(((f32[2,1,512,256]{3,0,1,2:T(2,128)}), f32[2,1,512,256]{3,0,1,2:T(2,128)S(1)}, u32[]{:S(2)}, u32[]{:S(2)}) %all-to-all-start.1) | async-done | bytes 1048608 | tf_op jit(solution)/shard_map/all_to_all | solution.py:124
  238.9 0.2 fusion.65
  239.0 0.2 fusion.64
  239.3 20.9 %constant_dynamic-update-slice_fusion.31 = (f32[2,32,16,256]{3,2,0,1:T(8,128)S(1)}, f32[2,1,16,256]{3,2,0,1:T(8,128)S(1)}, f32[2,1,16,256]{3,2,0,1:T(8,128)S(1)}...) fusion(f32[2,1,16,256]{3,0,2,1:T(2,128)S(1)} %get-tuple-element, ...), kind=kLoop, calls=%fused_computation.62 | loop fusion | flops 1269759 | bytes 2064756
  260.6 0.6 constant_dynamic-update-slice_fusion.1
  261.3 0.6 constant_dynamic-update-slice_fusion
  261.9 59.5 %all_to_all.29 = f32[2,32,16,256]{3,2,0,1:T(8,128)S(1)} all-to-all(f32[2,32,16,256]{3,2,0,1:T(8,128)S(1)} %constant_dynamic-update-slice_fusion), channel_id=1, replica_groups=mesh['par'=32,'perp'=16] {'par'}, dimensions={1} | all-to-all | bytes 2097152 | tf_op jit(solution)/shard_map/all_to_all | solution.py:146
  321.4 1.1 copy.210
  (47 shorter events, 0.4 us)
Async XLA Ops:
  0.0 2.8 copy-start
  2.8 2.2 copy-start.4
  5.1 1.4 copy-start.1
  14.2 10.4 %copy-start.5 = (s32[2,1,8]{2,1,0:T(1,128)S(1)}, s32[2,1,8]{2,1,0:T(1,128)}, u32[]{:S(2)}) copy-start(s32[2,1,8]{2,1,0:T(1,128)} %param.10) | copy-start | bytes 196
  14.2 97.2 %all-to-all-start = ((f32[2,16,2,128,128]{4,3,2,0,1:T(8,128)}), f32[2,16,2,128,128]{4,3,2,0,1:T(8,128)}, u32[]{:S(2)}, u32[]{:S(2)}) async-start(f32[2,16,2,128,128]{4,3,2,0,1:T(8,128)} %copy.173), calls=%async_computation | async-start | bytes 8388608 | tf_op jit(solution)/shard_map/all_to_all | solution.py:90
  118.3 2.9 collective-permute-start
  119.8 17.8 %collective-permute-start.1 = (f32[512,256]{1,0:T(8,128)S(1)}, f32[512,256]{1,0:T(8,128)S(1)}, u32[]{:S(2)}, u32[]{:S(2)}) collective-permute-start(f32[512,256]{1,0:T(8,128)S(1)} %bitcast.125), channel_id=1, source_target_pairs={{16,0},{32,16},{48,32},{64,48},{80,64},{96,80},{112,96},{128,112},... | collective-permute-start | bytes 1572872 | tf_op jit(solution)/shard_map/ppermute | solution.py:113
  138.1 16.7 %copy-start.2 = (f32[2,1,512,256]{3,2,1,0:T(8,128)S(1)}, f32[2,1,512,256]{3,2,1,0:T(8,128)}, u32[]{:S(2)}) copy-start(f32[2,1,512,256]{3,2,1,0:T(8,128)} %param.7) | copy-start | bytes 3145732
  138.1 16.7 %copy-start.6 = (f32[2]{0:T(128)S(1)}, f32[2]{0:T(128)}, u32[]{:S(2)}) copy-start(f32[2]{0:T(128)} %constant.25.clone) | copy-start | bytes 28
  138.1 6.3 %collective-permute-start.2 = (f32[2,1,256]{2,0,1:T(2,128)S(1)}, f32[2,1,256]{2,0,1:T(2,128)S(1)}, u32[]{:S(2)}, u32[]{:S(2)}) collective-permute-start(f32[2,1,256]{2,0,1:T(2,128)S(1)} %get-tuple-element.71), channel_id=1, source_target_pairs={{1,0},{2,1},{3,2},{4,3},{5,4},{6,5},{7,6},{8,7},{9,8},{10,9},{11,1... | collective-permute-start | bytes 6152 | tf_op jit(solution)/shard_map/ppermute | solution.py:21
  141.9 7.6 %collective-permute-start.3 = (f32[2,1,256]{2,0,1:T(2,128)S(1)}, f32[2,1,256]{2,0,1:T(2,128)S(1)}, u32[]{:S(2)}, u32[]{:S(2)}) collective-permute-start(f32[2,1,256]{2,0,1:T(2,128)S(1)} %get-tuple-element.70), channel_id=1, source_target_pairs={{0,1},{1,2},{2,3},{3,4},{4,5},{5,6},{6,7},{7,8},{8,9},{9,10},{10,1... | collective-permute-start | bytes 6152 | tf_op jit(solution)/shard_map/ppermute | solution.py:18
  161.0 22.1 %copy-start.3 = (f32[2,32]{1,0:T(2,128)S(1)}, f32[2,32]{1,0:T(2,128)}, u32[]{:S(2)}) copy-start(f32[2,32]{1,0:T(2,128)} %param.12) | copy-start | bytes 772
  161.0 77.9 %all-to-all-start.1 = ((f32[2,1,512,256]{3,0,1,2:T(2,128)}), f32[2,1,512,256]{3,0,1,2:T(2,128)S(1)}, u32[]{:S(2)}, u32[]{:S(2)}) async-start(f32[2,1,512,256]{3,0,1,2:T(2,128)} %multiply_bitcast_fusion), calls=%async_computation.1 | async-start | bytes 2097152 | tf_op jit(solution)/shard_map/all_to_all | solution.py:124
where the time goes:
time: 326 us; the launch traced here: 322 us
  blocking collectives  145 us (44%)
  starting transfers between devices  41.3 us (13%)
  between operations  39.5 us (12%)
  waiting for transfers between devices  35.3 us (11%)
  other arithmetic  34.2 us (10%)
  local copies, waits for them, and re-layouts  17.3 us (5%)
  matrix products  9.38 us (3%)
    all_gather x1, blocking collectives, local(): all_targets = lax.all_gather(target, 'perp', axis=1, tiled=True)  63.9 us
    all_to_all x1, blocking collectives, local(): lax.all_to_all(solved, 'par', split_axis=1, concat_axis=2, tiled=True)  59.5 us
    all_to_all x1, starting transfers between devices, local(): lax.all_to_all(right_side[:, None], 'par', split_axis=2, concat_axis=1, t...  22.1 us
    all_gather x1, blocking collectives, local(): all_slabs = lax.all_gather(dest_slabs, 'perp', axis=1, tiled=True)  22.1 us
    unnamed x16, other arithmetic  21.7 us
    ppermute x1, waiting for transfers between devices, local(): lax.ppermute(deposit[1], 'par', downward)  16.2 us
    all_to_all x1, waiting for transfers between devices, local(): lax.all_to_all(right_side[:, None], 'par', split_axis=2, concat_axis=1, t...  14 us
    all_to_all x1, starting transfers between devices, local(): lax.all_to_all(packed, 'perp', split_axis=1, concat_axis=1, tiled=True)  10.3 us
  transfers between devices with their start and end apart: 6, of which 3 were waited for; matrix products, arithmetic and copies ran while one was open for 1% of the time, Pallas kernels for 0%

commit v1 on v0

--- a/solution.py
+++ b/solution.py
@@ -1,6 +1,8 @@
 import jax
 import jax.numpy as jnp
 from jax import lax
+from jax.experimental import pallas as pl
+from jax.experimental.pallas import tpu as pltpu
 from jax.sharding import PartitionSpec as P
 
 TILE = 128
@@ -65,6 +67,30 @@
     return chosen
 
 
+def thomas_kernel(lower_ref, pivot_ref, ratio_ref, rhs_ref, out_ref):
+    depth = rhs_ref.shape[1]
+    previous = rhs_ref[:, 0] / pivot_ref[0]
+    out_ref[:, 0] = previous
+    for p in range(1, depth):
+        previous = (rhs_ref[:, p] - lower_ref[p] * previous) / pivot_ref[p]
+        out_ref[:, p] = previous
+    following = previous
+    for p in reversed(range(depth - 1)):
+        following = out_ref[:, p] - ratio_ref[p] * following
+        out_ref[:, p] = following
+
+
+def thomas(rhs, lower, pivots, ratios):
+    scalar = pl.BlockSpec(memory_space=pltpu.SMEM)
+    whole = pl.BlockSpec(memory_space=pltpu.VMEM)
+    return pl.pallas_call(
+        thomas_kernel,
+        out_shape=jax.ShapeDtypeStruct(rhs.shape, rhs.dtype),
+        in_specs=[scalar, scalar, scalar, whole],
+        out_specs=whole,
+    )(lower, pivots, ratios, rhs)
+
+
 def local(fields, weight_bank, dest_slab, dest_tile, tile_blocks, band_terms):
     peer_count = lax.axis_size("perp")
     plane_count = lax.axis_size("par")
@@ -89,17 +115,9 @@
     packed = jnp.einsum("dpcs,dsij->dpcij", picker, moved, precision=PRECISE)
     moved_tiles = lax.all_to_all(packed, "perp", split_axis=1, concat_axis=1, tiled=True)
 
-    all_slabs = lax.all_gather(dest_slabs, "perp", axis=1, tiled=True)
-    all_targets = lax.all_gather(target, "perp", axis=1, tiled=True)
-    field_count = all_slabs.shape[0]
-    all_slabs = all_slabs.reshape(field_count, peer_count, tile_count)
-    all_targets = all_targets.reshape(field_count, peer_count, tile_count)
-    source_chosen = slot_labels(all_slabs, all_targets, peer_count, capacity)
-    me = lax.axis_index("perp")
-    mine = source_chosen[:, :, me]
-    arrived_target = (
-        jnp.sum(mine.astype(jnp.int32) * (all_targets[:, :, None, :] + 1), axis=-1) - 1
-    )
+    slot_target = jnp.sum(chosen.astype(jnp.int32) * (target[:, None, None, :] + 1), axis=3) - 1
+    arrived_target = lax.all_to_all(slot_target, "perp", split_axis=1, concat_axis=1, tiled=True)
+    field_count = tile_set.shape[0]
     position = jnp.arange(tile_count, dtype=jnp.int32)
     flattened = moved_tiles.reshape(field_count, peer_count * capacity, TILE, TILE)
     flat_target = arrived_target.reshape(field_count, peer_count * capacity)
@@ -124,25 +142,7 @@
     column_block = lax.all_to_all(
         right_side[:, None], "par", split_axis=2, concat_axis=1, tiled=True
     )
-    depth_count = column_block.shape[1]
-    eliminated = []
-    previous = None
-    for p in range(depth_count):
-        current = column_block[:, p]
-        if previous is not None:
-            current = current - lower[p] * previous
-        current = current / pivots[p]
-        eliminated.append(current)
-        previous = current
-    solved = [None] * depth_count
-    following = None
-    for p in reversed(range(depth_count)):
-        current = eliminated[p]
-        if following is not None:
-            current = current - ratios[p] * following
-        solved[p] = current
-        following = current
-    solved = jnp.stack(solved, axis=1)
+    solved = thomas(column_block, jnp.stack(lower), jnp.stack(pivots), jnp.stack(ratios))
     result = lax.all_to_all(solved, "par", split_axis=1, concat_axis=2, tiled=True)
     return result
 

time: 326 us -> 289 us (0.89)
  blocking collectives: 145 us -> 68 us
  local copies, waits for them, and re-layouts: 17.3 us -> 43 us
  waiting for transfers between devices: 35.3 us -> 60.8 us
  other arithmetic: 34.2 us -> 14 us
  starting transfers between devices: 41.3 us -> 49.4 us
    all_gather x2 -> x0, blocking collectives: 86 us -> none  [the longest x1 63.9 us: local(): all_targets = lax.all_gather(target, 'perp', axis=1, tiled=True)]
    all_to_all x1, waiting for transfers between devices: 0.01 us -> 49.4 us  [local(): lax.all_to_all(packed, 'perp', split_axis=1, concat_axis=1, tiled=True)]
    another operation x0 -> x3, local copies, waits for them, and re-layouts: none -> 22.5 us  [the longest x1 20.6 us: local(): jnp.stack(lower)]
    unnamed x16 -> x0, other arithmetic: 21.7 us -> none
    all_to_all x1, waiting for transfers between devices: 14 us -> 0.01 us  [local(): lax.all_to_all(right_side[:, None], 'par', split_axis=2, concat_axis=1, t...]
    all_to_all x0 -> x1, starting transfers between devices: none -> 9.16 us  [local(): lax.all_to_all(slot_target, 'perp', split_axis=1, concat_axis=1, tiled=True)]
    all_to_all x1, blocking collectives: 59.5 us -> 68 us  [local(): lax.all_to_all(solved, 'par', split_axis=1, concat_axis=2, tiled=True)]
    ppermute x1, waiting for transfers between devices: 16.2 us -> 9.89 us  [local(): lax.ppermute(deposit[1], 'par', downward)]
  transfers between devices with their start and end apart: 6 -> 7, of which waited for: 3 -> 4; matrix products, arithmetic and copies ran while one was open for 1% -> 14% of each run, Pallas kernels for 0% -> 0%
where the time goes in v1:
time: 289 us; the launch traced here: 286 us
  blocking collectives  68 us (24%)
  waiting for transfers between devices  60.8 us (21%)
  starting transfers between devices  49.4 us (17%)
  local copies, waits for them, and re-layouts  43 us (15%)
  between operations  39.1 us (14%)
  other arithmetic  14 us (5%)
  matrix products  9.34 us (3%)
    all_to_all x1, blocking collectives, local(): lax.all_to_all(solved, 'par', split_axis=1, concat_axis=2, tiled=True)  68 us
    all_to_all x1, waiting for transfers between devices, local(): lax.all_to_all(packed, 'perp', split_axis=1, concat_axis=1, tiled=True)  49.4 us
    all_to_all x1, starting transfers between devices, local(): lax.all_to_all(right_side[:, None], 'par', split_axis=2, concat_axis=1, t...  21.8 us
    another operation x1, local copies, waits for them, and re-layouts, local(): jnp.stack(lower)  20.6 us
    ppermute x1, waiting for transfers between devices, local(): lax.ppermute(deposit[1], 'par', downward)  9.89 us
    all_to_all x1, starting transfers between devices, local(): lax.all_to_all(slot_target, 'perp', split_axis=1, concat_axis=1, tiled=True)  9.16 us
    all_to_all x1, starting transfers between devices, local(): lax.all_to_all(packed, 'perp', split_axis=1, concat_axis=1, tiled=True)  7.22 us
    ppermute x1, starting transfers between devices, extended(): lax.ppermute(lax.slice_in_dim(block, 0, width, axis=dim), axis, backward)  6.56 us
  transfers between devices with their start and end apart: 7, of which 4 were waited for; matrix products, arithmetic and copies ran while one was open for 14% of the time, Pallas kernels for 0%

profile of v1, /device:TPU:6, one launch (start us, length us, event | category | flops | bytes accessed | tf_op | source)
XLA Modules:
  0.0 286.1 jit_solution(11405825891281282597)
XLA Ops:
  0.0 0.0 copy-start
  0.0 0.7 broadcast_add_fusion.1
  0.8 0.8 iota_compare_fusion.1
  1.5 1.0 convert_reduce_fusion
  2.5 0.1 fusion.9
  2.6 0.7 copy.50
  3.3 9.2 %all-to-all-start = ((s32[2,16,2]{2,0,1:T(2,128)}), s32[2,16,2]{2,0,1:T(2,128)S(1)}, u32[]{:S(2)}, u32[]{:S(2)}) async-start(s32[2,16,2]{2,0,1:T(2,128)} %copy.50), calls=%async_computation | async-start | bytes 32768 | tf_op jit(solution)/shard_map/all_to_all | solution.py:119
  12.4 0.8 slice_reduce_fusion
  13.2 0.1 reshape.93
  13.3 0.1 reshape.85
  13.4 0.0 copy-done
  13.4 0.6 gather_fusion.1
  14.0 0.6 gather_fusion
  14.6 2.7 reshape_squeeze.3
  17.4 1.3 copy.52
  18.7 1.1 fusion.22
  19.9 2.3 convolution_bitcast_fusion
  22.2 2.1 fusion.7
  24.2 3.2 %copy.54 = f32[2,16,2,128,128]{4,3,2,0,1:T(8,128)} copy(f32[2,16,2,128,128]{4,1,3,2,0:T(8,128)S(1)} %fusion.7) | data formatting | bytes 8388608 | tf_op jit(solution)/shard_map/dpcs,dsij->dpcij/dot_general | solution.py:115
  27.5 0.0 all-to-all-done
  27.5 7.2 %all-to-all-start.1 = ((f32[2,16,2,128,128]{4,3,2,0,1:T(8,128)}), f32[2,16,2,128,128]{4,3,2,0,1:T(8,128)}, u32[]{:S(2)}, u32[]{:S(2)}) async-start(f32[2,16,2,128,128]{4,3,2,0,1:T(8,128)} %copy.54), calls=%async_computation.1 | async-start | bytes 8388608 | tf_op jit(solution)/shard_map/all_to_all | solution.py:116
  34.7 0.1 eq.76
  34.8 49.4 %all-to-all-done.1 = f32[2,16,2,128,128]{4,3,2,0,1:T(8,128)} async-done(((f32[2,16,2,128,128]{4,3,2,0,1:T(8,128)}), f32[2,16,2,128,128]{4,3,2,0,1:T(8,128)}, u32[]{:S(2)}, u32[]{:S(2)}) %all-to-all-start.1) | async-done | bytes 4194336 | tf_op jit(solution)/shard_map/all_to_all | solution.py:116
  84.2 2.5 copy.55
  86.7 3.8 %fusion = f32[2,8,128,128]{3,1,2,0:T(8,128)S(1)} fusion(f32[2,32,128,128]{3,2,1,0:T(8,128)S(1)} %bitcast.193, s32[2,32]{1,0:T(2,128)S(1)} %eq.76), kind=kOutput, calls=%fused_computation.2 | convolution fusion | flops 100663808 | bytes 5243136 | tf_op jit(solution)/shard_map/dts,dsij->dtij/dot_general | solution.py:125
  90.5 0.4 fusion.17
  90.9 0.2 copy.58
  91.1 0.2 copy.57
  91.3 1.3 collective-permute-start
  92.7 1.3 collective-permute-start.1
  94.0 0.2 collective-permute-done
  94.2 0.4 stack.273
  94.5 9.9 %collective-permute-done.1 = f32[512,256]{1,0:T(8,128)S(1)} collective-permute-done((f32[512,256]{1,0:T(8,128)S(1)}, f32[512,256]{1,0:T(8,128)S(1)}, u32[]{:S(2)}, u32[]{:S(2)}) %collective-permute-start.1) | collective-permute-done | bytes 524320 | tf_op jit(solution)/shard_map/ppermute | solution.py:131
  104.4 0.4 stack.274
  104.8 0.0 copy-start.1
  104.8 0.0 copy-start.3
  104.8 2.1 collective-permute-start.3
  106.9 6.6 %collective-permute-start.2 = (f32[2,1,256]{2,0,1:T(2,128)S(1)}, f32[2,1,256]{2,0,1:T(2,128)S(1)}, u32[]{:S(2)}, u32[]{:S(2)}) collective-permute-start(f32[2,1,256]{2,0,1:T(2,128)S(1)} %get-tuple-element.8), channel_id=1, source_target_pairs={{1,0},{2,1},{3,2},{4,3},{5,4},{6,5},{7,6},{8,7},{9,8},{10,9},{11,1... | collective-permute-start | bytes 6152 | tf_op jit(solution)/shard_map/ppermute | solution.py:23
  113.4 0.0 collective-permute-done.3
  113.5 1.3 collective-permute-done.2
  114.7 5.2 %select_maximum_fusion = f32[2,514,258]{2,0,1:T(2,128)S(1)} fusion(f32[2,1,256]{2,0,1:T(2,128)S(1)} %collective-permute-done.2, f32[2,1,256]{2,0,1:T(2,128)S(1)} %collective-permute-done.3, f32[1,512,256]{2,0,1:T(1,128)S(1)} %stack.274, f32[1,512,256]{2,0,1:T(1,128)S(1)} %stack.273), kind=kLoop, calls=%fused_computation.5 | loop fusion | flops 2652240 | bytes 2113568 | tf_op jit(solution)/shard_map/concatenate | solution.py:24
  120.0 0.0 copy-done.1
  120.0 0.0 copy-done.3
  120.0 6.2 %multiply_bitcast_fusion = f32[2,1,512,256]{3,0,1,2:T(2,128)} fusion(f32[2,514,258]{2,0,1:T(2,128)S(1)} %select_maximum_fusion, f32[1,512,256]{2,0,1:T(1,128)S(1)} %stack.274, f32[1,512,256]{2,0,1:T(1,128)S(1)} %stack.273, f32[2,1,256]{2,0,1:T(2,128)S(1)} %collective-permute-done.3, f32[2,1,256]{2,0,1:T(2,128)S(1)} %collective-permute-done.2, ...), kind=kLoop, calls=%fused_computation.27 | loop fusion | flops 3670016 | bytes 5246984 | tf_op jit(solution)/shard_map/broadcast_in_dim | solution.py:143
  126.2 0.0 copy-start.2
  126.2 21.8 %all-to-all-start.2 = ((f32[2,1,512,256]{3,0,1,2:T(2,128)}), f32[2,1,512,256]{3,0,1,2:T(2,128)S(1)}, u32[]{:S(2)}, u32[]{:S(2)}) async-start(f32[2,1,512,256]{3,0,1,2:T(2,128)} %multiply_bitcast_fusion), calls=%async_computation.2 | async-start | bytes 2097152 | tf_op jit(solution)/shard_map/all_to_all | solution.py:142
  148.0 0.0 copy-done.2
  148.0 0.7 fusion.21
  148.7 0.7 fusion.19
  156.2 0.7 fusion.20
  163.7 0.7 fusion.18
  189.8 1.3 stack.272.ratio_ref
  191.1 0.6 stack.239.pivot_ref
  191.8 20.6 %stack.207.lower_ref = f32[32]{0:T(128)} concatenate(f32[1]{0:T(128)} %constant.5.clone.1, f32[1]{0:T(128)} %bitcast, f32[1]{0:T(128)} %bitcast.1, f32[1]{0:T(128)} %bitcast.2, f32[1]{0:T(128)} %bitcast.3, f32[1]{0:T(128)} %bitcast.4, f32[1]{0:T(128)} %bitcast.5, f32[1]{0:T(128)} %bitcast.6, f32[1]{0:T(128)} %bitcast.7, f32[1]{0:T(128)} %bitcast.8, f32[1]{0:T(128)} %bitcast.9, ...), dimensions={0} | concatenate | bytes 256 | tf_op jit(solution)/shard_map/stack | solution.py:145
  212.3 0.0 all-to-all-done.2
  212.3 1.1 copy.59
  213.4 2.4 shard_map.73
  215.8 1.3 copy.60
  217.1 68.0 %all_to_all.34 = f32[2,32,16,256]{3,2,0,1:T(8,128)S(1)} all-to-all(f32[2,32,16,256]{3,2,0,1:T(8,128)S(1)} %copy.60), channel_id=1, replica_groups=mesh['par'=32,'perp'=16] {'par'}, dimensions={1} | all-to-all | bytes 2097152 | tf_op jit(solution)/shard_map/all_to_all | solution.py:146
  285.1 1.1 copy.61
  (9 shorter events, 0.1 us)
Async XLA Ops:
  0.0 13.4 %copy-start = (f32[8,128,128]{2,1,0:T(8,128)S(1)}, f32[8,128,128]{2,1,0:T(8,128)}, u32[]{:S(2)}) copy-start(f32[8,128,128]{2,1,0:T(8,128)} %param.8) | copy-start | bytes 1572868
  3.3 24.2 %all-to-all-start = ((s32[2,16,2]{2,0,1:T(2,128)}), s32[2,16,2]{2,0,1:T(2,128)S(1)}, u32[]{:S(2)}, u32[]{:S(2)}) async-start(s32[2,16,2]{2,0,1:T(2,128)} %copy.50), calls=%async_computation | async-start | bytes 32768 | tf_op jit(solution)/shard_map/all_to_all | solution.py:119
  27.5 56.8 %all-to-all-start.1 = ((f32[2,16,2,128,128]{4,3,2,0,1:T(8,128)}), f32[2,16,2,128,128]{4,3,2,0,1:T(8,128)}, u32[]{:S(2)}, u32[]{:S(2)}) async-start(f32[2,16,2,128,128]{4,3,2,0,1:T(8,128)} %copy.54), calls=%async_computation.1 | async-start | bytes 8388608 | tf_op jit(solution)/shard_map/all_to_all | solution.py:116
  91.3 2.8 collective-permute-start
  92.7 11.7 %collective-permute-start.1 = (f32[512,256]{1,0:T(8,128)S(1)}, f32[512,256]{1,0:T(8,128)S(1)}, u32[]{:S(2)}, u32[]{:S(2)}) collective-permute-start(f32[512,256]{1,0:T(8,128)S(1)} %bitcast.202), channel_id=1, source_target_pairs={{16,0},{32,16},{48,32},{64,48},{80,64},{96,80},{112,96},{128,112},... | collective-permute-start | bytes 1572872 | tf_op jit(solution)/shard_map/ppermute | solution.py:131
  104.8 15.2 %copy-start.1 = (f32[2,1,512,256]{3,2,1,0:T(8,128)S(1)}, f32[2,1,512,256]{3,2,1,0:T(8,128)}, u32[]{:S(2)}) copy-start(f32[2,1,512,256]{3,2,1,0:T(8,128)} %param.7) | copy-start | bytes 3145732
  104.8 15.2 %copy-start.3 = (f32[2]{0:T(128)S(1)}, f32[2]{0:T(128)}, u32[]{:S(2)}) copy-start(f32[2]{0:T(128)} %constant.25.clone) | copy-start | bytes 28
  104.8 8.6 %collective-permute-start.3 = (f32[2,1,256]{2,0,1:T(2,128)S(1)}, f32[2,1,256]{2,0,1:T(2,128)S(1)}, u32[]{:S(2)}, u32[]{:S(2)}) collective-permute-start(f32[2,1,256]{2,0,1:T(2,128)S(1)} %get-tuple-element.7), channel_id=1, source_target_pairs={{0,1},{1,2},{2,3},{3,4},{4,5},{5,6},{6,7},{7,8},{8,9},{9,10},{10,1... | collective-permute-start | bytes 6152 | tf_op jit(solution)/shard_map/ppermute | solution.py:20
  106.9 7.8 %collective-permute-start.2 = (f32[2,1,256]{2,0,1:T(2,128)S(1)}, f32[2,1,256]{2,0,1:T(2,128)S(1)}, u32[]{:S(2)}, u32[]{:S(2)}) collective-permute-start(f32[2,1,256]{2,0,1:T(2,128)S(1)} %get-tuple-element.8), channel_id=1, source_target_pairs={{1,0},{2,1},{3,2},{4,3},{5,4},{6,5},{7,6},{8,7},{9,8},{10,9},{11,1... | collective-permute-start | bytes 6152 | tf_op jit(solution)/shard_map/ppermute | solution.py:23
  126.2 21.8 %copy-start.2 = (f32[2,32]{1,0:T(2,128)S(1)}, f32[2,32]{1,0:T(2,128)}, u32[]{:S(2)}) copy-start(f32[2,32]{1,0:T(2,128)} %param.12) | copy-start | bytes 772
  126.2 86.1 %all-to-all-start.2 = ((f32[2,1,512,256]{3,0,1,2:T(2,128)}), f32[2,1,512,256]{3,0,1,2:T(2,128)S(1)}, u32[]{:S(2)}, u32[]{:S(2)}) async-start(f32[2,1,512,256]{3,0,1,2:T(2,128)} %multiply_bitcast_fusion), calls=%async_computation.2 | async-start | bytes 2097152 | tf_op jit(solution)/shard_map/all_to_all | solution.py:142

commit v2 on v1

v2 whole, which is shorter than its diff:
```python
import jax
import jax.numpy as jnp
from jax import lax
from jax.experimental import pallas as pl
from jax.experimental.pallas import tpu as pltpu
from jax.sharding import PartitionSpec as P

TILE = 128


PRECISE = lax.Precision.HIGHEST
KAPPA = 0.125


def split_tiles(plane_pair):
    field_count, row_count, col_count = plane_pair.shape
    shaped = plane_pair.reshape(field_count, row_count // TILE, TILE, col_count // TILE, TILE)
    return shaped.transpose(0, 1, 3, 2, 4).reshape(field_count, -1, TILE, TILE)


def join_tiles(tile_set, row_count, col_count):
    field_count = tile_set.shape[0]
    shaped = tile_set.reshape(field_count, row_count // TILE, col_count // TILE, TILE, TILE)
    return shaped.transpose(0, 1, 3, 2, 4).reshape(field_count, row_count, col_count)


def coefficients(band_terms):
    plane_total = band_terms.shape[1]
    lower, pivots, ratios = [], [], []
    previous = jnp.zeros((), jnp.float32)
    for p in range(plane_total):
        lower_now = band_terms[0, p] if p > 0 else jnp.zeros((), jnp.float32)
        upper_now = band_terms[1, p] if p < plane_total - 1 else jnp.zeros((), jnp.float32)
        pivot_now = 1.0 - lower_now * previous
        ratio_now = upper_now / pivot_now
        lower.append(lower_now)
        pivots.append(pivot_now)
        ratios.append(ratio_now)
        previous = ratio_now
    return lower, pivots, ratios


def slot_labels(dest_slabs, peer_count, capacity):
    tile_count = dest_slabs.shape[-1]
    position = jnp.arange(tile_count, dtype=jnp.int32)
    earlier = position[:, None] > position[None, :]
    shared = dest_slabs[..., :, None] == dest_slabs[..., None, :]
    slot_rank = jnp.sum((shared & earlier).astype(jnp.int32), axis=-1)
    peer_ids = jnp.arange(peer_count, dtype=jnp.int32)
    slot_ids = jnp.arange(capacity, dtype=jnp.int32)
    chosen = (dest_slabs[..., None, None, :] == peer_ids[:, None, None]) & (
        slot_rank[..., None, None, :] == slot_ids[None, :, None]
    )
    return chosen


def thomas_kernel(lower_ref, pivot_ref, ratio_ref, rhs_ref, out_ref):
    depth = rhs_ref.shape[0]
    previous = rhs_ref[0] / pivot_ref[0]
    out_ref[0] = previous
    for p in range(1, depth):
        previous = (rhs_ref[p] - lower_ref[p] * previous) / pivot_ref[p]
        out_ref[p] = previous
    following = previous
    for p in reversed(range(depth - 1)):
        following = out_ref[p] - ratio_ref[p] * following
        out_ref[p] = following


def thomas(rhs, lower, pivots, ratios):
    scalar = pl.BlockSpec(memory_space=pltpu.SMEM)
    whole = pl.BlockSpec(memory_space=pltpu.VMEM)
    return pl.pallas_call(
        thomas_kernel,
        out_shape=jax.ShapeDtypeStruct(rhs.shape, rhs.dtype),
        in_specs=[scalar, scalar, scalar, whole],
        out_specs=whole,
    )(lower, pivots, ratios, rhs)


def smooth_slab(plane, above_row, below_row):
    row_count, col_count = plane.shape
    zero_col = jnp.zeros((row_count, 1), plane.dtype)
    above = jnp.concatenate([above_row, plane[:-1]], axis=0)
    below = jnp.concatenate([plane[1:], below_row], axis=0)
    left = jnp.concatenate([zero_col, plane[:, :-1]], axis=1)
    right = jnp.concatenate([plane[:, 1:], zero_col], axis=1)
    beside_all = below + above + right + left
    return plane + KAPPA * (beside_all - 4.0 * plane)


def local(fields, weight_bank, dest_slab, dest_tile, tile_blocks, band_terms):
    peer_count = lax.axis_size("perp")
    plane_count = lax.axis_size("par")
    field_count, _, row_count, col_count = fields.shape
    local_pair = fields[:, 0]
    tile_set = split_tiles(local_pair)
    tile_count = tile_set.shape[1]
    capacity = max(2, (tile_count + peer_count - 1) // peer_count)
    dest_slabs = dest_slab[:, 0, :, 0]
    target = dest_tile[:, 0, :]
    left_index = tile_blocks[:, 0, :, 0]
    right_index = tile_blocks[:, 0, :, 1]

    left_block = jnp.take(weight_bank, left_index, axis=0, mode="clip")
    right_block = jnp.take(weight_bank, right_index, axis=0, mode="clip")
    shifted = jnp.einsum("dsij,dsjk->dsik", left_block, tile_set, precision=PRECISE)
    moved = jnp.einsum("dsik,dslk->dsil", shifted, right_block, precision=PRECISE)
    moved = moved.reshape(field_count * tile_count, TILE, TILE)

    chosen = slot_labels(dest_slabs, peer_count, capacity)
    same_field = jnp.eye(field_count, dtype=jnp.bool_)
    picker = chosen.transpose(1, 2, 0, 3)[:, :, :, None, :] & same_field[None, None, :, :, None]
    picker = picker.astype(jnp.float32).reshape(
        peer_count, capacity, field_count, field_count * tile_count
    )
    packed = jnp.einsum("pcdk,kij->pcdij", picker, moved, precision=PRECISE)
    moved_tiles = lax.all_to_all(packed, "perp", split_axis=0, concat_axis=0, tiled=True)
    slot_target = jnp.sum(chosen.astype(jnp.int32) * (target[:, None, None, :] + 1), axis=3) - 1
    arrived_target = lax.all_to_all(
        slot_target.transpose(1, 2, 0), "perp", split_axis=0, concat_axis=0, tiled=True
    )

    position = jnp.arange(tile_count, dtype=jnp.int32)
    hit = arrived_target[None, None] == position[None, :, None, None, None]
    landing = hit & same_field[:, None, None, None, :]
    landing = landing.astype(jnp.float32).reshape(field_count, tile_count, -1)
    summed = jnp.einsum(
        "dtk,kij->dtij", landing, moved_tiles.reshape(-1, TILE, TILE), precision=PRECISE
    )
    deposit = join_tiles(summed, row_count, col_count)

    upward = [(i, i + 1) for i in range(plane_count - 1)]
    downward = [(i + 1, i) for i in range(plane_count - 1)]
    mapped = (
        lax.ppermute(deposit[0], "par", upward),
        lax.ppermute(deposit[1], "par", downward),
    )
    forward = [(i, i + 1) for i in range(peer_count - 1)]
    backward = [(i + 1, i) for i in range(peer_count - 1)]
    from_above = lax.ppermute(jnp.stack([m[-1:] for m in mapped]), "perp", forward)
    from_below = lax.ppermute(jnp.stack([m[:1] for m in mapped]), "perp", backward)
    chunk_rows = row_count // plane_count
    sides = []
    for f in range(field_count):
        smoothed = smooth_slab(mapped[f], from_above[f], from_below[f])
        side = local_pair[f] - smoothed
        if f == 1:
            side = -side
        sides.append(side.reshape(plane_count, chunk_rows, col_count))
    right_side = jnp.stack(sides, axis=1)
    lower, pivots, ratios = coefficients(band_terms)
    column_block = lax.all_to_all(right_side, "par", split_axis=0, concat_axis=0, tiled=True)
    solved = thomas(column_block, jnp.stack(lower), jnp.stack(pivots), jnp.stack(ratios))
    back = lax.all_to_all(solved, "par", split_axis=0, concat_axis=0, tiled=True)
    result = back.transpose(1, 0, 2, 3).reshape(field_count, 1, row_count, col_count)
    return result


def solution(mesh):
    placed = (
        P(None, "par", "perp", None),
        P(),
        P(None, "par", "perp", None),
        P(None, "par", "perp"),
        P(None, "par", "perp", None),
        P(),
    )
    return jax.shard_map(
        local, mesh=mesh, in_specs=placed, out_specs=P(None, "par", "perp", None), check_vma=False
    )
```

time: 289 us -> 278 us (0.962)
  other arithmetic: 14 us -> 5.09 us
  local copies, waits for them, and re-layouts: 43 us -> 38.2 us
  matrix products: 9.34 us -> 12.8 us
    broadcast_in_dim x1 -> x0, other arithmetic: 6.2 us -> none  [local(): right_side[:, None]]
    concatenate x1 -> x0, other arithmetic: 5.22 us -> none  [extended(): block = jnp.concatenate([low, block, high], axis=dim)]
    all_to_all x4 -> x1, local copies, waits for them, and re-layouts: 4.56 us -> 0.2 us  [local(): lax.all_to_all(slot_target.transpose(1, 2, 0), 'perp', split_axis=0, conc...]
  transfers between devices with their start and end apart: 7 -> 7, of which waited for: 4 -> 3; matrix products, arithmetic and copies ran while one was open for 14% -> 16% of each run, Pallas kernels for 0% -> 0%
where the time goes in v2:
time: 278 us; the launch traced here: 275 us
  blocking collectives  68.2 us (25%)
  waiting for transfers between devices  60.1 us (22%)
  starting transfers between devices  49.5 us (18%)
  between operations  39.1 us (14%)
  local copies, waits for them, and re-layouts  38.2 us (14%)
  matrix products  12.8 us (5%)
  other arithmetic  5.09 us (2%)
    all_to_all x1, blocking collectives, local(): lax.all_to_all(solved, 'par', split_axis=0, concat_axis=0, tiled=True)  68.2 us
    all_to_all x1, waiting for transfers between devices, local(): lax.all_to_all(packed, 'perp', split_axis=0, concat_axis=0, tiled=True)  49.1 us
    all_to_all x1, starting transfers between devices, local(): lax.all_to_all(right_side, 'par', split_axis=0, concat_axis=0, tiled=True)  21.9 us
    another operation x1, local copies, waits for them, and re-layouts, local(): jnp.stack(lower)  20.5 us
    ppermute x1, waiting for transfers between devices, local(): lax.ppermute(deposit[1], 'par', downward)  10.3 us
    all_to_all x1, starting transfers between devices, local(): lax.all_to_all(slot_target.transpose(1, 2, 0), 'perp', split_axis=0, conc...  9.13 us
    all_to_all x1, starting transfers between devices, local(): lax.all_to_all(packed, 'perp', split_axis=0, concat_axis=0, tiled=True)  7.21 us
    ppermute x1, starting transfers between devices, local(): lax.ppermute(jnp.stack([m[:1] for m in mapped]), 'perp', backward)  6.69 us
  transfers between devices with their start and end apart: 7, of which 3 were waited for; matrix products, arithmetic and copies ran while one was open for 16% of the time, Pallas kernels for 0%

profile of v2, /device:TPU:6, one launch (start us, length us, event | category | flops | bytes accessed | tf_op | source)
XLA Modules:
  0.0 275.3 jit_solution(6420337905841707840)
XLA Ops:
  0.0 0.0 copy-start
  0.0 0.8 iota_compare_fusion.1
  0.8 1.0 convert_reduce_fusion
  1.8 0.7 broadcast_add_fusion
  2.5 0.1 select_reduce_fusion
  2.6 0.7 copy.38
  3.3 9.1 %all-to-all-start = ((s32[16,2,2]{1,2,0:T(2,128)}), s32[16,2,2]{1,2,0:T(2,128)S(1)}, u32[]{:S(2)}, u32[]{:S(2)}) async-start(s32[16,2,2]{1,2,0:T(2,128)} %copy.38), calls=%async_computation | async-start | bytes 32768 | tf_op jit(solution)/shard_map/all_to_all | solution.py:120
  12.4 0.8 iota_compare_fusion
  13.2 0.8 slice_reduce_fusion
  13.9 0.1 reshape.120
  14.0 1.7 reshape_squeeze.3
  15.8 0.1 copy.40
  15.9 0.1 reshape.128
  16.0 0.0 copy-done
  16.0 0.6 gather_fusion
  16.6 1.6 gather_fusion.1
  18.2 0.1 broadcast_and_fusion
  18.3 1.1 fusion.36
  19.4 3.5 %convolution_bitcast_fusion.1 = f32[2,8,128,128,1,1]{3,2,1,0,5,4:T(8,128)S(1)} fusion(f32[2,8,128,128]{3,2,1,0:T(8,128)S(1)} %fusion.36, f32[2,8,128,128]{3,2,1,0:T(8,128)} %bitcast.217), kind=kOutput, calls=%fused_computation.6 | convolution fusion | flops 402653184 | bytes 3145728 | tf_op jit(solution)/shard_map/dsik,dslk->dsil/dot_general | solution.py:108
  22.9 2.1 convolution_bitcast_fusion
  25.1 3.2 %copy.42 = f32[16,2,2,128,128]{4,3,2,1,0:T(8,128)} copy(f32[16,2,2,128,128]{4,0,3,2,1:T(8,128)S(1)} %convolution_bitcast_fusion) | data formatting | bytes 8388608 | tf_op jit(solution)/shard_map/pcdk,kij->pcdij/dot_general | solution.py:117
  28.3 0.0 all-to-all-done
  28.3 7.2 %all-to-all-start.1 = ((f32[16,2,2,128,128]{4,3,2,1,0:T(8,128)}), f32[16,2,2,128,128]{4,3,2,1,0:T(8,128)}, u32[]{:S(2)}, u32[]{:S(2)}) async-start(f32[16,2,2,128,128]{4,3,2,1,0:T(8,128)} %copy.42), calls=%async_computation.1 | async-start | bytes 8388608 | tf_op jit(solution)/shard_map/all_to_all | solution.py:118
  35.6 0.1 and.71
  35.7 0.2 copy.39
  35.9 0.1 eq.118
  36.0 0.1 broadcast_compare_fusion
  36.1 49.1 %all-to-all-done.1 = f32[16,2,2,128,128]{4,3,2,1,0:T(8,128)} async-done(((f32[16,2,2,128,128]{4,3,2,1,0:T(8,128)}), f32[16,2,2,128,128]{4,3,2,1,0:T(8,128)}, u32[]{:S(2)}, u32[]{:S(2)}) %all-to-all-start.1) | async-done | bytes 4194336 | tf_op jit(solution)/shard_map/all_to_all | solution.py:118
  85.1 6.0 %fusion.2 = f32[2,4,128,2,128]{4,1,2,3,0:T(4,128)S(1)} fusion(f32[64,128,128,1,1]{2,1,0,4,3:T(8,128)} %bitcast.161, pred[2,64]{1,0:T(4,128)(4,1)S(1)} %and.71, pred[4,2,64]{2,0,1:T(4,128)(4,1)S(1)} %broadcast_compare_fusion), kind=kOutput, calls=%fused_computation.5 | convolution fusion | flops 201327616 | bytes 5243520 | tf_op jit(solution)/shard_map/dtk,kij->dtij/dot_general | solution.py:128
  91.2 0.1 fusion.27
  91.2 0.4 copy.44
  91.7 1.3 collective-permute-start
  93.0 0.4 copy.45
  93.5 1.3 collective-permute-start.1
  94.8 0.0 collective-permute-done
  94.8 10.3 %collective-permute-done.1 = f32[512,256]{1,0:T(8,128)S(1)} collective-permute-done((f32[512,256]{1,0:T(8,128)S(1)}, f32[512,256]{1,0:T(8,128)S(1)}, u32[]{:S(2)}, u32[]{:S(2)}) %collective-permute-start.1) | collective-permute-done | bytes 524320 | tf_op jit(solution)/shard_map/ppermute | solution.py:137
  105.1 1.9 collective-permute-start.3
  107.1 0.0 copy-start.1
  107.1 6.7 %collective-permute-start.2 = (f32[2,1,256]{2,1,0:T(1,128)S(1)}, f32[2,1,256]{2,1,0:T(1,128)S(1)}, u32[]{:S(2)}, u32[]{:S(2)}) collective-permute-start(f32[2,1,256]{2,1,0:T(1,128)S(1)} %pad_maximum_fusion.1), channel_id=1, source_target_pairs={{1,0},{2,1},{3,2},{4,3},{5,4},{6,5},{7,6},{8,7},{9,8},{10,9},{11,1... | collective-permute-start | bytes 6152 | tf_op jit(solution)/shard_map/ppermute | solution.py:142
  113.8 0.2 fusion.28
  114.0 0.1 fusion.29
  114.1 0.2 fusion.30
  114.3 0.1 fusion.31
  114.4 0.0 collective-permute-done.3
  114.4 0.7 collective-permute-done.2
  115.1 0.0 copy-done.1
  115.1 0.0 copy-start.3
  115.1 0.5 fusion.11
  115.6 1.0 pad_maximum_fusion
  116.7 21.9 %all-to-all-start.2 = ((f32[32,2,16,256]{3,2,1,0:T(8,128)}), f32[32,2,16,256]{3,2,1,0:T(8,128)S(1)}, u32[]{:S(2)}, u32[]{:S(2)}) async-start(f32[32,2,16,256]{3,2,1,0:T(8,128)} %pad_maximum_fusion), calls=%async_computation.2 | async-start | bytes 2097152 | tf_op jit(solution)/shard_map/all_to_all | solution.py:153
  138.5 0.0 copy-done.3
  138.6 0.7 fusion.35
  139.2 0.7 fusion.33
  146.9 0.7 fusion.34
  154.4 0.7 fusion.32
  180.2 1.3 stack.284.ratio_ref
  181.5 0.6 stack.251.pivot_ref
  182.2 20.5 %stack.219.lower_ref = f32[32]{0:T(128)} concatenate(f32[1]{0:T(128)} %constant.4.clone.1, f32[1]{0:T(128)} %bitcast, f32[1]{0:T(128)} %bitcast.1, f32[1]{0:T(128)} %bitcast.2, f32[1]{0:T(128)} %bitcast.3, f32[1]{0:T(128)} %bitcast.4, f32[1]{0:T(128)} %bitcast.5, f32[1]{0:T(128)} %bitcast.6, f32[1]{0:T(128)} %bitcast.7, f32[1]{0:T(128)} %bitcast.8, f32[1]{0:T(128)} %bitcast.9, ...), dimensions={0} | concatenate | bytes 256 | tf_op jit(solution)/shard_map/stack | solution.py:154
  202.7 0.0 all-to-all-done.2.rhs_ref
  202.7 0.0 copy-start.2
  202.7 1.0 copy-done.2
  203.7 2.4 shard_map.64
  206.1 68.2 %all_to_all.20 = f32[32,2,16,256]{3,2,1,0:T(8,128)S(1)} all-to-all(f32[32,2,16,256]{3,2,1,0:T(8,128)} %shard_map.64), channel_id=1, replica_groups=mesh['par'=32,'perp'=16] {'par'}, dimensions={0} | all-to-all | bytes 2097152 | tf_op jit(solution)/shard_map/all_to_all | solution.py:155
  274.3 1.1 copy.46
  (16 shorter events, 0.2 us)
Async XLA Ops:
  0.0 16.0 %copy-start = (f32[8,128,128]{2,1,0:T(8,128)S(1)}, f32[8,128,128]{2,1,0:T(8,128)}, u32[]{:S(2)}) copy-start(f32[8,128,128]{2,1,0:T(8,128)} %param.7) | copy-start | bytes 1572868
  3.3 25.1 %all-to-all-start = ((s32[16,2,2]{1,2,0:T(2,128)}), s32[16,2,2]{1,2,0:T(2,128)S(1)}, u32[]{:S(2)}, u32[]{:S(2)}) async-start(s32[16,2,2]{1,2,0:T(2,128)} %copy.38), calls=%async_computation | async-start | bytes 32768 | tf_op jit(solution)/shard_map/all_to_all | solution.py:120
  28.3 56.8 %all-to-all-start.1 = ((f32[16,2,2,128,128]{4,3,2,1,0:T(8,128)}), f32[16,2,2,128,128]{4,3,2,1,0:T(8,128)}, u32[]{:S(2)}, u32[]{:S(2)}) async-start(f32[16,2,2,128,128]{4,3,2,1,0:T(8,128)} %copy.42), calls=%async_computation.1 | async-start | bytes 8388608 | tf_op jit(solution)/shard_map/all_to_all | solution.py:118
  91.7 3.1 %collective-permute-start = (f32[512,256]{1,0:T(8,128)S(1)}, f32[512,256]{1,0:T(8,128)S(1)}, u32[]{:S(2)}, u32[]{:S(2)}) collective-permute-start(f32[512,256]{1,0:T(8,128)S(1)} %bitcast.224), channel_id=1, source_target_pairs={{0,16},{16,32},{32,48},{48,64},{64,80},{80,96},{96,112},{112,128},... | collective-permute-start | bytes 1572872 | tf_op jit(solution)/shard_map/ppermute | solution.py:136
  93.5 11.6 %collective-permute-start.1 = (f32[512,256]{1,0:T(8,128)S(1)}, f32[512,256]{1,0:T(8,128)S(1)}, u32[]{:S(2)}, u32[]{:S(2)}) collective-permute-start(f32[512,256]{1,0:T(8,128)S(1)} %bitcast.225), channel_id=1, source_target_pairs={{16,0},{32,16},{48,32},{64,48},{80,64},{96,80},{112,96},{128,112},... | collective-permute-start | bytes 1572872 | tf_op jit(solution)/shard_map/ppermute | solution.py:137
  105.1 9.2 %collective-permute-start.3 = (f32[2,1,256]{2,1,0:T(1,128)S(1)}, f32[2,1,256]{2,1,0:T(1,128)S(1)}, u32[]{:S(2)}, u32[]{:S(2)}) collective-permute-start(f32[2,1,256]{2,1,0:T(1,128)S(1)} %pad_maximum_fusion.2), channel_id=1, source_target_pairs={{0,1},{1,2},{2,3},{3,4},{4,5},{5,6},{6,7},{7,8},{8,9},{9,10},{10,1... | collective-permute-start | bytes 6152 | tf_op jit(solution)/shard_map/ppermute | solution.py:141
  107.1 8.0 %copy-start.1 = (f32[2,1,512,256]{3,2,1,0:T(8,128)S(1)}, f32[2,1,512,256]{3,2,1,0:T(8,128)}, u32[]{:S(2)}) copy-start(f32[2,1,512,256]{3,2,1,0:T(8,128)} %param.6) | copy-start | bytes 3145732
  107.1 8.0 %collective-permute-start.2 = (f32[2,1,256]{2,1,0:T(1,128)S(1)}, f32[2,1,256]{2,1,0:T(1,128)S(1)}, u32[]{:S(2)}, u32[]{:S(2)}) collective-permute-start(f32[2,1,256]{2,1,0:T(1,128)S(1)} %pad_maximum_fusion.1), channel_id=1, source_target_pairs={{1,0},{2,1},{3,2},{4,3},{5,4},{6,5},{7,6},{8,7},{9,8},{10,9},{11,1... | collective-permute-start | bytes 6152 | tf_op jit(solution)/shard_map/ppermute | solution.py:142
  115.1 23.5 %copy-start.3 = (f32[2,32]{1,0:T(2,128)S(1)}, f32[2,32]{1,0:T(2,128)}, u32[]{:S(2)}) copy-start(f32[2,32]{1,0:T(2,128)} %param.11) | copy-start | bytes 772
  116.7 86.1 %all-to-all-start.2 = ((f32[32,2,16,256]{3,2,1,0:T(8,128)}), f32[32,2,16,256]{3,2,1,0:T(8,128)S(1)}, u32[]{:S(2)}, u32[]{:S(2)}) async-start(f32[32,2,16,256]{3,2,1,0:T(8,128)} %pad_maximum_fusion), calls=%async_computation.2 | async-start | bytes 2097152 | tf_op jit(solution)/shard_map/all_to_all | solution.py:153
  202.7 1.0 copy-start.2

commit v3 on v2

--- a/solution.py
+++ b/solution.py
@@ -24,22 +24,6 @@
     return shaped.transpose(0, 1, 3, 2, 4).reshape(field_count, row_count, col_count)
 
 
-def coefficients(band_terms):
-    plane_total = band_terms.shape[1]
-    lower, pivots, ratios = [], [], []
-    previous = jnp.zeros((), jnp.float32)
-    for p in range(plane_total):
-        lower_now = band_terms[0, p] if p > 0 else jnp.zeros((), jnp.float32)
-        upper_now = band_terms[1, p] if p < plane_total - 1 else jnp.zeros((), jnp.float32)
-        pivot_now = 1.0 - lower_now * previous
-        ratio_now = upper_now / pivot_now
-        lower.append(lower_now)
-        pivots.append(pivot_now)
-        ratios.append(ratio_now)
-        previous = ratio_now
-    return lower, pivots, ratios
-
-
 def slot_labels(dest_slabs, peer_count, capacity):
     tile_count = dest_slabs.shape[-1]
     position = jnp.arange(tile_count, dtype=jnp.int32)
@@ -54,12 +38,18 @@
     return chosen
 
 
-def thomas_kernel(lower_ref, pivot_ref, ratio_ref, rhs_ref, out_ref):
+def thomas_kernel(band_ref, rhs_ref, out_ref, ratio_ref):
     depth = rhs_ref.shape[0]
-    previous = rhs_ref[0] / pivot_ref[0]
-    out_ref[0] = previous
-    for p in range(1, depth):
-        previous = (rhs_ref[p] - lower_ref[p] * previous) / pivot_ref[p]
+    shape = rhs_ref.shape[1:]
+    ratio = jnp.zeros(shape, jnp.float32)
+    previous = jnp.zeros(shape, jnp.float32)
+    for p in range(depth):
+        lower_now = band_ref[0, p] if p > 0 else 0.0
+        upper_now = band_ref[1, p] if p < depth - 1 else 0.0
+        pivot = 1.0 - lower_now * ratio
+        ratio = upper_now / pivot
+        ratio_ref[p] = ratio
+        previous = (rhs_ref[p] - lower_now * previous) / pivot
         out_ref[p] = previous
     following = previous
     for p in reversed(range(depth - 1)):
@@ -67,15 +57,16 @@
         out_ref[p] = following
 
 
-def thomas(rhs, lower, pivots, ratios):
+def thomas(rhs, band_terms):
     scalar = pl.BlockSpec(memory_space=pltpu.SMEM)
     whole = pl.BlockSpec(memory_space=pltpu.VMEM)
     return pl.pallas_call(
         thomas_kernel,
         out_shape=jax.ShapeDtypeStruct(rhs.shape, rhs.dtype),
-        in_specs=[scalar, scalar, scalar, whole],
+        in_specs=[scalar, whole],
         out_specs=whole,
-    )(lower, pivots, ratios, rhs)
+        scratch_shapes=[pltpu.VMEM(rhs.shape, jnp.float32)],
+    )(band_terms, rhs)
 
 
 def smooth_slab(plane, above_row, below_row):
@@ -136,10 +127,24 @@
         lax.ppermute(deposit[0], "par", upward),
         lax.ppermute(deposit[1], "par", downward),
     )
-    forward = [(i, i + 1) for i in range(peer_count - 1)]
-    backward = [(i + 1, i) for i in range(peer_count - 1)]
-    from_above = lax.ppermute(jnp.stack([m[-1:] for m in mapped]), "perp", forward)
-    from_below = lax.ppermute(jnp.stack([m[:1] for m in mapped]), "perp", backward)
+
+    def diagonal(plane_step, slab_step):
+        pairs = []
+        for p in range(plane_count):
+            for j in range(peer_count):
+                q, i = p - plane_step, j - slab_step
+                if 0 <= q < plane_count and 0 <= i < peer_count:
+                    pairs.append((q * peer_count + i, p * peer_count + j))
+        return pairs
+
+    from_above = [
+        lax.ppermute(deposit[0, -1:], ("par", "perp"), diagonal(1, 1)),
+        lax.ppermute(deposit[1, -1:], ("par", "perp"), diagonal(-1, 1)),
+    ]
+    from_below = [
+        lax.ppermute(deposit[0, :1], ("par", "perp"), diagonal(1, -1)),
+        lax.ppermute(deposit[1, :1], ("par", "perp"), diagonal(-1, -1)),
+    ]
     chunk_rows = row_count // plane_count
     sides = []
     for f in range(field_count):
@@ -149,9 +154,8 @@
             side = -side
         sides.append(side.reshape(plane_count, chunk_rows, col_count))
     right_side = jnp.stack(sides, axis=1)
-    lower, pivots, ratios = coefficients(band_terms)
     column_block = lax.all_to_all(right_side, "par", split_axis=0, concat_axis=0, tiled=True)
-    solved = thomas(column_block, jnp.stack(lower), jnp.stack(pivots), jnp.stack(ratios))
+    solved = thomas(column_block, band_terms)
     back = lax.all_to_all(solved, "par", split_axis=0, concat_axis=0, tiled=True)
     result = back.transpose(1, 0, 2, 3).reshape(field_count, 1, row_count, col_count)
     return result

time: 278 us -> 272 us (0.978)
  blocking collectives: 68.2 us -> 140 us
  between operations: 39.1 us -> 0.23 us
  local copies, waits for them, and re-layouts: 38.2 us -> 18.9 us
  starting transfers between devices: 49.5 us -> 40.4 us
  waiting for transfers between devices: 60.1 us -> 52.1 us
    all_to_all x0 -> x1, blocking collectives: none -> 79.3 us  [local(): lax.all_to_all(right_side, 'par', split_axis=0, concat_axis=0, tiled=True)]
    another operation x5 -> x0, local copies, waits for them, and re-layouts: 22.5 us -> none  [the longest x1 20.5 us: local(): jnp.stack(lower)]
    all_to_all x1 -> x0, starting transfers between devices: 21.9 us -> none  [local(): lax.all_to_all(right_side, 'par', split_axis=0, concat_axis=0, tiled=True)]
    ppermute x2 -> x4, starting transfers between devices: 8.61 us -> 21.4 us  [the longest x1 9.44 us: local(): lax.ppermute(deposit[0, -1:], ('par', 'perp'), diagonal(1, 1))]
    all_to_all x1, blocking collectives: 68.2 us -> 60.4 us  [local(): lax.all_to_all(solved, 'par', split_axis=0, concat_axis=0, tiled=True)]
    ppermute x1, waiting for transfers between devices: 10.3 us -> 3.1 us  [local(): lax.ppermute(deposit[1], 'par', downward)]
    slice x4 -> x0, local copies, waits for them, and re-layouts: 2.84 us -> none  [the longest x2 1.47 us: coefficients(): band_terms[1, p]]
  transfers between devices with their start and end apart: 7 -> 8, of which waited for: 3 -> 2; matrix products, arithmetic and copies ran while one was open for 16% -> 8% of each run, Pallas kernels for 0% -> 0%
where the time goes in v3:
time: 272 us; the launch traced here: 271 us
  blocking collectives  140 us (51%)
  waiting for transfers between devices  52.1 us (19%)
  starting transfers between devices  40.4 us (15%)
  local copies, waits for them, and re-layouts  18.9 us (7%)
  matrix products  12.8 us (5%)
  other arithmetic  4.17 us (2%)
    all_to_all x1, blocking collectives, local(): lax.all_to_all(right_side, 'par', split_axis=0, concat_axis=0, tiled=True)  79.3 us
    all_to_all x1, blocking collectives, local(): lax.all_to_all(solved, 'par', split_axis=0, concat_axis=0, tiled=True)  60.4 us
    all_to_all x1, waiting for transfers between devices, local(): lax.all_to_all(packed, 'perp', split_axis=0, concat_axis=0, tiled=True)  49 us
    ppermute x1, starting transfers between devices, local(): lax.ppermute(deposit[0, -1:], ('par', 'perp'), diagonal(1, 1))  9.44 us
    ppermute x1, starting transfers between devices, local(): lax.ppermute(deposit[0, :1], ('par', 'perp'), diagonal(1, -1))  9.41 us
    all_to_all x1, starting transfers between devices, local(): lax.all_to_all(slot_target.transpose(1, 2, 0), 'perp', split_axis=0, conc...  9.16 us
    all_to_all x1, starting transfers between devices, local(): lax.all_to_all(packed, 'perp', split_axis=0, concat_axis=0, tiled=True)  7.21 us
    dot_general x1, matrix products, local(): jnp.einsum('dtk,kij->dtij', landing, moved_tiles.reshape(-1, TILE, TILE),...  6.03 us
  transfers between devices with their start and end apart: 8, of which 2 were waited for; matrix products, arithmetic and copies ran while one was open for 8% of the time, Pallas kernels for 0%

profile of v3, /device:TPU:6, one launch (start us, length us, event | category | flops | bytes accessed | tf_op | source)
XLA Modules:
  0.0 270.8 jit_solution(5193601613154429896)
XLA Ops:
  0.0 0.0 copy-start
  0.0 0.0 copy-start.1
  0.0 0.8 broadcast_add_fusion
  0.8 0.8 iota_compare_fusion.1
  1.6 1.0 convert_reduce_fusion
  2.5 0.1 select_reduce_fusion
  2.6 0.7 copy.42
  3.3 9.2 %all-to-all-start = ((s32[16,2,2]{1,2,0:T(2,128)}), s32[16,2,2]{1,2,0:T(2,128)S(1)}, u32[]{:S(2)}, u32[]{:S(2)}) async-start(s32[16,2,2]{1,2,0:T(2,128)} %copy.42), calls=%async_computation | async-start | bytes 32768 | tf_op jit(solution)/shard_map/all_to_all | solution.py:111
  12.5 0.8 iota_compare_fusion
  13.3 0.8 slice_reduce_fusion
  14.0 0.1 reshape.114
  14.1 0.1 reshape.106
  14.2 0.0 copy-done
  14.2 0.6 gather_fusion.1
  14.9 1.6 gather_fusion
  16.4 0.0 copy-done.1
  16.4 1.5 reshape_squeeze.3
  17.9 1.3 copy.44
  19.3 0.1 broadcast_and_fusion
  19.3 2.4 fusion.32
  21.7 2.3 convolution_bitcast_fusion.1
  24.0 2.1 convolution_bitcast_fusion
  26.2 3.2 %copy.46 = f32[16,2,2,128,128]{4,3,2,1,0:T(8,128)} copy(f32[16,2,2,128,128]{4,0,3,2,1:T(8,128)S(1)} %convolution_bitcast_fusion) | data formatting | bytes 8388608 | tf_op jit(solution)/shard_map/pcdk,kij->pcdij/dot_general | solution.py:108
  29.4 0.0 all-to-all-done
  29.4 7.2 %all-to-all-start.1 = ((f32[16,2,2,128,128]{4,3,2,1,0:T(8,128)}), f32[16,2,2,128,128]{4,3,2,1,0:T(8,128)}, u32[]{:S(2)}, u32[]{:S(2)}) async-start(f32[16,2,2,128,128]{4,3,2,1,0:T(8,128)} %copy.46), calls=%async_computation.1 | async-start | bytes 8388608 | tf_op jit(solution)/shard_map/all_to_all | solution.py:109
  36.6 0.1 and.71
  36.7 0.2 copy.43
  37.0 0.1 eq.118
  37.1 0.1 broadcast_compare_fusion
  37.1 49.0 %all-to-all-done.1 = f32[16,2,2,128,128]{4,3,2,1,0:T(8,128)} async-done(((f32[16,2,2,128,128]{4,3,2,1,0:T(8,128)}), f32[16,2,2,128,128]{4,3,2,1,0:T(8,128)}, u32[]{:S(2)}, u32[]{:S(2)}) %all-to-all-start.1) | async-done | bytes 4194336 | tf_op jit(solution)/shard_map/all_to_all | solution.py:109
  86.1 6.0 %fusion.2 = f32[2,4,128,2,128]{4,1,2,3,0:T(4,128)S(1)} fusion(f32[64,128,128,1,1]{2,1,0,4,3:T(8,128)} %bitcast.16, pred[2,64]{1,0:T(4,128)(4,1)S(1)} %and.71, pred[4,2,64]{2,0,1:T(4,128)(4,1)S(1)} %broadcast_compare_fusion), kind=kOutput, calls=%fused_computation.5 | convolution fusion | flops 201327616 | bytes 5243520 | tf_op jit(solution)/shard_map/dtk,kij->dtij/dot_general | solution.py:119
  92.2 0.9 fusion.27
  93.0 0.4 copy.48
  93.4 0.8 copy.73
  94.3 1.3 collective-permute-start
  95.6 0.8 copy.49
  96.4 1.8 reshape.102
  98.2 0.8 slice_bitcast_fusion.2
  99.0 9.4 %collective-permute-start.2 = (f32[1,256]{1,0:T(1,128)S(1)}, f32[1,256]{1,0:T(1,128)S(1)}, u32[]{:S(2)}, u32[]{:S(2)}) collective-permute-start(f32[1,256]{1,0:T(1,128)S(1)} %get-tuple-element.9), channel_id=1, source_target_pairs={{0,17},{1,18},{2,19},{3,20},{4,21},{5,22},{6,23},{7,24},{8,25},{9,... | collective-permute-start | bytes 3080 | tf_op jit(solution)/shard_map/ppermute | solution.py:141
  108.4 1.3 collective-permute-start.5
  109.7 1.3 collective-permute-start.4
  111.0 9.4 %collective-permute-start.1 = (f32[1,256]{1,0:T(1,128)S(1)}, f32[1,256]{1,0:T(1,128)S(1)}, u32[]{:S(2)}, u32[]{:S(2)}) collective-permute-start(f32[1,256]{1,0:T(1,128)S(1)} %get-tuple-element.12), channel_id=1, source_target_pairs={{1,16},{2,17},{3,18},{4,19},{5,20},{6,21},{7,22},{8,23},{9,24},{10... | collective-permute-start | bytes 3080 | tf_op jit(solution)/shard_map/ppermute | solution.py:145
  120.4 1.4 copy.50
  121.9 0.0 collective-permute-done
  121.9 1.3 collective-permute-start.3
  123.2 0.2 fusion.28
  123.4 0.1 fusion.29
  123.5 3.1 %collective-permute-done.3 = f32[512,256]{1,0:T(8,128)S(1)} collective-permute-done((f32[512,256]{1,0:T(8,128)S(1)}, f32[512,256]{1,0:T(8,128)S(1)}, u32[]{:S(2)}, u32[]{:S(2)}) %collective-permute-start.3) | collective-permute-done | bytes 524320 | tf_op jit(solution)/shard_map/ppermute | solution.py:128
  126.6 0.2 fusion.30
  126.8 0.1 fusion.31
  126.9 0.0 collective-permute-done.2
  126.9 0.0 collective-permute-done.5
  126.9 0.0 collective-permute-done.4
  126.9 0.0 collective-permute-done.1
  126.9 0.5 fusion.11
  127.5 0.1 pad_maximum_fusion
  127.6 79.3 %all_to_all.20.rhs_ref = f32[32,2,16,256]{3,2,1,0:T(8,128)} all-to-all(f32[32,2,16,256]{3,2,1,0:T(8,128)S(1)} %pad_maximum_fusion), channel_id=1, replica_groups=mesh['par'=32,'perp'=16] {'par'}, dimensions={0} | all-to-all | bytes 2097152 | tf_op jit(solution)/shard_map/all_to_all | solution.py:157
  206.8 2.6 shard_map.64
  209.4 60.4 %all_to_all.21 = f32[32,2,16,256]{3,2,1,0:T(8,128)S(1)} all-to-all(f32[32,2,16,256]{3,2,1,0:T(8,128)} %shard_map.64), channel_id=1, replica_groups=mesh['par'=32,'perp'=16] {'par'}, dimensions={0} | all-to-all | bytes 2097152 | tf_op jit(solution)/shard_map/all_to_all | solution.py:159
  269.8 1.1 copy.51
  (9 shorter events, 0.1 us)
Async XLA Ops:
  0.0 14.2 %copy-start = (f32[8,128,128]{2,1,0:T(8,128)S(1)}, f32[8,128,128]{2,1,0:T(8,128)}, u32[]{:S(2)}) copy-start(f32[8,128,128]{2,1,0:T(8,128)} %param.7) | copy-start | bytes 1572868
  0.0 16.4 %copy-start.1 = (f32[2,1,512,256]{3,2,1,0:T(8,128)S(1)}, f32[2,1,512,256]{3,2,1,0:T(8,128)}, u32[]{:S(2)}) copy-start(f32[2,1,512,256]{3,2,1,0:T(8,128)} %param.6) | copy-start | bytes 3145732
  3.3 26.1 %all-to-all-start = ((s32[16,2,2]{1,2,0:T(2,128)}), s32[16,2,2]{1,2,0:T(2,128)S(1)}, u32[]{:S(2)}, u32[]{:S(2)}) async-start(s32[16,2,2]{1,2,0:T(2,128)} %copy.42), calls=%async_computation | async-start | bytes 32768 | tf_op jit(solution)/shard_map/all_to_all | solution.py:111
  29.4 56.7 %all-to-all-start.1 = ((f32[16,2,2,128,128]{4,3,2,1,0:T(8,128)}), f32[16,2,2,128,128]{4,3,2,1,0:T(8,128)}, u32[]{:S(2)}, u32[]{:S(2)}) async-start(f32[16,2,2,128,128]{4,3,2,1,0:T(8,128)} %copy.46), calls=%async_computation.1 | async-start | bytes 8388608 | tf_op jit(solution)/shard_map/all_to_all | solution.py:109
  94.3 27.7 %collective-permute-start = (f32[512,256]{1,0:T(8,128)}, f32[512,256]{1,0:T(8,128)S(1)}, u32[]{:S(2)}, u32[]{:S(2)}) collective-permute-start(f32[512,256]{1,0:T(8,128)} %bitcast.61), channel_id=1, source_target_pairs={{0,16},{16,32},{32,48},{48,64},{64,80},{80,96},{96,112},{112,128},... | collective-permute-start | bytes 1572872 | tf_op jit(solution)/shard_map/ppermute | solution.py:127
  99.0 28.0 %collective-permute-start.2 = (f32[1,256]{1,0:T(1,128)S(1)}, f32[1,256]{1,0:T(1,128)S(1)}, u32[]{:S(2)}, u32[]{:S(2)}) collective-permute-start(f32[1,256]{1,0:T(1,128)S(1)} %get-tuple-element.9), channel_id=1, source_target_pairs={{0,17},{1,18},{2,19},{3,20},{4,21},{5,22},{6,23},{7,24},{8,25},{9,... | collective-permute-start | bytes 3080 | tf_op jit(solution)/shard_map/ppermute | solution.py:141
  108.4 18.5 %collective-permute-start.5 = (f32[1,256]{1,0:T(1,128)S(1)}, f32[1,256]{1,0:T(1,128)S(1)}, u32[]{:S(2)}, u32[]{:S(2)}) collective-permute-start(f32[1,256]{1,0:T(1,128)S(1)} %get-tuple-element.10), channel_id=1, source_target_pairs={{16,1},{17,2},{18,3},{19,4},{20,5},{21,6},{22,7},{23,8},{24,9},{25... | collective-permute-start | bytes 3080 | tf_op jit(solution)/shard_map/ppermute | solution.py:142
  109.7 17.2 %collective-permute-start.4 = (f32[1,256]{1,0:T(1,128)S(1)}, f32[1,256]{1,0:T(1,128)S(1)}, u32[]{:S(2)}, u32[]{:S(2)}) collective-permute-start(f32[1,256]{1,0:T(1,128)S(1)} %get-tuple-element.11), channel_id=1, source_target_pairs={{17,0},{18,1},{19,2},{20,3},{21,4},{22,5},{23,6},{24,7},{25,8},{26... | collective-permute-start | bytes 3080 | tf_op jit(solution)/shard_map/ppermute | solution.py:146
  111.0 15.9 %collective-permute-start.1 = (f32[1,256]{1,0:T(1,128)S(1)}, f32[1,256]{1,0:T(1,128)S(1)}, u32[]{:S(2)}, u32[]{:S(2)}) collective-permute-start(f32[1,256]{1,0:T(1,128)S(1)} %get-tuple-element.12), channel_id=1, source_target_pairs={{1,16},{2,17},{3,18},{4,19},{5,20},{6,21},{7,22},{8,23},{9,24},{10... | collective-permute-start | bytes 3080 | tf_op jit(solution)/shard_map/ppermute | solution.py:145
  121.9 4.7 %collective-permute-start.3 = (f32[512,256]{1,0:T(8,128)S(1)}, f32[512,256]{1,0:T(8,128)S(1)}, u32[]{:S(2)}, u32[]{:S(2)}) collective-permute-start(f32[512,256]{1,0:T(8,128)S(1)} %bitcast.71), channel_id=1, source_target_pairs={{16,0},{32,16},{48,32},{64,48},{80,64},{96,80},{112,96},{128,112},... | collective-permute-start | bytes 1572872 | tf_op jit(solution)/shard_map/ppermute | solution.py:128

commit v4 on v3

--- a/solution.py
+++ b/solution.py
@@ -128,23 +128,10 @@
         lax.ppermute(deposit[1], "par", downward),
     )
 
-    def diagonal(plane_step, slab_step):
-        pairs = []
-        for p in range(plane_count):
-            for j in range(peer_count):
-                q, i = p - plane_step, j - slab_step
-                if 0 <= q < plane_count and 0 <= i < peer_count:
-                    pairs.append((q * peer_count + i, p * peer_count + j))
-        return pairs
-
-    from_above = [
-        lax.ppermute(deposit[0, -1:], ("par", "perp"), diagonal(1, 1)),
-        lax.ppermute(deposit[1, -1:], ("par", "perp"), diagonal(-1, 1)),
-    ]
-    from_below = [
-        lax.ppermute(deposit[0, :1], ("par", "perp"), diagonal(1, -1)),
-        lax.ppermute(deposit[1, :1], ("par", "perp"), diagonal(-1, -1)),
-    ]
+    forward = [(i, i + 1) for i in range(peer_count - 1)]
+    backward = [(i + 1, i) for i in range(peer_count - 1)]
+    from_above = lax.ppermute(jnp.stack([m[-1:] for m in mapped]), "perp", forward)
+    from_below = lax.ppermute(jnp.stack([m[:1] for m in mapped]), "perp", backward)
     chunk_rows = row_count // plane_count
     sides = []
     for f in range(field_count):

time: 272 us -> 264 us (0.971)
  starting transfers between devices: 40.4 us -> 28.3 us
  blocking collectives: 140 us -> 146 us
  local copies, waits for them, and re-layouts: 18.9 us -> 12.9 us
  waiting for transfers between devices: 52.1 us -> 55.5 us
    ppermute x4 -> x2, starting transfers between devices: 21.4 us -> 7.56 us  [the longest x1 5.64 us: local(): lax.ppermute(jnp.stack([m[:1] for m in mapped]), 'perp', backward)]
    all_to_all x1, blocking collectives: 79.3 us -> 85.9 us  [local(): lax.all_to_all(right_side, 'par', split_axis=0, concat_axis=0, tiled=True)]
    ppermute x4 -> x2, waiting for transfers between devices: 0.01 us -> 5.07 us  [the longest x1 5.07 us: local(): lax.ppermute(jnp.stack([m[-1:] for m in mapped]), 'perp', forward)]
    ppermute x1, waiting for transfers between devices: 3.1 us -> 0.01 us  [local(): lax.ppermute(deposit[1], 'par', downward)]
  transfers between devices with their start and end apart: 8 -> 6, of which waited for: 2 -> 3; matrix products, arithmetic and copies ran while one was open for 8% -> 7% of each run, Pallas kernels for 0% -> 0%
where the time goes in v4:
time: 264 us; the launch traced here: 263 us
  blocking collectives  146 us (55%)
  waiting for transfers between devices  55.5 us (21%)
  starting transfers between devices  28.3 us (11%)
  local copies, waits for them, and re-layouts  12.9 us (5%)
  matrix products  12.8 us (5%)
  other arithmetic  4.18 us (2%)
    all_to_all x1, blocking collectives, local(): lax.all_to_all(right_side, 'par', split_axis=0, concat_axis=0, tiled=True)  85.9 us
    all_to_all x1, blocking collectives, local(): lax.all_to_all(solved, 'par', split_axis=0, concat_axis=0, tiled=True)  60.4 us
    all_to_all x1, waiting for transfers between devices, local(): lax.all_to_all(packed, 'perp', split_axis=0, concat_axis=0, tiled=True)  49 us
    all_to_all x1, starting transfers between devices, local(): lax.all_to_all(slot_target.transpose(1, 2, 0), 'perp', split_axis=0, conc...  9.16 us
    all_to_all x1, starting transfers between devices, local(): lax.all_to_all(packed, 'perp', split_axis=0, concat_axis=0, tiled=True)  7.21 us
    dot_general x1, matrix products, local(): jnp.einsum('dtk,kij->dtij', landing, moved_tiles.reshape(-1, TILE, TILE),...  6.03 us
    ppermute x1, starting transfers between devices, local(): lax.ppermute(jnp.stack([m[:1] for m in mapped]), 'perp', backward)  5.64 us
  transfers between devices with their start and end apart: 6, of which 3 were waited for; matrix products, arithmetic and copies ran while one was open for 7% of the time, Pallas kernels for 0%

profile of v4, /device:TPU:6, one launch (start us, length us, event | category | flops | bytes accessed | tf_op | source)
XLA Modules:
  0.0 262.8 jit_solution(14315716018713773456)
XLA Ops:
  0.0 0.0 copy-start
  0.0 0.0 copy-start.1
  0.0 0.8 broadcast_add_fusion
  0.8 0.8 iota_compare_fusion.1
  1.6 1.0 convert_reduce_fusion
  2.5 0.1 select_reduce_fusion
  2.6 0.7 copy.38
  3.3 9.2 %all-to-all-start = ((s32[16,2,2]{1,2,0:T(2,128)}), s32[16,2,2]{1,2,0:T(2,128)S(1)}, u32[]{:S(2)}, u32[]{:S(2)}) async-start(s32[16,2,2]{1,2,0:T(2,128)} %copy.38), calls=%async_computation | async-start | bytes 32768 | tf_op jit(solution)/shard_map/all_to_all | solution.py:111
  12.5 0.8 iota_compare_fusion
  13.3 0.8 slice_reduce_fusion
  14.0 0.1 reshape.111
  14.1 0.1 reshape.103
  14.2 0.0 copy-done
  14.2 0.6 gather_fusion.1
  14.9 1.6 gather_fusion
  16.4 0.0 copy-done.1
  16.4 1.5 reshape_squeeze.3
  17.9 1.3 copy.40
  19.3 0.1 broadcast_and_fusion
  19.4 2.4 fusion.32
  21.7 2.3 convolution_bitcast_fusion.1
  24.0 2.1 convolution_bitcast_fusion
  26.2 3.2 %copy.42 = f32[16,2,2,128,128]{4,3,2,1,0:T(8,128)} copy(f32[16,2,2,128,128]{4,0,3,2,1:T(8,128)S(1)} %convolution_bitcast_fusion) | data formatting | bytes 8388608 | tf_op jit(solution)/shard_map/pcdk,kij->pcdij/dot_general | solution.py:108
  29.4 0.0 all-to-all-done
  29.4 7.2 %all-to-all-start.1 = ((f32[16,2,2,128,128]{4,3,2,1,0:T(8,128)}), f32[16,2,2,128,128]{4,3,2,1,0:T(8,128)}, u32[]{:S(2)}, u32[]{:S(2)}) async-start(f32[16,2,2,128,128]{4,3,2,1,0:T(8,128)} %copy.42), calls=%async_computation.1 | async-start | bytes 8388608 | tf_op jit(solution)/shard_map/all_to_all | solution.py:109
  36.6 0.1 and.71
  36.8 0.2 copy.39
  37.0 0.1 eq.118
  37.1 0.1 broadcast_compare_fusion
  37.2 49.0 %all-to-all-done.1 = f32[16,2,2,128,128]{4,3,2,1,0:T(8,128)} async-done(((f32[16,2,2,128,128]{4,3,2,1,0:T(8,128)}), f32[16,2,2,128,128]{4,3,2,1,0:T(8,128)}, u32[]{:S(2)}, u32[]{:S(2)}) %all-to-all-start.1) | async-done | bytes 4194336 | tf_op jit(solution)/shard_map/all_to_all | solution.py:109
  86.2 6.0 %fusion.2 = f32[2,4,128,2,128]{4,1,2,3,0:T(4,128)S(1)} fusion(f32[64,128,128,1,1]{2,1,0,4,3:T(8,128)} %bitcast.16, pred[2,64]{1,0:T(4,128)(4,1)S(1)} %and.71, pred[4,2,64]{2,0,1:T(4,128)(4,1)S(1)} %broadcast_compare_fusion), kind=kOutput, calls=%fused_computation.5 | convolution fusion | flops 201327616 | bytes 5243520 | tf_op jit(solution)/shard_map/dtk,kij->dtij/dot_general | solution.py:119
  92.2 0.1 fusion.27
  92.3 0.4 copy.45
  92.7 1.3 collective-permute-start.1
  94.0 0.4 copy.44
  94.5 3.1 %collective-permute-start = (f32[512,256]{1,0:T(8,128)S(1)}, f32[512,256]{1,0:T(8,128)S(1)}, u32[]{:S(2)}, u32[]{:S(2)}) collective-permute-start(f32[512,256]{1,0:T(8,128)S(1)} %bitcast.80), channel_id=1, source_target_pairs={{0,16},{16,32},{32,48},{48,64},{64,80},{80,96},{96,112},{112,128},... | collective-permute-start | bytes 1572872 | tf_op jit(solution)/shard_map/ppermute | solution.py:127
  97.5 0.0 collective-permute-done.1
  97.6 1.5 collective-permute-done
  99.0 5.6 %collective-permute-start.2 = (f32[2,1,256]{2,1,0:T(1,128)S(1)}, f32[2,1,256]{2,1,0:T(1,128)S(1)}, u32[]{:S(2)}, u32[]{:S(2)}) collective-permute-start(f32[2,1,256]{2,1,0:T(1,128)S(1)} %pad_maximum_fusion.1), channel_id=1, source_target_pairs={{1,0},{2,1},{3,2},{4,3},{5,4},{6,5},{7,6},{8,7},{9,8},{10,9},{11,1... | collective-permute-start | bytes 6152 | tf_op jit(solution)/shard_map/ppermute | solution.py:134
  104.7 1.9 collective-permute-start.3
  106.6 0.1 fusion.29
  106.7 0.2 fusion.28
  106.9 0.1 fusion.31
  107.0 0.2 fusion.30
  107.2 0.0 collective-permute-done.2
  107.2 5.1 %collective-permute-done.3 = f32[2,1,256]{2,1,0:T(1,128)S(1)} collective-permute-done((f32[2,1,256]{2,1,0:T(1,128)S(1)}, f32[2,1,256]{2,1,0:T(1,128)S(1)}, u32[]{:S(2)}, u32[]{:S(2)}) %collective-permute-start.3) | collective-permute-done | bytes 2080 | tf_op jit(solution)/shard_map/ppermute | solution.py:133
  112.3 0.5 fusion.11
  112.8 0.1 pad_maximum_fusion
  112.9 85.9 %all_to_all.20.rhs_ref = f32[32,2,16,256]{3,2,1,0:T(8,128)} all-to-all(f32[32,2,16,256]{3,2,1,0:T(8,128)S(1)} %pad_maximum_fusion), channel_id=1, replica_groups=mesh['par'=32,'perp'=16] {'par'}, dimensions={0} | all-to-all | bytes 2097152 | tf_op jit(solution)/shard_map/all_to_all | solution.py:144
  198.8 2.6 shard_map.64
  201.4 60.4 %all_to_all.21 = f32[32,2,16,256]{3,2,1,0:T(8,128)S(1)} all-to-all(f32[32,2,16,256]{3,2,1,0:T(8,128)} %shard_map.64), channel_id=1, replica_groups=mesh['par'=32,'perp'=16] {'par'}, dimensions={0} | all-to-all | bytes 2097152 | tf_op jit(solution)/shard_map/all_to_all | solution.py:146
  261.8 1.1 copy.46
  (16 shorter events, 0.2 us)
Async XLA Ops:
  0.0 14.2 %copy-start = (f32[8,128,128]{2,1,0:T(8,128)S(1)}, f32[8,128,128]{2,1,0:T(8,128)}, u32[]{:S(2)}) copy-start(f32[8,128,128]{2,1,0:T(8,128)} %param.7) | copy-start | bytes 1572868
  0.0 16.4 %copy-start.1 = (f32[2,1,512,256]{3,2,1,0:T(8,128)S(1)}, f32[2,1,512,256]{3,2,1,0:T(8,128)}, u32[]{:S(2)}) copy-start(f32[2,1,512,256]{3,2,1,0:T(8,128)} %param.6) | copy-start | bytes 3145732
  3.3 26.1 %all-to-all-start = ((s32[16,2,2]{1,2,0:T(2,128)}), s32[16,2,2]{1,2,0:T(2,128)S(1)}, u32[]{:S(2)}, u32[]{:S(2)}) async-start(s32[16,2,2]{1,2,0:T(2,128)} %copy.38), calls=%async_computation | async-start | bytes 32768 | tf_op jit(solution)/shard_map/all_to_all | solution.py:111
  29.4 56.7 %all-to-all-start.1 = ((f32[16,2,2,128,128]{4,3,2,1,0:T(8,128)}), f32[16,2,2,128,128]{4,3,2,1,0:T(8,128)}, u32[]{:S(2)}, u32[]{:S(2)}) async-start(f32[16,2,2,128,128]{4,3,2,1,0:T(8,128)} %copy.42), calls=%async_computation.1 | async-start | bytes 8388608 | tf_op jit(solution)/shard_map/all_to_all | solution.py:109
  92.7 4.8 %collective-permute-start.1 = (f32[512,256]{1,0:T(8,128)S(1)}, f32[512,256]{1,0:T(8,128)S(1)}, u32[]{:S(2)}, u32[]{:S(2)}) collective-permute-start(f32[512,256]{1,0:T(8,128)S(1)} %bitcast.79), channel_id=1, source_target_pairs={{16,0},{32,16},{48,32},{64,48},{80,64},{96,80},{112,96},{128,112},... | collective-permute-start | bytes 1572872 | tf_op jit(solution)/shard_map/ppermute | solution.py:128
  94.5 4.6 %collective-permute-start = (f32[512,256]{1,0:T(8,128)S(1)}, f32[512,256]{1,0:T(8,128)S(1)}, u32[]{:S(2)}, u32[]{:S(2)}) collective-permute-start(f32[512,256]{1,0:T(8,128)S(1)} %bitcast.80), channel_id=1, source_target_pairs={{0,16},{16,32},{32,48},{48,64},{64,80},{80,96},{96,112},{112,128},... | collective-permute-start | bytes 1572872 | tf_op jit(solution)/shard_map/ppermute | solution.py:127
  99.0 8.2 %collective-permute-start.2 = (f32[2,1,256]{2,1,0:T(1,128)S(1)}, f32[2,1,256]{2,1,0:T(1,128)S(1)}, u32[]{:S(2)}, u32[]{:S(2)}) collective-permute-start(f32[2,1,256]{2,1,0:T(1,128)S(1)} %pad_maximum_fusion.1), channel_id=1, source_target_pairs={{1,0},{2,1},{3,2},{4,3},{5,4},{6,5},{7,6},{8,7},{9,8},{10,9},{11,1... | collective-permute-start | bytes 6152 | tf_op jit(solution)/shard_map/ppermute | solution.py:134
  104.7 7.6 %collective-permute-start.3 = (f32[2,1,256]{2,1,0:T(1,128)S(1)}, f32[2,1,256]{2,1,0:T(1,128)S(1)}, u32[]{:S(2)}, u32[]{:S(2)}) collective-permute-start(f32[2,1,256]{2,1,0:T(1,128)S(1)} %pad_maximum_fusion.2), channel_id=1, source_target_pairs={{0,1},{1,2},{2,3},{3,4},{4,5},{5,6},{6,7},{7,8},{8,9},{9,10},{10,1... | collective-permute-start | bytes 6152 | tf_op jit(solution)/shard_map/ppermute | solution.py:133

commit v5 on v4

--- a/solution.py
+++ b/solution.py
@@ -85,13 +85,30 @@
     plane_count = lax.axis_size("par")
     field_count, _, row_count, col_count = fields.shape
     local_pair = fields[:, 0]
-    tile_set = split_tiles(local_pair)
+    upward = [(i, i + 1) for i in range(plane_count - 1)]
+    downward = [(i + 1, i) for i in range(plane_count - 1)]
+    indices = jnp.concatenate(
+        [dest_slab[:, 0], dest_tile[:, 0, :, None], tile_blocks[:, 0]], axis=2
+    )
+    source_pair = jnp.stack(
+        (
+            lax.ppermute(local_pair[0], "par", upward),
+            lax.ppermute(local_pair[1], "par", downward),
+        )
+    )
+    source_indices = jnp.stack(
+        (
+            lax.ppermute(indices[0], "par", upward),
+            lax.ppermute(indices[1], "par", downward),
+        )
+    )
+    tile_set = split_tiles(source_pair)
     tile_count = tile_set.shape[1]
     capacity = max(2, (tile_count + peer_count - 1) // peer_count)
-    dest_slabs = dest_slab[:, 0, :, 0]
-    target = dest_tile[:, 0, :]
-    left_index = tile_blocks[:, 0, :, 0]
-    right_index = tile_blocks[:, 0, :, 1]
+    dest_slabs = source_indices[:, :, 0]
+    target = source_indices[:, :, 1]
+    left_index = source_indices[:, :, 2]
+    right_index = source_indices[:, :, 3]
 
     left_block = jnp.take(weight_bank, left_index, axis=0, mode="clip")
     right_block = jnp.take(weight_bank, right_index, axis=0, mode="clip")
@@ -121,13 +138,7 @@
     )
     deposit = join_tiles(summed, row_count, col_count)
 
-    upward = [(i, i + 1) for i in range(plane_count - 1)]
-    downward = [(i + 1, i) for i in range(plane_count - 1)]
-    mapped = (
-        lax.ppermute(deposit[0], "par", upward),
-        lax.ppermute(deposit[1], "par", downward),
-    )
-
+    mapped = (deposit[0], deposit[1])
     forward = [(i, i + 1) for i in range(peer_count - 1)]
     backward = [(i + 1, i) for i in range(peer_count - 1)]
     from_above = lax.ppermute(jnp.stack([m[-1:] for m in mapped]), "perp", forward)

time: 264 us -> 268 us (1.015)
  waiting for transfers between devices: 55.5 us -> 64.3 us
  blocking collectives: 146 us -> 138 us
  starting transfers between devices: 28.3 us -> 32.9 us
    all_to_all x1, waiting for transfers between devices: 49 us -> 58.6 us  [local(): lax.all_to_all(packed, 'perp', split_axis=0, concat_axis=0, tiled=True)]
    all_to_all x1, blocking collectives: 85.9 us -> 77.7 us  [local(): lax.all_to_all(right_side, 'par', split_axis=0, concat_axis=0, tiled=True)]
    ppermute x2 -> x4, starting transfers between devices: 4.36 us -> 9.82 us  [the longest x1 5.51 us: local(): lax.ppermute(local_pair[0], 'par', upward)]
  transfers between devices with their start and end apart: 6 -> 8, of which waited for: 3 -> 2; matrix products, arithmetic and copies ran while one was open for 7% -> 7% of each run, Pallas kernels for 0% -> 0%
where the time goes in v5:
time: 268 us; the launch traced here: 267 us
  blocking collectives  138 us (51%)
  waiting for transfers between devices  64.3 us (24%)
  starting transfers between devices  32.9 us (12%)
  local copies, waits for them, and re-layouts  13.9 us (5%)
  matrix products  11.6 us (4%)
  other arithmetic  3.58 us (1%)
    all_to_all x1, blocking collectives, local(): lax.all_to_all(right_side, 'par', split_axis=0, concat_axis=0, tiled=True)  77.7 us
    all_to_all x1, blocking collectives, local(): lax.all_to_all(solved, 'par', split_axis=0, concat_axis=0, tiled=True)  60.4 us
    all_to_all x1, waiting for transfers between devices, local(): lax.all_to_all(packed, 'perp', split_axis=0, concat_axis=0, tiled=True)  58.6 us
    all_to_all x1, starting transfers between devices, local(): lax.all_to_all(slot_target.transpose(1, 2, 0), 'perp', split_axis=0, conc...  7.43 us
    all_to_all x1, starting transfers between devices, local(): lax.all_to_all(packed, 'perp', split_axis=0, concat_axis=0, tiled=True)  7.22 us
    ppermute x1, starting transfers between devices, local(): lax.ppermute(jnp.stack([m[:1] for m in mapped]), 'perp', backward)  6.5 us
    dot_general x1, matrix products, local(): jnp.einsum('dtk,kij->dtij', landing, moved_tiles.reshape(-1, TILE, TILE),...  6.03 us
    ppermute x1, waiting for transfers between devices, local(): lax.ppermute(jnp.stack([m[-1:] for m in mapped]), 'perp', forward)  5.64 us
  transfers between devices with their start and end apart: 8, of which 2 were waited for; matrix products, arithmetic and copies ran while one was open for 7% of the time, Pallas kernels for 0%

profile of v5, /device:TPU:6, one launch (start us, length us, event | category | flops | bytes accessed | tf_op | source)
XLA Modules:
  0.0 267.2 jit_solution(7078466920315052084)
XLA Ops:
  0.0 0.0 copy-start
  0.0 0.8 pad_add_fusion
  0.8 1.7 collective-permute-start
  2.5 1.3 collective-permute-start.1
  3.8 2.1 slice_bitcast_fusion.1
  5.9 5.5 %collective-permute-start.2 = (f32[512,256]{1,0:T(8,128)S(1)}, f32[512,256]{1,0:T(8,128)}, u32[]{:S(2)}, u32[]{:S(2)}) collective-permute-start(f32[512,256]{1,0:T(8,128)S(1)} %get-tuple-element.11), channel_id=1, source_target_pairs={{0,16},{16,32},{32,48},{48,64},{64,80},{80,96},{96,112},{112,128},... | collective-permute-start | bytes 1572872 | tf_op jit(solution)/shard_map/ppermute | solution.py:95
  11.4 1.3 collective-permute-start.3
  12.7 0.0 collective-permute-done
  12.7 0.0 collective-permute-done.1
  12.8 0.1 iota_compare_fusion.1
  12.8 0.2 convert_reduce_fusion
  13.1 0.1 reshape.113
  13.1 0.1 reshape.105
  13.2 0.1 select_reduce_fusion
  13.3 0.7 copy.50
  14.0 7.4 %all-to-all-start = ((s32[16,2,2]{1,2,0:T(2,128)}), s32[16,2,2]{1,2,0:T(2,128)S(1)}, u32[]{:S(2)}, u32[]{:S(2)}) async-start(s32[16,2,2]{1,2,0:T(2,128)} %copy.50), calls=%async_computation | async-start | bytes 32768 | tf_op jit(solution)/shard_map/all_to_all | solution.py:128
  21.5 0.0 copy-done
  21.5 0.6 gather_fusion.1
  22.1 0.6 gather_fusion
  22.7 0.1 iota_compare_fusion
  22.8 0.1 broadcast_and_fusion
  22.9 0.0 collective-permute-done.2
  22.9 1.3 stack.42
  24.2 0.0 collective-permute-done.3
  24.2 2.1 stack.43
  26.3 1.5 maximum_bitcast_fusion
  27.8 0.1 copy.52
  27.9 1.2 fusion.38
  29.1 2.3 convolution_bitcast_fusion.1
  31.4 2.1 convolution_bitcast_fusion
  33.5 3.2 %copy.54 = f32[16,2,2,128,128]{4,3,2,1,0:T(8,128)} copy(f32[16,2,2,128,128]{4,0,3,2,1:T(8,128)S(1)} %convolution_bitcast_fusion) | data formatting | bytes 8388608 | tf_op jit(solution)/shard_map/pcdk,kij->pcdij/dot_general | solution.py:125
  36.8 0.0 all-to-all-done
  36.8 7.2 %all-to-all-start.1 = ((f32[16,2,2,128,128]{4,3,2,1,0:T(8,128)}), f32[16,2,2,128,128]{4,3,2,1,0:T(8,128)}, u32[]{:S(2)}, u32[]{:S(2)}) async-start(f32[16,2,2,128,128]{4,3,2,1,0:T(8,128)} %copy.54), calls=%async_computation.1 | async-start | bytes 8388608 | tf_op jit(solution)/shard_map/all_to_all | solution.py:126
  44.0 0.1 and.71
  44.1 0.2 copy.51
  44.3 0.1 eq.118
  44.5 0.1 broadcast_compare_fusion
  44.5 58.6 %all-to-all-done.1 = f32[16,2,2,128,128]{4,3,2,1,0:T(8,128)} async-done(((f32[16,2,2,128,128]{4,3,2,1,0:T(8,128)}), f32[16,2,2,128,128]{4,3,2,1,0:T(8,128)}, u32[]{:S(2)}, u32[]{:S(2)}) %all-to-all-start.1) | async-done | bytes 4194336 | tf_op jit(solution)/shard_map/all_to_all | solution.py:126
  103.2 6.0 %fusion.2 = f32[2,4,128,2,128]{4,1,2,3,0:T(4,128)S(1)} fusion(f32[64,128,128,1,1]{2,1,0,4,3:T(8,128)} %bitcast.26, pred[2,64]{1,0:T(4,128)(4,1)S(1)} %and.71, pred[4,2,64]{2,0,1:T(4,128)(4,1)S(1)} %broadcast_compare_fusion), kind=kOutput, calls=%fused_computation.5 | convolution fusion | flops 201327616 | bytes 5243520 | tf_op jit(solution)/shard_map/dtk,kij->dtij/dot_general | solution.py:136
  109.2 0.1 fusion.33
  109.3 0.4 copy.56
  109.7 0.4 copy.57
  110.2 0.0 copy-start.1
  110.2 0.2 fusion.35
  110.4 0.3 fusion.34
  110.7 6.5 %collective-permute-start.4 = (f32[2,1,256]{2,1,0:T(1,128)S(1)}, f32[2,1,256]{2,1,0:T(1,128)S(1)}, u32[]{:S(2)}, u32[]{:S(2)}) collective-permute-start(f32[2,1,256]{2,1,0:T(1,128)S(1)} %pad_maximum_fusion.1), channel_id=1, source_target_pairs={{1,0},{2,1},{3,2},{4,3},{5,4},{6,5},{7,6},{8,7},{9,8},{10,9},{11,1... | collective-permute-start | bytes 6152 | tf_op jit(solution)/shard_map/ppermute | solution.py:145
  117.3 1.9 collective-permute-start.5
  119.2 0.0 collective-permute-done.4
  119.2 5.6 %collective-permute-done.5 = f32[2,1,256]{2,1,0:T(1,128)S(1)} collective-permute-done((f32[2,1,256]{2,1,0:T(1,128)S(1)}, f32[2,1,256]{2,1,0:T(1,128)S(1)}, u32[]{:S(2)}, u32[]{:S(2)}) %collective-permute-start.5) | collective-permute-done | bytes 2080 | tf_op jit(solution)/shard_map/ppermute | solution.py:144
  124.9 0.0 copy-done.1
  124.9 0.5 fusion.11
  125.4 0.1 pad_maximum_fusion
  125.5 77.7 %all_to_all.20.rhs_ref = f32[32,2,16,256]{3,2,1,0:T(8,128)} all-to-all(f32[32,2,16,256]{3,2,1,0:T(8,128)S(1)} %pad_maximum_fusion), channel_id=1, replica_groups=mesh['par'=32,'perp'=16] {'par'}, dimensions={0} | all-to-all | bytes 2097152 | tf_op jit(solution)/shard_map/all_to_all | solution.py:155
  203.2 2.6 shard_map.64
  205.8 60.4 %all_to_all.21 = f32[32,2,16,256]{3,2,1,0:T(8,128)S(1)} all-to-all(f32[32,2,16,256]{3,2,1,0:T(8,128)} %shard_map.64), channel_id=1, replica_groups=mesh['par'=32,'perp'=16] {'par'}, dimensions={0} | all-to-all | bytes 2097152 | tf_op jit(solution)/shard_map/all_to_all | solution.py:157
  266.2 1.1 copy.58
  (17 shorter events, 0.2 us)
Async XLA Ops:
  0.0 21.5 %copy-start = (f32[8,128,128]{2,1,0:T(8,128)S(1)}, f32[8,128,128]{2,1,0:T(8,128)}, u32[]{:S(2)}) copy-start(f32[8,128,128]{2,1,0:T(8,128)} %param.7) | copy-start | bytes 1572868
  0.8 11.9 %collective-permute-start = (s32[8,4]{0,1:T(4,128)S(1)}, s32[8,4]{0,1:T(4,128)S(1)}, u32[]{:S(2)}, u32[]{:S(2)}) collective-permute-start(s32[8,4]{0,1:T(4,128)S(1)} %get-tuple-element.27), channel_id=1, source_target_pairs={{0,16},{16,32},{32,48},{48,64},{64,80},{80,96},{96,112},{112,128},... | collective-permute-start | bytes 392 | tf_op jit(solution)/shard_map/ppermute | solution.py:101
  2.5 10.2 %collective-permute-start.1 = (s32[8,4]{0,1:T(4,128)S(1)}, s32[8,4]{0,1:T(4,128)S(1)}, u32[]{:S(2)}, u32[]{:S(2)}) collective-permute-start(s32[8,4]{0,1:T(4,128)S(1)} %get-tuple-element.28), channel_id=1, source_target_pairs={{16,0},{32,16},{48,32},{64,48},{80,64},{96,80},{112,96},{128,112},... | collective-permute-start | bytes 392 | tf_op jit(solution)/shard_map/ppermute | solution.py:102
  5.9 17.0 %collective-permute-start.2 = (f32[512,256]{1,0:T(8,128)S(1)}, f32[512,256]{1,0:T(8,128)}, u32[]{:S(2)}, u32[]{:S(2)}) collective-permute-start(f32[512,256]{1,0:T(8,128)S(1)} %get-tuple-element.11), channel_id=1, source_target_pairs={{0,16},{16,32},{32,48},{48,64},{64,80},{80,96},{96,112},{112,128},... | collective-permute-start | bytes 1572872 | tf_op jit(solution)/shard_map/ppermute | solution.py:95
  11.4 12.8 %collective-permute-start.3 = (f32[512,256]{1,0:T(8,128)}, f32[512,256]{1,0:T(8,128)}, u32[]{:S(2)}, u32[]{:S(2)}) collective-permute-start(f32[512,256]{1,0:T(8,128)} %get-tuple-element.12), channel_id=1, source_target_pairs={{16,0},{32,16},{48,32},{64,48},{80,64},{96,80},{112,96},{128,112},... | collective-permute-start | bytes 1572872 | tf_op jit(solution)/shard_map/ppermute | solution.py:96
  14.0 22.7 %all-to-all-start = ((s32[16,2,2]{1,2,0:T(2,128)}), s32[16,2,2]{1,2,0:T(2,128)S(1)}, u32[]{:S(2)}, u32[]{:S(2)}) async-start(s32[16,2,2]{1,2,0:T(2,128)} %copy.50), calls=%async_computation | async-start | bytes 32768 | tf_op jit(solution)/shard_map/all_to_all | solution.py:128
  36.8 66.4 %all-to-all-start.1 = ((f32[16,2,2,128,128]{4,3,2,1,0:T(8,128)}), f32[16,2,2,128,128]{4,3,2,1,0:T(8,128)}, u32[]{:S(2)}, u32[]{:S(2)}) async-start(f32[16,2,2,128,128]{4,3,2,1,0:T(8,128)} %copy.54), calls=%async_computation.1 | async-start | bytes 8388608 | tf_op jit(solution)/shard_map/all_to_all | solution.py:126
  110.2 14.7 %copy-start.1 = (f32[2,1,512,256]{3,2,1,0:T(8,128)S(1)}, f32[2,1,512,256]{3,2,1,0:T(8,128)}, u32[]{:S(2)}) copy-start(f32[2,1,512,256]{3,2,1,0:T(8,128)} %param.6) | copy-start | bytes 3145732
  110.7 8.5 %collective-permute-start.4 = (f32[2,1,256]{2,1,0:T(1,128)S(1)}, f32[2,1,256]{2,1,0:T(1,128)S(1)}, u32[]{:S(2)}, u32[]{:S(2)}) collective-permute-start(f32[2,1,256]{2,1,0:T(1,128)S(1)} %pad_maximum_fusion.1), channel_id=1, source_target_pairs={{1,0},{2,1},{3,2},{4,3},{5,4},{6,5},{7,6},{8,7},{9,8},{10,9},{11,1... | collective-permute-start | bytes 6152 | tf_op jit(solution)/shard_map/ppermute | solution.py:145
  117.3 7.6 %collective-permute-start.5 = (f32[2,1,256]{2,1,0:T(1,128)S(1)}, f32[2,1,256]{2,1,0:T(1,128)S(1)}, u32[]{:S(2)}, u32[]{:S(2)}) collective-permute-start(f32[2,1,256]{2,1,0:T(1,128)S(1)} %pad_maximum_fusion.2), channel_id=1, source_target_pairs={{0,1},{1,2},{2,3},{3,4},{4,5},{5,6},{6,7},{7,8},{8,9},{9,10},{10,1... | collective-permute-start | bytes 6152 | tf_op jit(solution)/shard_map/ppermute | solution.py:144

commit v6 on v4

--- a/solution.py
+++ b/solution.py
@@ -9,6 +9,7 @@
 
 
 PRECISE = lax.Precision.HIGHEST
+THREE_PASS = lax.Precision.HIGH
 KAPPA = 0.125
 
 
@@ -95,8 +96,8 @@
 
     left_block = jnp.take(weight_bank, left_index, axis=0, mode="clip")
     right_block = jnp.take(weight_bank, right_index, axis=0, mode="clip")
-    shifted = jnp.einsum("dsij,dsjk->dsik", left_block, tile_set, precision=PRECISE)
-    moved = jnp.einsum("dsik,dslk->dsil", shifted, right_block, precision=PRECISE)
+    shifted = jnp.einsum("dsij,dsjk->dsik", left_block, tile_set, precision=THREE_PASS)
+    moved = jnp.einsum("dsik,dslk->dsil", shifted, right_block, precision=THREE_PASS)
     moved = moved.reshape(field_count * tile_count, TILE, TILE)
 
     chosen = slot_labels(dest_slabs, peer_count, capacity)
@@ -105,7 +106,7 @@
     picker = picker.astype(jnp.float32).reshape(
         peer_count, capacity, field_count, field_count * tile_count
     )
-    packed = jnp.einsum("pcdk,kij->pcdij", picker, moved, precision=PRECISE)
+    packed = jnp.einsum("pcdk,kij->pcdij", picker, moved, precision=THREE_PASS)
     moved_tiles = lax.all_to_all(packed, "perp", split_axis=0, concat_axis=0, tiled=True)
     slot_target = jnp.sum(chosen.astype(jnp.int32) * (target[:, None, None, :] + 1), axis=3) - 1
     arrived_target = lax.all_to_all(
@@ -117,7 +118,7 @@
     landing = hit & same_field[:, None, None, None, :]
     landing = landing.astype(jnp.float32).reshape(field_count, tile_count, -1)
     summed = jnp.einsum(
-        "dtk,kij->dtij", landing, moved_tiles.reshape(-1, TILE, TILE), precision=PRECISE
+        "dtk,kij->dtij", landing, moved_tiles.reshape(-1, TILE, TILE), precision=THREE_PASS
     )
     deposit = join_tiles(summed, row_count, col_count)
 

time: 264 us -> 261 us (0.989)
  matrix products: 12.8 us -> 9.72 us
  transfers between devices with their start and end apart: 6 -> 6, of which waited for: 3 -> 3; matrix products, arithmetic and copies ran while one was open for 7% -> 6% of each run, Pallas kernels for 0% -> 0%
where the time goes in v6:
time: 261 us; the launch traced here: 260 us
  blocking collectives  147 us (56%)
  waiting for transfers between devices  55.5 us (21%)
  starting transfers between devices  28.3 us (11%)
  local copies, waits for them, and re-layouts  12.9 us (5%)
  matrix products  9.72 us (4%)
  other arithmetic  4.18 us (2%)
    all_to_all x1, blocking collectives, local(): lax.all_to_all(right_side, 'par', split_axis=0, concat_axis=0, tiled=True)  86.2 us
    all_to_all x1, blocking collectives, local(): lax.all_to_all(solved, 'par', split_axis=0, concat_axis=0, tiled=True)  60.4 us
    all_to_all x1, waiting for transfers between devices, local(): lax.all_to_all(packed, 'perp', split_axis=0, concat_axis=0, tiled=True)  49 us
    all_to_all x1, starting transfers between devices, local(): lax.all_to_all(slot_target.transpose(1, 2, 0), 'perp', split_axis=0, conc...  9.16 us
    all_to_all x1, starting transfers between devices, local(): lax.all_to_all(packed, 'perp', split_axis=0, concat_axis=0, tiled=True)  7.21 us
    ppermute x1, starting transfers between devices, local(): lax.ppermute(jnp.stack([m[:1] for m in mapped]), 'perp', backward)  5.64 us
  transfers between devices with their start and end apart: 6, of which 3 were waited for; matrix products, arithmetic and copies ran while one was open for 6% of the time, Pallas kernels for 0%

profile of v6, /device:TPU:6, one launch (start us, length us, event | category | flops | bytes accessed | tf_op | source)
XLA Modules:
  0.0 260.0 jit_solution(12040301873737159679)
XLA Ops:
  0.0 0.0 copy-start
  0.0 0.0 copy-start.1
  0.0 0.8 broadcast_add_fusion
  0.8 0.8 iota_compare_fusion.1
  1.6 1.0 convert_reduce_fusion
  2.5 0.1 select_reduce_fusion
  2.6 0.7 copy.38
  3.3 9.2 %all-to-all-start = ((s32[16,2,2]{1,2,0:T(2,128)}), s32[16,2,2]{1,2,0:T(2,128)S(1)}, u32[]{:S(2)}, u32[]{:S(2)}) async-start(s32[16,2,2]{1,2,0:T(2,128)} %copy.38), calls=%async_computation | async-start | bytes 32768 | tf_op jit(solution)/shard_map/all_to_all | solution.py:112
  12.5 0.8 iota_compare_fusion
  13.3 0.8 slice_reduce_fusion
  14.0 0.1 reshape.111
  14.1 0.1 reshape.103
  14.2 0.0 copy-done
  14.2 0.6 gather_fusion.1
  14.9 1.6 gather_fusion
  16.4 0.0 copy-done.1
  16.4 1.5 reshape_squeeze.3
  17.9 1.3 copy.40
  19.3 0.1 broadcast_and_fusion
  19.4 1.8 fusion.32
  21.2 1.2 convolution_bitcast_fusion.1
  22.4 1.5 convolution_bitcast_fusion
  23.9 3.2 %copy.42 = f32[16,2,2,128,128]{4,3,2,1,0:T(8,128)} copy(f32[16,2,2,128,128]{4,0,3,2,1:T(8,128)S(1)} %convolution_bitcast_fusion) | data formatting | bytes 8388608 | tf_op jit(solution)/shard_map/pcdk,kij->pcdij/dot_general | solution.py:109
  27.1 0.0 all-to-all-done
  27.1 7.2 %all-to-all-start.1 = ((f32[16,2,2,128,128]{4,3,2,1,0:T(8,128)}), f32[16,2,2,128,128]{4,3,2,1,0:T(8,128)}, u32[]{:S(2)}, u32[]{:S(2)}) async-start(f32[16,2,2,128,128]{4,3,2,1,0:T(8,128)} %copy.42), calls=%async_computation.1 | async-start | bytes 8388608 | tf_op jit(solution)/shard_map/all_to_all | solution.py:110
  34.4 0.1 and.71
  34.5 0.2 copy.39
  34.7 0.1 eq.118
  34.8 0.1 broadcast_compare_fusion
  34.9 49.0 %all-to-all-done.1 = f32[16,2,2,128,128]{4,3,2,1,0:T(8,128)} async-done(((f32[16,2,2,128,128]{4,3,2,1,0:T(8,128)}), f32[16,2,2,128,128]{4,3,2,1,0:T(8,128)}, u32[]{:S(2)}, u32[]{:S(2)}) %all-to-all-start.1) | async-done | bytes 4194336 | tf_op jit(solution)/shard_map/all_to_all | solution.py:110
  83.9 5.2 %fusion.2 = f32[2,4,128,2,128]{4,1,2,3,0:T(4,128)S(1)} fusion(f32[64,128,128,1,1]{2,1,0,4,3:T(8,128)} %bitcast.16, pred[2,64]{1,0:T(4,128)(4,1)S(1)} %and.71, pred[4,2,64]{2,0,1:T(4,128)(4,1)S(1)} %broadcast_compare_fusion), kind=kOutput, calls=%fused_computation.5 | convolution fusion | flops 100664320 | bytes 5243520 | tf_op jit(solution)/shard_map/dtk,kij->dtij/dot_general | solution.py:120
  89.1 0.1 fusion.27
  89.2 0.4 copy.45
  89.6 1.3 collective-permute-start.1
  90.9 0.4 copy.44
  91.4 3.1 %collective-permute-start = (f32[512,256]{1,0:T(8,128)S(1)}, f32[512,256]{1,0:T(8,128)S(1)}, u32[]{:S(2)}, u32[]{:S(2)}) collective-permute-start(f32[512,256]{1,0:T(8,128)S(1)} %bitcast.80), channel_id=1, source_target_pairs={{0,16},{16,32},{32,48},{48,64},{64,80},{80,96},{96,112},{112,128},... | collective-permute-start | bytes 1572872 | tf_op jit(solution)/shard_map/ppermute | solution.py:128
  94.5 0.0 collective-permute-done.1
  94.5 1.5 collective-permute-done
  96.0 5.6 %collective-permute-start.2 = (f32[2,1,256]{2,1,0:T(1,128)S(1)}, f32[2,1,256]{2,1,0:T(1,128)S(1)}, u32[]{:S(2)}, u32[]{:S(2)}) collective-permute-start(f32[2,1,256]{2,1,0:T(1,128)S(1)} %pad_maximum_fusion.1), channel_id=1, source_target_pairs={{1,0},{2,1},{3,2},{4,3},{5,4},{6,5},{7,6},{8,7},{9,8},{10,9},{11,1... | collective-permute-start | bytes 6152 | tf_op jit(solution)/shard_map/ppermute | solution.py:135
  101.6 1.9 collective-permute-start.3
  103.5 0.1 fusion.29
  103.6 0.2 fusion.28
  103.8 0.1 fusion.31
  103.9 0.2 fusion.30
  104.1 0.0 collective-permute-done.2
  104.1 5.1 %collective-permute-done.3 = f32[2,1,256]{2,1,0:T(1,128)S(1)} collective-permute-done((f32[2,1,256]{2,1,0:T(1,128)S(1)}, f32[2,1,256]{2,1,0:T(1,128)S(1)}, u32[]{:S(2)}, u32[]{:S(2)}) %collective-permute-start.3) | collective-permute-done | bytes 2080 | tf_op jit(solution)/shard_map/ppermute | solution.py:134
  109.2 0.5 fusion.11
  109.7 0.1 pad_maximum_fusion
  109.8 86.2 %all_to_all.20.rhs_ref = f32[32,2,16,256]{3,2,1,0:T(8,128)} all-to-all(f32[32,2,16,256]{3,2,1,0:T(8,128)S(1)} %pad_maximum_fusion), channel_id=1, replica_groups=mesh['par'=32,'perp'=16] {'par'}, dimensions={0} | all-to-all | bytes 2097152 | tf_op jit(solution)/shard_map/all_to_all | solution.py:145
  196.0 2.6 shard_map.64
  198.6 60.4 %all_to_all.21 = f32[32,2,16,256]{3,2,1,0:T(8,128)S(1)} all-to-all(f32[32,2,16,256]{3,2,1,0:T(8,128)} %shard_map.64), channel_id=1, replica_groups=mesh['par'=32,'perp'=16] {'par'}, dimensions={0} | all-to-all | bytes 2097152 | tf_op jit(solution)/shard_map/all_to_all | solution.py:147
  259.0 1.1 copy.46
  (16 shorter events, 0.2 us)
Async XLA Ops:
  0.0 14.2 %copy-start = (f32[8,128,128]{2,1,0:T(8,128)S(1)}, f32[8,128,128]{2,1,0:T(8,128)}, u32[]{:S(2)}) copy-start(f32[8,128,128]{2,1,0:T(8,128)} %param.7) | copy-start | bytes 1572868
  0.0 16.4 %copy-start.1 = (f32[2,1,512,256]{3,2,1,0:T(8,128)S(1)}, f32[2,1,512,256]{3,2,1,0:T(8,128)}, u32[]{:S(2)}) copy-start(f32[2,1,512,256]{3,2,1,0:T(8,128)} %param.6) | copy-start | bytes 3145732
  3.3 23.8 %all-to-all-start = ((s32[16,2,2]{1,2,0:T(2,128)}), s32[16,2,2]{1,2,0:T(2,128)S(1)}, u32[]{:S(2)}, u32[]{:S(2)}) async-start(s32[16,2,2]{1,2,0:T(2,128)} %copy.38), calls=%async_computation | async-start | bytes 32768 | tf_op jit(solution)/shard_map/all_to_all | solution.py:112
  27.1 56.8 %all-to-all-start.1 = ((f32[16,2,2,128,128]{4,3,2,1,0:T(8,128)}), f32[16,2,2,128,128]{4,3,2,1,0:T(8,128)}, u32[]{:S(2)}, u32[]{:S(2)}) async-start(f32[16,2,2,128,128]{4,3,2,1,0:T(8,128)} %copy.42), calls=%async_computation.1 | async-start | bytes 8388608 | tf_op jit(solution)/shard_map/all_to_all | solution.py:110
  89.6 4.8 %collective-permute-start.1 = (f32[512,256]{1,0:T(8,128)S(1)}, f32[512,256]{1,0:T(8,128)S(1)}, u32[]{:S(2)}, u32[]{:S(2)}) collective-permute-start(f32[512,256]{1,0:T(8,128)S(1)} %bitcast.79), channel_id=1, source_target_pairs={{16,0},{32,16},{48,32},{64,48},{80,64},{96,80},{112,96},{128,112},... | collective-permute-start | bytes 1572872 | tf_op jit(solution)/shard_map/ppermute | solution.py:129
  91.4 4.6 %collective-permute-start = (f32[512,256]{1,0:T(8,128)S(1)}, f32[512,256]{1,0:T(8,128)S(1)}, u32[]{:S(2)}, u32[]{:S(2)}) collective-permute-start(f32[512,256]{1,0:T(8,128)S(1)} %bitcast.80), channel_id=1, source_target_pairs={{0,16},{16,32},{32,48},{48,64},{64,80},{80,96},{96,112},{112,128},... | collective-permute-start | bytes 1572872 | tf_op jit(solution)/shard_map/ppermute | solution.py:128
  96.0 8.2 %collective-permute-start.2 = (f32[2,1,256]{2,1,0:T(1,128)S(1)}, f32[2,1,256]{2,1,0:T(1,128)S(1)}, u32[]{:S(2)}, u32[]{:S(2)}) collective-permute-start(f32[2,1,256]{2,1,0:T(1,128)S(1)} %pad_maximum_fusion.1), channel_id=1, source_target_pairs={{1,0},{2,1},{3,2},{4,3},{5,4},{6,5},{7,6},{8,7},{9,8},{10,9},{11,1... | collective-permute-start | bytes 6152 | tf_op jit(solution)/shard_map/ppermute | solution.py:135
  101.6 7.6 %collective-permute-start.3 = (f32[2,1,256]{2,1,0:T(1,128)S(1)}, f32[2,1,256]{2,1,0:T(1,128)S(1)}, u32[]{:S(2)}, u32[]{:S(2)}) collective-permute-start(f32[2,1,256]{2,1,0:T(1,128)S(1)} %pad_maximum_fusion.2), channel_id=1, source_target_pairs={{0,1},{1,2},{2,3},{3,4},{4,5},{5,6},{6,7},{7,8},{8,9},{9,10},{10,1... | collective-permute-start | bytes 6152 | tf_op jit(solution)/shard_map/ppermute | solution.py:134

commit v7 on v6

--- a/solution.py
+++ b/solution.py
@@ -70,6 +70,32 @@
     )(band_terms, rhs)
 
 
+def landing_kernel(label_ref, recv_ref, out_ref, acc_ref):
+    field_count = out_ref.shape[0]
+    tiles_across = out_ref.shape[2] // TILE
+    acc_ref[...] = jnp.zeros(acc_ref.shape, jnp.float32)
+    for k in range(recv_ref.shape[0]):
+        field = k % field_count
+        label = label_ref[k]
+        acc_ref[field, label] = acc_ref[field, label] + recv_ref[k]
+    for field in range(field_count):
+        for t in range(acc_ref.shape[1] - 1):
+            a, b = divmod(t, tiles_across)
+            out_ref[field, a * TILE:(a + 1) * TILE, b * TILE:(b + 1) * TILE] = acc_ref[field, t + 1]
+
+
+def land(labels, received, field_count, tile_count, row_count, col_count):
+    scalar = pl.BlockSpec(memory_space=pltpu.SMEM)
+    whole = pl.BlockSpec(memory_space=pltpu.VMEM)
+    return pl.pallas_call(
+        landing_kernel,
+        out_shape=jax.ShapeDtypeStruct((field_count, row_count, col_count), received.dtype),
+        in_specs=[scalar, whole],
+        out_specs=whole,
+        scratch_shapes=[pltpu.VMEM((field_count, tile_count + 1, TILE, TILE), jnp.float32)],
+    )(labels, received)
+
+
 def smooth_slab(plane, above_row, below_row):
     row_count, col_count = plane.shape
     zero_col = jnp.zeros((row_count, 1), plane.dtype)
@@ -113,14 +139,10 @@
         slot_target.transpose(1, 2, 0), "perp", split_axis=0, concat_axis=0, tiled=True
     )
 
-    position = jnp.arange(tile_count, dtype=jnp.int32)
-    hit = arrived_target[None, None] == position[None, :, None, None, None]
-    landing = hit & same_field[:, None, None, None, :]
-    landing = landing.astype(jnp.float32).reshape(field_count, tile_count, -1)
-    summed = jnp.einsum(
-        "dtk,kij->dtij", landing, moved_tiles.reshape(-1, TILE, TILE), precision=THREE_PASS
+    labels = jnp.clip(arrived_target.reshape(-1) + 1, 0, tile_count)
+    deposit = land(
+        labels, moved_tiles.reshape(-1, TILE, TILE), field_count, tile_count, row_count, col_count
     )
-    deposit = join_tiles(summed, row_count, col_count)
 
     upward = [(i, i + 1) for i in range(plane_count - 1)]
     downward = [(i + 1, i) for i in range(plane_count - 1)]

time: 261 us -> 259 us (level)
  blocking collectives: 147 us -> 138 us
  waiting for transfers between devices: 55.5 us -> 64.3 us
  matrix products: 9.72 us -> 4.54 us
  Pallas kernels: 2.57 us -> 6.31 us
    ppermute x1, waiting for transfers between devices: 0.01 us -> 10.4 us  [local(): lax.ppermute(deposit[1], 'par', downward)]
    all_to_all x1, blocking collectives: 86.2 us -> 77.8 us  [local(): lax.all_to_all(right_side, 'par', split_axis=0, concat_axis=0, tiled=True)]
    dot_general x1 -> x0, matrix products: 5.19 us -> none  [local(): jnp.einsum('dtk,kij->dtij', landing, moved_tiles.reshape(-1, TILE, TILE),...]
    pallas_call x0 -> x1, Pallas kernels: none -> 3.75 us  [land(): pl.pallas_call(landing_kernel, out_shape=jax.ShapeDtypeStruct((field_coun...]
  transfers between devices with their start and end apart: 6 -> 6, of which waited for: 3 -> 4; matrix products, arithmetic and copies ran while one was open for 6% -> 6% of each run, Pallas kernels for 0% -> 0%
where the time goes in v7:
time: 259 us
  blocking collectives  138 us (53%)
  waiting for transfers between devices  64.3 us (25%)
  starting transfers between devices  27.5 us (11%)
  local copies, waits for them, and re-layouts  13.6 us (5%)
  Pallas kernels  6.31 us (2%)
  matrix products  4.54 us (2%)
  other arithmetic  4.1 us (2%)
    all_to_all x1, blocking collectives, local(): lax.all_to_all(right_side, 'par', split_axis=0, concat_axis=0, tiled=True)  77.8 us
    all_to_all x1, blocking collectives, local(): lax.all_to_all(solved, 'par', split_axis=0, concat_axis=0, tiled=True)  60.4 us
    all_to_all x1, waiting for transfers between devices, local(): lax.all_to_all(packed, 'perp', split_axis=0, concat_axis=0, tiled=True)  48.7 us
    ppermute x1, waiting for transfers between devices, local(): lax.ppermute(deposit[1], 'par', downward)  10.4 us
    all_to_all x1, starting transfers between devices, local(): lax.all_to_all(slot_target.transpose(1, 2, 0), 'perp', split_axis=0, conc...  9.16 us
    all_to_all x1, starting transfers between devices, local(): lax.all_to_all(packed, 'perp', split_axis=0, concat_axis=0, tiled=True)  7.21 us
    ppermute x1, starting transfers between devices, local(): lax.ppermute(jnp.stack([m[:1] for m in mapped]), 'perp', backward)  6.56 us
  transfers between devices with their start and end apart: 6, of which 4 were waited for; matrix products, arithmetic and copies ran while one was open for 6% of the time, Pallas kernels for 0%

profile of v7, /device:TPU:6, one launch (start us, length us, event | category | flops | bytes accessed | tf_op | source)
XLA Modules:
  0.0 258.7 jit_solution(10850100587968734611)
XLA Ops:
  0.0 0.0 copy-start
  0.0 0.0 copy-start.1
  0.0 0.8 broadcast_add_fusion
  0.8 0.8 iota_compare_fusion.1
  1.6 1.0 convert_reduce_fusion
  2.5 0.1 select_reduce_fusion
  2.6 0.7 copy.34
  3.3 9.2 %all-to-all-start = ((s32[16,2,2]{1,2,0:T(2,128)}), s32[16,2,2]{1,2,0:T(2,128)S(1)}, u32[]{:S(2)}, u32[]{:S(2)}) async-start(s32[16,2,2]{1,2,0:T(2,128)} %copy.34), calls=%async_computation | async-start | bytes 32768 | tf_op jit(solution)/shard_map/all_to_all | solution.py:138
  12.5 0.8 iota_compare_fusion
  13.3 0.8 slice_reduce_fusion
  14.0 0.1 reshape.87
  14.1 0.1 reshape.79
  14.2 0.0 copy-done
  14.2 0.6 gather_fusion.1
  14.9 1.6 gather_fusion
  16.4 0.0 copy-done.1
  16.4 1.5 reshape_squeeze.3
  17.9 1.3 copy.37
  19.3 0.1 broadcast_and_fusion
  19.4 1.8 fusion.22
  21.2 1.2 convolution_bitcast_fusion.1
  22.4 1.5 convolution_bitcast_fusion
  23.9 3.2 %copy.39 = f32[16,2,2,128,128]{4,3,2,1,0:T(8,128)} copy(f32[16,2,2,128,128]{4,0,3,2,1:T(8,128)S(1)} %convolution_bitcast_fusion) | data formatting | bytes 8388608 | tf_op jit(solution)/shard_map/pcdk,kij->pcdij/dot_general | solution.py:135
  27.1 0.0 all-to-all-done
  27.1 7.2 %all-to-all-start.1 = ((f32[16,2,2,128,128]{4,3,2,1,0:T(8,128)}), f32[16,2,2,128,128]{4,3,2,1,0:T(8,128)}, u32[]{:S(2)}, u32[]{:S(2)}) async-start(f32[16,2,2,128,128]{4,3,2,1,0:T(8,128)} %copy.39), calls=%async_computation.1 | async-start | bytes 8388608 | tf_op jit(solution)/shard_map/all_to_all | solution.py:136
  34.4 0.1 copy.35
  34.5 0.1 copy.36
  34.6 0.7 min.12.label_ref
  35.2 48.7 %all-to-all-done.1 = f32[16,2,2,128,128]{4,3,2,1,0:T(8,128)} async-done(((f32[16,2,2,128,128]{4,3,2,1,0:T(8,128)}), f32[16,2,2,128,128]{4,3,2,1,0:T(8,128)}, u32[]{:S(2)}, u32[]{:S(2)}) %all-to-all-start.1) | async-done | bytes 4194336 | tf_op jit(solution)/shard_map/all_to_all | solution.py:136
  83.9 3.7 %shard_map.64 = f32[2,512,256]{2,1,0:T(8,128)} custom-call(s32[64]{0:T(128)} %min.12.label_ref, f32[64,128,128]{2,1,0:T(8,128)} %bitcast.13.recv_ref), custom_call_target="tpu_custom_call" | custom-call | tf_op jit(solution)/shard_map/pallas_call | solution.py:90
  87.6 1.3 slice_bitcast_fusion.1
  88.9 1.3 collective-permute-start
  90.2 1.3 collective-permute-start.1
  91.5 0.2 collective-permute-done
  91.7 10.4 %collective-permute-done.1 = f32[512,256]{1,0:T(8,128)S(1)} collective-permute-done((f32[512,256]{1,0:T(8,128)S(1)}, f32[512,256]{1,0:T(8,128)S(1)}, u32[]{:S(2)}, u32[]{:S(2)}) %collective-permute-start.1) | collective-permute-done | bytes 524320 | tf_op jit(solution)/shard_map/ppermute | solution.py:151
  102.1 6.6 %collective-permute-start.2 = (f32[2,1,256]{2,1,0:T(1,128)S(1)}, f32[2,1,256]{2,1,0:T(1,128)S(1)}, u32[]{:S(2)}, u32[]{:S(2)}) collective-permute-start(f32[2,1,256]{2,1,0:T(1,128)S(1)} %pad_maximum_fusion.1), channel_id=1, source_target_pairs={{1,0},{2,1},{3,2},{4,3},{5,4},{6,5},{7,6},{8,7},{9,8},{10,9},{11,1... | collective-permute-start | bytes 6152 | tf_op jit(solution)/shard_map/ppermute | solution.py:157
  108.7 1.9 collective-permute-start.3
  110.6 0.1 fusion.21
  110.7 0.2 fusion.20
  110.9 0.1 fusion.19
  111.0 0.2 fusion.18
  111.2 0.0 collective-permute-done.2
  111.2 5.1 %collective-permute-done.3 = f32[2,1,256]{2,1,0:T(1,128)S(1)} collective-permute-done((f32[2,1,256]{2,1,0:T(1,128)S(1)}, f32[2,1,256]{2,1,0:T(1,128)S(1)}, u32[]{:S(2)}, u32[]{:S(2)}) %collective-permute-start.3) | collective-permute-done | bytes 2080 | tf_op jit(solution)/shard_map/ppermute | solution.py:156
  116.3 0.5 fusion.6
  116.8 0.1 pad_maximum_fusion
  116.9 77.8 %all_to_all.20.rhs_ref = f32[32,2,16,256]{3,2,1,0:T(8,128)} all-to-all(f32[32,2,16,256]{3,2,1,0:T(8,128)S(1)} %pad_maximum_fusion), channel_id=1, replica_groups=mesh['par'=32,'perp'=16] {'par'}, dimensions={0} | all-to-all | bytes 2097152 | tf_op jit(solution)/shard_map/all_to_all | solution.py:167
  194.7 2.6 shard_map.65
  197.3 60.4 %all_to_all.21 = f32[32,2,16,256]{3,2,1,0:T(8,128)S(1)} all-to-all(f32[32,2,16,256]{3,2,1,0:T(8,128)} %shard_map.65), channel_id=1, replica_groups=mesh['par'=32,'perp'=16] {'par'}, dimensions={0} | all-to-all | bytes 2097152 | tf_op jit(solution)/shard_map/all_to_all | solution.py:169
  257.7 1.1 copy.40
  (13 shorter events, 0.1 us)
Async XLA Ops:
  0.0 14.2 %copy-start = (f32[8,128,128]{2,1,0:T(8,128)S(1)}, f32[8,128,128]{2,1,0:T(8,128)}, u32[]{:S(2)}) copy-start(f32[8,128,128]{2,1,0:T(8,128)} %param.7) | copy-start | bytes 1572868
  0.0 16.4 %copy-start.1 = (f32[2,1,512,256]{3,2,1,0:T(8,128)S(1)}, f32[2,1,512,256]{3,2,1,0:T(8,128)}, u32[]{:S(2)}) copy-start(f32[2,1,512,256]{3,2,1,0:T(8,128)} %param.6) | copy-start | bytes 3145732
  3.3 23.8 %all-to-all-start = ((s32[16,2,2]{1,2,0:T(2,128)}), s32[16,2,2]{1,2,0:T(2,128)S(1)}, u32[]{:S(2)}, u32[]{:S(2)}) async-start(s32[16,2,2]{1,2,0:T(2,128)} %copy.34), calls=%async_computation | async-start | bytes 32768 | tf_op jit(solution)/shard_map/all_to_all | solution.py:138
  27.1 56.8 %all-to-all-start.1 = ((f32[16,2,2,128,128]{4,3,2,1,0:T(8,128)}), f32[16,2,2,128,128]{4,3,2,1,0:T(8,128)}, u32[]{:S(2)}, u32[]{:S(2)}) async-start(f32[16,2,2,128,128]{4,3,2,1,0:T(8,128)} %copy.39), calls=%async_computation.1 | async-start | bytes 8388608 | tf_op jit(solution)/shard_map/all_to_all | solution.py:136
  88.9 2.8 %collective-permute-start = (f32[512,256]{1,0:T(8,128)S(1)}, f32[512,256]{1,0:T(8,128)S(1)}, u32[]{:S(2)}, u32[]{:S(2)}) collective-permute-start(f32[512,256]{1,0:T(8,128)S(1)} %get-tuple-element.9), channel_id=1, source_target_pairs={{0,16},{16,32},{32,48},{48,64},{64,80},{80,96},{96,112},{112,128},... | collective-permute-start | bytes 1572872 | tf_op jit(solution)/shard_map/ppermute | solution.py:150
  90.2 11.9 %collective-permute-start.1 = (f32[512,256]{1,0:T(8,128)S(1)}, f32[512,256]{1,0:T(8,128)S(1)}, u32[]{:S(2)}, u32[]{:S(2)}) collective-permute-start(f32[512,256]{1,0:T(8,128)S(1)} %get-tuple-element.10), channel_id=1, source_target_pairs={{16,0},{32,16},{48,32},{64,48},{80,64},{96,80},{112,96},{128,112},... | collective-permute-start | bytes 1572872 | tf_op jit(solution)/shard_map/ppermute | solution.py:151
  102.1 9.1 %collective-permute-start.2 = (f32[2,1,256]{2,1,0:T(1,128)S(1)}, f32[2,1,256]{2,1,0:T(1,128)S(1)}, u32[]{:S(2)}, u32[]{:S(2)}) collective-permute-start(f32[2,1,256]{2,1,0:T(1,128)S(1)} %pad_maximum_fusion.1), channel_id=1, source_target_pairs={{1,0},{2,1},{3,2},{4,3},{5,4},{6,5},{7,6},{8,7},{9,8},{10,9},{11,1... | collective-permute-start | bytes 6152 | tf_op jit(solution)/shard_map/ppermute | solution.py:157
  108.7 7.6 %collective-permute-start.3 = (f32[2,1,256]{2,1,0:T(1,128)S(1)}, f32[2,1,256]{2,1,0:T(1,128)S(1)}, u32[]{:S(2)}, u32[]{:S(2)}) collective-permute-start(f32[2,1,256]{2,1,0:T(1,128)S(1)} %pad_maximum_fusion.2), channel_id=1, source_target_pairs={{0,1},{1,2},{2,3},{3,4},{4,5},{5,6},{6,7},{7,8},{8,9},{9,10},{10,1... | collective-permute-start | bytes 6152 | tf_op jit(solution)/shard_map/ppermute | solution.py:156

commit v8 on v7

--- a/solution.py
+++ b/solution.py
@@ -127,12 +127,14 @@
     moved = moved.reshape(field_count * tile_count, TILE, TILE)
 
     chosen = slot_labels(dest_slabs, peer_count, capacity)
-    same_field = jnp.eye(field_count, dtype=jnp.bool_)
-    picker = chosen.transpose(1, 2, 0, 3)[:, :, :, None, :] & same_field[None, None, :, :, None]
-    picker = picker.astype(jnp.float32).reshape(
-        peer_count, capacity, field_count, field_count * tile_count
+    tile_ids = (
+        jnp.arange(field_count, dtype=jnp.int32)[:, None] * tile_count
+        + jnp.arange(tile_count, dtype=jnp.int32)[None, :]
     )
-    packed = jnp.einsum("pcdk,kij->pcdij", picker, moved, precision=THREE_PASS)
+    source_id = jnp.sum(chosen.astype(jnp.int32) * (tile_ids[:, None, None, :] + 1), axis=3) - 1
+    source_id = jnp.where(source_id < 0, field_count * tile_count, source_id)
+    with_blank = jnp.concatenate([moved, jnp.zeros((1, TILE, TILE), moved.dtype)], axis=0)
+    packed = jnp.take(with_blank, source_id.transpose(1, 2, 0), axis=0, mode="clip")
     moved_tiles = lax.all_to_all(packed, "perp", split_axis=0, concat_axis=0, tiled=True)
     slot_target = jnp.sum(chosen.astype(jnp.int32) * (target[:, None, None, :] + 1), axis=3) - 1
     arrived_target = lax.all_to_all(

time: 259 us -> 257 us (level)
    dot_general x1 -> x0, local copies, waits for them, and re-layouts: 3.23 us -> none  [local(): packed = jnp.einsum('pcdk,kij->pcdij', picker, moved, precision=THREE_PASS)]
    gather x0 -> x1, local copies, waits for them, and re-layouts: none -> 2.76 us  [local(): jnp.take(with_blank, source_id.transpose(1, 2, 0), axis=0, mode='clip')]
  transfers between devices with their start and end apart: 6 -> 6, of which waited for: 4 -> 4; matrix products, arithmetic and copies ran while one was open for 6% -> 5% of each run, Pallas kernels for 0% -> 0%
where the time goes in v8:
time: 257 us; the launch traced here: 256 us
  blocking collectives  138 us (54%)
  waiting for transfers between devices  64.4 us (25%)
  starting transfers between devices  27.4 us (11%)
  local copies, waits for them, and re-layouts  13.5 us (5%)
  Pallas kernels  6.31 us (2%)
  other arithmetic  3.34 us (1%)
  matrix products  3.02 us (1%)
    all_to_all x1, blocking collectives, local(): lax.all_to_all(right_side, 'par', split_axis=0, concat_axis=0, tiled=True)  77.4 us
    all_to_all x1, blocking collectives, local(): lax.all_to_all(solved, 'par', split_axis=0, concat_axis=0, tiled=True)  60.4 us
    all_to_all x1, waiting for transfers between devices, local(): lax.all_to_all(packed, 'perp', split_axis=0, concat_axis=0, tiled=True)  48.7 us
    ppermute x1, waiting for transfers between devices, local(): lax.ppermute(deposit[1], 'par', downward)  10.5 us
    all_to_all x1, starting transfers between devices, local(): lax.all_to_all(slot_target.transpose(1, 2, 0), 'perp', split_axis=0, conc...  9.13 us
    all_to_all x1, starting transfers between devices, local(): lax.all_to_all(packed, 'perp', split_axis=0, concat_axis=0, tiled=True)  7.22 us
    ppermute x1, starting transfers between devices, local(): lax.ppermute(jnp.stack([m[:1] for m in mapped]), 'perp', backward)  6.55 us
  transfers between devices with their start and end apart: 6, of which 4 were waited for; matrix products, arithmetic and copies ran while one was open for 5% of the time, Pallas kernels for 0%

profile of v8, /device:TPU:6, one launch (start us, length us, event | category | flops | bytes accessed | tf_op | source)
XLA Modules:
  0.0 256.0 jit_solution(13876772278180543403)
XLA Ops:
  0.0 0.0 copy-start
  0.0 0.0 copy-start.1
  0.0 0.1 add_add_fusion
  0.1 0.8 broadcast_add_fusion
  0.9 0.8 iota_compare_fusion
  1.6 1.0 convert_reduce_fusion
  2.6 0.1 fusion.14
  2.7 0.7 copy.17
  3.4 9.1 %all-to-all-start = ((s32[16,2,2]{1,2,0:T(2,128)}), s32[16,2,2]{1,2,0:T(2,128)S(1)}, u32[]{:S(2)}, u32[]{:S(2)}) async-start(s32[16,2,2]{1,2,0:T(2,128)} %copy.17), calls=%async_computation | async-start | bytes 32768 | tf_op jit(solution)/shard_map/all_to_all | solution.py:140
  12.5 0.8 slice_reduce_fusion
  13.3 0.1 reshape.101
  13.4 0.1 reshape.93
  13.5 0.1 copy.21
  13.6 0.1 reshape.109
  13.7 0.0 copy-done
  13.7 0.6 gather_fusion.1
  14.4 1.6 gather_fusion
  15.9 0.0 copy-done.1
  15.9 1.5 reshape_squeeze.3
  17.4 1.3 copy.20
  18.8 1.8 fusion.19
  20.6 1.2 fusion.20
  21.8 0.1 concatenate.27
  21.9 2.8 %gather_fusion.2 = f32[64,128,128]{2,1,0:T(8,128)} fusion(f32[17,128,128]{2,1,0:T(8,128)S(1)} %concatenate.27, s32[1024]{0:T(1024)S(1)} %pad_clamp_fusion), kind=kCustom, calls=%fused_computation.2 | custom fusion | bytes 8388864 | tf_op jit(solution)/shard_map/jit(_take)/gather | solution.py:137
  24.7 0.0 all-to-all-done
  24.7 7.2 %all-to-all-start.1 = ((f32[16,2,2,128,128]{4,3,2,1,0:T(8,128)}), f32[16,2,2,128,128]{4,3,2,1,0:T(8,128)}, u32[]{:S(2)}, u32[]{:S(2)}) async-start(f32[16,2,2,128,128]{4,3,2,1,0:T(8,128)} %bitcast.49), calls=%async_computation.1 | async-start | bytes 8388608 | tf_op jit(solution)/shard_map/all_to_all | solution.py:138
  31.9 0.1 copy.18
  32.0 0.1 copy.19
  32.1 0.7 min.12.label_ref
  32.8 48.7 %all-to-all-done.1 = f32[16,2,2,128,128]{4,3,2,1,0:T(8,128)} async-done(((f32[16,2,2,128,128]{4,3,2,1,0:T(8,128)}), f32[16,2,2,128,128]{4,3,2,1,0:T(8,128)}, u32[]{:S(2)}, u32[]{:S(2)}) %all-to-all-start.1) | async-done | bytes 4194336 | tf_op jit(solution)/shard_map/all_to_all | solution.py:138
  81.5 3.7 %shard_map.64 = f32[2,512,256]{2,1,0:T(8,128)} custom-call(s32[64]{0:T(128)} %min.12.label_ref, f32[64,128,128]{2,1,0:T(8,128)} %bitcast.11.recv_ref), custom_call_target="tpu_custom_call" | custom-call | tf_op jit(solution)/shard_map/pallas_call | solution.py:90
  85.2 1.3 slice_bitcast_fusion.1
  86.5 1.3 collective-permute-start
  87.8 1.3 collective-permute-start.1
  89.1 0.2 collective-permute-done
  89.3 10.5 %collective-permute-done.1 = f32[512,256]{1,0:T(8,128)S(1)} collective-permute-done((f32[512,256]{1,0:T(8,128)S(1)}, f32[512,256]{1,0:T(8,128)S(1)}, u32[]{:S(2)}, u32[]{:S(2)}) %collective-permute-start.1) | collective-permute-done | bytes 524320 | tf_op jit(solution)/shard_map/ppermute | solution.py:153
  99.8 6.6 %collective-permute-start.2 = (f32[2,1,256]{2,1,0:T(1,128)S(1)}, f32[2,1,256]{2,1,0:T(1,128)S(1)}, u32[]{:S(2)}, u32[]{:S(2)}) collective-permute-start(f32[2,1,256]{2,1,0:T(1,128)S(1)} %pad_maximum_fusion.1), channel_id=1, source_target_pairs={{1,0},{2,1},{3,2},{4,3},{5,4},{6,5},{7,6},{8,7},{9,8},{10,9},{11,1... | collective-permute-start | bytes 6152 | tf_op jit(solution)/shard_map/ppermute | solution.py:159
  106.4 1.9 collective-permute-start.3
  108.3 0.1 fusion.18
  108.4 0.2 fusion.17
  108.6 0.1 fusion.16
  108.7 0.2 fusion.15
  108.9 0.0 collective-permute-done.2
  108.9 5.1 %collective-permute-done.3 = f32[2,1,256]{2,1,0:T(1,128)S(1)} collective-permute-done((f32[2,1,256]{2,1,0:T(1,128)S(1)}, f32[2,1,256]{2,1,0:T(1,128)S(1)}, u32[]{:S(2)}, u32[]{:S(2)}) %collective-permute-start.3) | collective-permute-done | bytes 2080 | tf_op jit(solution)/shard_map/ppermute | solution.py:158
  114.0 0.5 fusion.5
  114.5 0.1 pad_maximum_fusion
  114.6 77.4 %all_to_all.20.rhs_ref = f32[32,2,16,256]{3,2,1,0:T(8,128)} all-to-all(f32[32,2,16,256]{3,2,1,0:T(8,128)S(1)} %pad_maximum_fusion), channel_id=1, replica_groups=mesh['par'=32,'perp'=16] {'par'}, dimensions={0} | all-to-all | bytes 2097152 | tf_op jit(solution)/shard_map/all_to_all | solution.py:169
  192.0 2.6 %shard_map.65 = f32[32,2,16,256]{3,2,1,0:T(8,128)} custom-call(f32[2,32]{1,0:T(2,128)} %band_ref.1, f32[32,2,16,256]{3,2,1,0:T(8,128)} %all_to_all.20.rhs_ref), custom_call_target="tpu_custom_call" | custom-call | tf_op jit(solution)/shard_map/pallas_call | solution.py:64
  194.5 60.4 %all_to_all.21 = f32[32,2,16,256]{3,2,1,0:T(8,128)S(1)} all-to-all(f32[32,2,16,256]{3,2,1,0:T(8,128)} %shard_map.65), channel_id=1, replica_groups=mesh['par'=32,'perp'=16] {'par'}, dimensions={0} | all-to-all | bytes 2097152 | tf_op jit(solution)/shard_map/all_to_all | solution.py:171
  254.9 1.1 copy.22
  (15 shorter events, 0.1 us)
Async XLA Ops:
  0.0 13.7 %copy-start = (f32[8,128,128]{2,1,0:T(8,128)S(1)}, f32[8,128,128]{2,1,0:T(8,128)}, u32[]{:S(2)}) copy-start(f32[8,128,128]{2,1,0:T(8,128)} %param.7) | copy-start | bytes 1572868
  0.0 15.9 %copy-start.1 = (f32[2,1,512,256]{3,2,1,0:T(8,128)S(1)}, f32[2,1,512,256]{3,2,1,0:T(8,128)}, u32[]{:S(2)}) copy-start(f32[2,1,512,256]{3,2,1,0:T(8,128)} %param.6) | copy-start | bytes 3145732
  3.4 21.3 %all-to-all-start = ((s32[16,2,2]{1,2,0:T(2,128)}), s32[16,2,2]{1,2,0:T(2,128)S(1)}, u32[]{:S(2)}, u32[]{:S(2)}) async-start(s32[16,2,2]{1,2,0:T(2,128)} %copy.17), calls=%async_computation | async-start | bytes 32768 | tf_op jit(solution)/shard_map/all_to_all | solution.py:140
  24.7 56.8 %all-to-all-start.1 = ((f32[16,2,2,128,128]{4,3,2,1,0:T(8,128)}), f32[16,2,2,128,128]{4,3,2,1,0:T(8,128)}, u32[]{:S(2)}, u32[]{:S(2)}) async-start(f32[16,2,2,128,128]{4,3,2,1,0:T(8,128)} %bitcast.49), calls=%async_computation.1 | async-start | bytes 8388608 | tf_op jit(solution)/shard_map/all_to_all | solution.py:138
  86.5 2.8 %collective-permute-start = (f32[512,256]{1,0:T(8,128)S(1)}, f32[512,256]{1,0:T(8,128)S(1)}, u32[]{:S(2)}, u32[]{:S(2)}) collective-permute-start(f32[512,256]{1,0:T(8,128)S(1)} %get-tuple-element.11), channel_id=1, source_target_pairs={{0,16},{16,32},{32,48},{48,64},{64,80},{80,96},{96,112},{112,128},... | collective-permute-start | bytes 1572872 | tf_op jit(solution)/shard_map/ppermute | solution.py:152
  87.8 11.9 %collective-permute-start.1 = (f32[512,256]{1,0:T(8,128)S(1)}, f32[512,256]{1,0:T(8,128)S(1)}, u32[]{:S(2)}, u32[]{:S(2)}) collective-permute-start(f32[512,256]{1,0:T(8,128)S(1)} %get-tuple-element.12), channel_id=1, source_target_pairs={{16,0},{32,16},{48,32},{64,48},{80,64},{96,80},{112,96},{128,112},... | collective-permute-start | bytes 1572872 | tf_op jit(solution)/shard_map/ppermute | solution.py:153
  99.8 9.1 %collective-permute-start.2 = (f32[2,1,256]{2,1,0:T(1,128)S(1)}, f32[2,1,256]{2,1,0:T(1,128)S(1)}, u32[]{:S(2)}, u32[]{:S(2)}) collective-permute-start(f32[2,1,256]{2,1,0:T(1,128)S(1)} %pad_maximum_fusion.1), channel_id=1, source_target_pairs={{1,0},{2,1},{3,2},{4,3},{5,4},{6,5},{7,6},{8,7},{9,8},{10,9},{11,1... | collective-permute-start | bytes 6152 | tf_op jit(solution)/shard_map/ppermute | solution.py:159
  106.4 7.6 %collective-permute-start.3 = (f32[2,1,256]{2,1,0:T(1,128)S(1)}, f32[2,1,256]{2,1,0:T(1,128)S(1)}, u32[]{:S(2)}, u32[]{:S(2)}) collective-permute-start(f32[2,1,256]{2,1,0:T(1,128)S(1)} %pad_maximum_fusion.2), channel_id=1, source_target_pairs={{0,1},{1,2},{2,3},{3,4},{4,5},{5,6},{6,7},{7,8},{8,9},{9,10},{10,1... | collective-permute-start | bytes 6152 | tf_op jit(solution)/shard_map/ppermute | solution.py:158

commit v9 on v8

--- a/solution.py
+++ b/solution.py
@@ -70,6 +70,41 @@
     )(band_terms, rhs)
 
 
+def moving_kernel(source_ref, block_ref, plane_ref, bank_ref, out_ref, moved_ref):
+    field_count = plane_ref.shape[0]
+    tiles_across = plane_ref.shape[2] // TILE
+    tile_count = (plane_ref.shape[1] // TILE) * tiles_across
+    blank = field_count * tile_count
+    moved_ref[blank] = jnp.zeros((TILE, TILE), jnp.float32)
+    for field in range(field_count):
+        for s in range(tile_count):
+            a, b = divmod(s, tiles_across)
+            tile = plane_ref[field, a * TILE:(a + 1) * TILE, b * TILE:(b + 1) * TILE]
+            left = bank_ref[block_ref[0, field * tile_count + s]]
+            right = bank_ref[block_ref[1, field * tile_count + s]]
+            shifted = jnp.dot(left, tile, precision=PRECISE, preferred_element_type=jnp.float32)
+            moved_ref[field * tile_count + s] = lax.dot_general(
+                shifted, right, (((1,), (1,)), ((), ())),
+                precision=PRECISE, preferred_element_type=jnp.float32,
+            )
+    for k in range(out_ref.shape[0]):
+        out_ref[k] = moved_ref[source_ref[k]]
+
+
+def move_and_pack(source_ids, blocks, planes, weight_bank, slot_count):
+    scalar = pl.BlockSpec(memory_space=pltpu.SMEM)
+    whole = pl.BlockSpec(memory_space=pltpu.VMEM)
+    field_count, row_count, col_count = planes.shape
+    tile_total = field_count * (row_count // TILE) * (col_count // TILE)
+    return pl.pallas_call(
+        moving_kernel,
+        out_shape=jax.ShapeDtypeStruct((slot_count, TILE, TILE), planes.dtype),
+        in_specs=[scalar, scalar, whole, whole],
+        out_specs=whole,
+        scratch_shapes=[pltpu.VMEM((tile_total + 1, TILE, TILE), jnp.float32)],
+    )(source_ids, blocks, planes, weight_bank)
+
+
 def landing_kernel(label_ref, recv_ref, out_ref, acc_ref):
     field_count = out_ref.shape[0]
     tiles_across = out_ref.shape[2] // TILE
@@ -112,20 +147,13 @@
     plane_count = lax.axis_size("par")
     field_count, _, row_count, col_count = fields.shape
     local_pair = fields[:, 0]
-    tile_set = split_tiles(local_pair)
-    tile_count = tile_set.shape[1]
+    tile_count = (row_count // TILE) * (col_count // TILE)
     capacity = max(2, (tile_count + peer_count - 1) // peer_count)
     dest_slabs = dest_slab[:, 0, :, 0]
     target = dest_tile[:, 0, :]
     left_index = tile_blocks[:, 0, :, 0]
     right_index = tile_blocks[:, 0, :, 1]
 
-    left_block = jnp.take(weight_bank, left_index, axis=0, mode="clip")
-    right_block = jnp.take(weight_bank, right_index, axis=0, mode="clip")
-    shifted = jnp.einsum("dsij,dsjk->dsik", left_block, tile_set, precision=THREE_PASS)
-    moved = jnp.einsum("dsik,dslk->dsil", shifted, right_block, precision=THREE_PASS)
-    moved = moved.reshape(field_count * tile_count, TILE, TILE)
-
     chosen = slot_labels(dest_slabs, peer_count, capacity)
     tile_ids = (
         jnp.arange(field_count, dtype=jnp.int32)[:, None] * tile_count
@@ -133,8 +161,13 @@
     )
     source_id = jnp.sum(chosen.astype(jnp.int32) * (tile_ids[:, None, None, :] + 1), axis=3) - 1
     source_id = jnp.where(source_id < 0, field_count * tile_count, source_id)
-    with_blank = jnp.concatenate([moved, jnp.zeros((1, TILE, TILE), moved.dtype)], axis=0)
-    packed = jnp.take(with_blank, source_id.transpose(1, 2, 0), axis=0, mode="clip")
+    blocks = jnp.clip(
+        jnp.stack((left_index.reshape(-1), right_index.reshape(-1))), 0, weight_bank.shape[0] - 1
+    )
+    slot_sources = source_id.transpose(1, 2, 0)
+    packed = move_and_pack(
+        slot_sources.reshape(-1), blocks, local_pair, weight_bank, slot_sources.size
+    ).reshape(slot_sources.shape + (TILE, TILE))
     moved_tiles = lax.all_to_all(packed, "perp", split_axis=0, concat_axis=0, tiled=True)
     slot_target = jnp.sum(chosen.astype(jnp.int32) * (target[:, None, None, :] + 1), axis=3) - 1
     arrived_target = lax.all_to_all(

time: 257 us -> 254 us (0.988)
  local copies, waits for them, and re-layouts: 13.5 us -> 6.12 us
  Pallas kernels: 6.31 us -> 13.6 us
  matrix products: 3.02 us -> 0 us
    pallas_call x0 -> x1, Pallas kernels: none -> 7.3 us  [move_and_pack(): pl.pallas_call(moving_kernel, out_shape=jax.ShapeDtypeStruct((slot_count,...]
    gather x3 -> x0, local copies, waits for them, and re-layouts: 4.96 us -> none  [the longest x1 2.76 us: local(): jnp.take(with_blank, source_id.transpose(1, 2, 0), axis=0, mode='clip')]
    dot_general x2 -> x0, matrix products: 3.02 us -> none  [the longest x1 1.82 us: local(): jnp.einsum('dsij,dsjk->dsik', left_block, tile_set, precision=THREE_PASS)]
  transfers between devices with their start and end apart: 6 -> 6, of which waited for: 4 -> 4; matrix products, arithmetic and copies ran while one was open for 5% -> 1% of each run, Pallas kernels for 0% -> 3%
where the time goes in v9:
time: 254 us; the launch traced here: 253 us
  blocking collectives  138 us (54%)
  waiting for transfers between devices  64.5 us (25%)
  starting transfers between devices  27.6 us (11%)
  Pallas kernels  13.6 us (5%)
  local copies, waits for them, and re-layouts  6.12 us (2%)
  other arithmetic  3.79 us (1%)
    all_to_all x1, blocking collectives, local(): lax.all_to_all(right_side, 'par', split_axis=0, concat_axis=0, tiled=True)  77.2 us
    all_to_all x1, blocking collectives, local(): lax.all_to_all(solved, 'par', split_axis=0, concat_axis=0, tiled=True)  60.4 us
    all_to_all x1, waiting for transfers between devices, local(): lax.all_to_all(packed, 'perp', split_axis=0, concat_axis=0, tiled=True)  48.6 us
    ppermute x1, waiting for transfers between devices, local(): lax.ppermute(deposit[1], 'par', downward)  10.6 us
    all_to_all x1, starting transfers between devices, local(): lax.all_to_all(slot_target.transpose(1, 2, 0), 'perp', split_axis=0, conc...  9.18 us
    pallas_call x1, Pallas kernels, move_and_pack(): pl.pallas_call(moving_kernel, out_shape=jax.ShapeDtypeStruct((slot_count,...  7.3 us
    all_to_all x1, starting transfers between devices, local(): lax.all_to_all(packed, 'perp', split_axis=0, concat_axis=0, tiled=True)  7.21 us
    ppermute x1, starting transfers between devices, local(): lax.ppermute(jnp.stack([m[:1] for m in mapped]), 'perp', backward)  6.56 us
  transfers between devices with their start and end apart: 6, of which 4 were waited for; matrix products, arithmetic and copies ran while one was open for 1% of the time, Pallas kernels for 3%

profile of v9, /device:TPU:6, one launch (start us, length us, event | category | flops | bytes accessed | tf_op | source)
XLA Modules:
  0.0 253.4 jit_solution(8580260360258664507)
XLA Ops:
  0.0 0.1 add_add_fusion
  0.1 0.7 broadcast_add_fusion
  0.8 0.8 iota_compare_fusion
  1.5 1.0 convert_reduce_fusion
  2.5 0.1 fusion.14
  2.6 0.7 copy.13
  3.3 9.2 %all-to-all-start = ((s32[16,2,2]{1,2,0:T(2,128)}), s32[16,2,2]{1,2,0:T(2,128)S(1)}, u32[]{:S(2)}, u32[]{:S(2)}) async-start(s32[16,2,2]{1,2,0:T(2,128)} %copy.13), calls=%async_computation | async-start | bytes 32768 | tf_op jit(solution)/shard_map/all_to_all | solution.py:173
  12.5 0.8 slice_reduce_fusion.1
  13.3 0.1 stack_reshape_squeeze.6
  13.3 0.1 stack_reshape_squeeze.7
  13.4 0.1 copy.16
  13.5 0.7 reshape.85.source_ref
  14.2 0.6 add_clamp_fusion.1.block_ref
  14.8 7.3 %shard_map.64 = f32[64,128,128]{2,1,0:T(8,128)} custom-call(s32[64]{0:T(128)} %reshape.85.source_ref, s32[2,16]{1,0:T(2,128)} %add_clamp_fusion.1.block_ref, f32[2,512,256]{2,1,0:T(8,128)} %bitcast.40, f32[8,128,128]{2,1,0:T(8,128)} %bank_ref.1), custom_call_target="tpu_custom_call" | custom-call | tf_op jit(solution)/shard_map/pallas_call | solution.py:99
  22.1 0.0 all-to-all-done
  22.1 7.2 %all-to-all-start.1 = ((f32[16,2,2,128,128]{4,3,2,1,0:T(8,128)}), f32[16,2,2,128,128]{4,3,2,1,0:T(8,128)}, u32[]{:S(2)}, u32[]{:S(2)}) async-start(f32[16,2,2,128,128]{4,3,2,1,0:T(8,128)} %bitcast.39), calls=%async_computation.1 | async-start | bytes 8388608 | tf_op jit(solution)/shard_map/all_to_all | solution.py:171
  29.3 0.1 copy.14
  29.4 0.1 copy.15
  29.5 0.7 min.20.label_ref
  30.1 48.6 %all-to-all-done.1 = f32[16,2,2,128,128]{4,3,2,1,0:T(8,128)} async-done(((f32[16,2,2,128,128]{4,3,2,1,0:T(8,128)}), f32[16,2,2,128,128]{4,3,2,1,0:T(8,128)}, u32[]{:S(2)}, u32[]{:S(2)}) %all-to-all-start.1) | async-done | bytes 4194336 | tf_op jit(solution)/shard_map/all_to_all | solution.py:171
  78.8 3.7 %shard_map.65 = f32[2,512,256]{2,1,0:T(8,128)} custom-call(s32[64]{0:T(128)} %min.20.label_ref, f32[64,128,128]{2,1,0:T(8,128)} %bitcast.7.recv_ref), custom_call_target="tpu_custom_call" | custom-call | tf_op jit(solution)/shard_map/pallas_call | solution.py:125
  82.5 1.3 slice_bitcast_fusion.1
  83.8 1.3 collective-permute-start
  85.1 1.3 collective-permute-start.1
  86.4 0.2 collective-permute-done
  86.6 10.6 %collective-permute-done.1 = f32[512,256]{1,0:T(8,128)S(1)} collective-permute-done((f32[512,256]{1,0:T(8,128)S(1)}, f32[512,256]{1,0:T(8,128)S(1)}, u32[]{:S(2)}, u32[]{:S(2)}) %collective-permute-start.1) | collective-permute-done | bytes 524320 | tf_op jit(solution)/shard_map/ppermute | solution.py:186
  97.2 6.6 %collective-permute-start.2 = (f32[2,1,256]{2,1,0:T(1,128)S(1)}, f32[2,1,256]{2,1,0:T(1,128)S(1)}, u32[]{:S(2)}, u32[]{:S(2)}) collective-permute-start(f32[2,1,256]{2,1,0:T(1,128)S(1)} %pad_maximum_fusion.1), channel_id=1, source_target_pairs={{1,0},{2,1},{3,2},{4,3},{5,4},{6,5},{7,6},{8,7},{9,8},{10,9},{11,1... | collective-permute-start | bytes 6152 | tf_op jit(solution)/shard_map/ppermute | solution.py:192
  103.8 0.0 copy-start
  103.8 2.1 collective-permute-start.3
  105.9 0.1 fusion.18
  106.0 0.2 fusion.17
  106.2 0.1 fusion.16
  106.3 0.2 fusion.15
  106.5 0.0 collective-permute-done.2
  106.5 5.1 %collective-permute-done.3 = f32[2,1,256]{2,1,0:T(1,128)S(1)} collective-permute-done((f32[2,1,256]{2,1,0:T(1,128)S(1)}, f32[2,1,256]{2,1,0:T(1,128)S(1)}, u32[]{:S(2)}, u32[]{:S(2)}) %collective-permute-start.3) | collective-permute-done | bytes 2080 | tf_op jit(solution)/shard_map/ppermute | solution.py:191
  111.6 0.0 copy-done
  111.6 0.5 fusion.5
  112.1 0.1 pad_maximum_fusion
  112.2 77.2 %all_to_all.20.rhs_ref = f32[32,2,16,256]{3,2,1,0:T(8,128)} all-to-all(f32[32,2,16,256]{3,2,1,0:T(8,128)S(1)} %pad_maximum_fusion), channel_id=1, replica_groups=mesh['par'=32,'perp'=16] {'par'}, dimensions={0} | all-to-all | bytes 2097152 | tf_op jit(solution)/shard_map/all_to_all | solution.py:202
  189.4 2.6 %shard_map.66 = f32[32,2,16,256]{3,2,1,0:T(8,128)} custom-call(f32[2,32]{1,0:T(2,128)} %band_ref.1, f32[32,2,16,256]{3,2,1,0:T(8,128)} %all_to_all.20.rhs_ref), custom_call_target="tpu_custom_call" | custom-call | tf_op jit(solution)/shard_map/pallas_call | solution.py:64
  192.0 60.4 %all_to_all.21 = f32[32,2,16,256]{3,2,1,0:T(8,128)S(1)} all-to-all(f32[32,2,16,256]{3,2,1,0:T(8,128)} %shard_map.66), channel_id=1, replica_groups=mesh['par'=32,'perp'=16] {'par'}, dimensions={0} | all-to-all | bytes 2097152 | tf_op jit(solution)/shard_map/all_to_all | solution.py:204
  252.4 1.1 copy.17
  (12 shorter events, 0.1 us)
Async XLA Ops:
  3.3 18.8 %all-to-all-start = ((s32[16,2,2]{1,2,0:T(2,128)}), s32[16,2,2]{1,2,0:T(2,128)S(1)}, u32[]{:S(2)}, u32[]{:S(2)}) async-start(s32[16,2,2]{1,2,0:T(2,128)} %copy.13), calls=%async_computation | async-start | bytes 32768 | tf_op jit(solution)/shard_map/all_to_all | solution.py:173
  22.1 56.7 %all-to-all-start.1 = ((f32[16,2,2,128,128]{4,3,2,1,0:T(8,128)}), f32[16,2,2,128,128]{4,3,2,1,0:T(8,128)}, u32[]{:S(2)}, u32[]{:S(2)}) async-start(f32[16,2,2,128,128]{4,3,2,1,0:T(8,128)} %bitcast.39), calls=%async_computation.1 | async-start | bytes 8388608 | tf_op jit(solution)/shard_map/all_to_all | solution.py:171
  83.8 2.8 %collective-permute-start = (f32[512,256]{1,0:T(8,128)S(1)}, f32[512,256]{1,0:T(8,128)S(1)}, u32[]{:S(2)}, u32[]{:S(2)}) collective-permute-start(f32[512,256]{1,0:T(8,128)S(1)} %get-tuple-element.11), channel_id=1, source_target_pairs={{0,16},{16,32},{32,48},{48,64},{64,80},{80,96},{96,112},{112,128},... | collective-permute-start | bytes 1572872 | tf_op jit(solution)/shard_map/ppermute | solution.py:185
  85.1 12.1 %collective-permute-start.1 = (f32[512,256]{1,0:T(8,128)S(1)}, f32[512,256]{1,0:T(8,128)S(1)}, u32[]{:S(2)}, u32[]{:S(2)}) collective-permute-start(f32[512,256]{1,0:T(8,128)S(1)} %get-tuple-element.12), channel_id=1, source_target_pairs={{16,0},{32,16},{48,32},{64,48},{80,64},{96,80},{112,96},{128,112},... | collective-permute-start | bytes 1572872 | tf_op jit(solution)/shard_map/ppermute | solution.py:186
  97.2 9.2 %collective-permute-start.2 = (f32[2,1,256]{2,1,0:T(1,128)S(1)}, f32[2,1,256]{2,1,0:T(1,128)S(1)}, u32[]{:S(2)}, u32[]{:S(2)}) collective-permute-start(f32[2,1,256]{2,1,0:T(1,128)S(1)} %pad_maximum_fusion.1), channel_id=1, source_target_pairs={{1,0},{2,1},{3,2},{4,3},{5,4},{6,5},{7,6},{8,7},{9,8},{10,9},{11,1... | collective-permute-start | bytes 6152 | tf_op jit(solution)/shard_map/ppermute | solution.py:192
  103.8 7.7 %copy-start = (f32[2,1,512,256]{3,2,1,0:T(8,128)S(1)}, f32[2,1,512,256]{3,2,1,0:T(8,128)}, u32[]{:S(2)}) copy-start(f32[2,1,512,256]{3,2,1,0:T(8,128)} %param.6) | copy-start | bytes 3145732
  103.8 7.7 %collective-permute-start.3 = (f32[2,1,256]{2,1,0:T(1,128)S(1)}, f32[2,1,256]{2,1,0:T(1,128)S(1)}, u32[]{:S(2)}, u32[]{:S(2)}) collective-permute-start(f32[2,1,256]{2,1,0:T(1,128)S(1)} %pad_maximum_fusion.2), channel_id=1, source_target_pairs={{0,1},{1,2},{2,3},{3,4},{4,5},{5,6},{6,7},{7,8},{8,9},{9,10},{10,1... | collective-permute-start | bytes 6152 | tf_op jit(solution)/shard_map/ppermute | solution.py:191

commit v10 on v9

--- a/solution.py
+++ b/solution.py
@@ -82,10 +82,10 @@
             tile = plane_ref[field, a * TILE:(a + 1) * TILE, b * TILE:(b + 1) * TILE]
             left = bank_ref[block_ref[0, field * tile_count + s]]
             right = bank_ref[block_ref[1, field * tile_count + s]]
-            shifted = jnp.dot(left, tile, precision=PRECISE, preferred_element_type=jnp.float32)
+            shifted = jnp.dot(left, tile, precision=THREE_PASS, preferred_element_type=jnp.float32)
             moved_ref[field * tile_count + s] = lax.dot_general(
                 shifted, right, (((1,), (1,)), ((), ())),
-                precision=PRECISE, preferred_element_type=jnp.float32,
+                precision=THREE_PASS, preferred_element_type=jnp.float32,
             )
     for k in range(out_ref.shape[0]):
         out_ref[k] = moved_ref[source_ref[k]]

time: 254 us -> 252 us (level)
  transfers between devices with their start and end apart: 6 -> 6, of which waited for: 4 -> 4; matrix products, arithmetic and copies ran while one was open for 1% -> 1% of each run, Pallas kernels for 3% -> 2%
where the time goes in v10:
time: 252 us
  blocking collectives  138 us (55%)
  waiting for transfers between devices  64.2 us (25%)
  starting transfers between devices  27.6 us (11%)
  Pallas kernels  12 us (5%)
  local copies, waits for them, and re-layouts  6.12 us (2%)
  other arithmetic  3.79 us (2%)
    all_to_all x1, blocking collectives, local(): lax.all_to_all(right_side, 'par', split_axis=0, concat_axis=0, tiled=True)  77.6 us
    all_to_all x1, blocking collectives, local(): lax.all_to_all(solved, 'par', split_axis=0, concat_axis=0, tiled=True)  60.4 us
    all_to_all x1, waiting for transfers between devices, local(): lax.all_to_all(packed, 'perp', split_axis=0, concat_axis=0, tiled=True)  48.7 us
    ppermute x1, waiting for transfers between devices, local(): lax.ppermute(deposit[1], 'par', downward)  10.3 us
    all_to_all x1, starting transfers between devices, local(): lax.all_to_all(slot_target.transpose(1, 2, 0), 'perp', split_axis=0, conc...  9.18 us
    all_to_all x1, starting transfers between devices, local(): lax.all_to_all(packed, 'perp', split_axis=0, concat_axis=0, tiled=True)  7.21 us
    ppermute x1, starting transfers between devices, local(): lax.ppermute(jnp.stack([m[:1] for m in mapped]), 'perp', backward)  6.56 us
    pallas_call x1, Pallas kernels, move_and_pack(): pl.pallas_call(moving_kernel, out_shape=jax.ShapeDtypeStruct((slot_count,...  5.65 us
  transfers between devices with their start and end apart: 6, of which 4 were waited for; matrix products, arithmetic and copies ran while one was open for 1% of the time, Pallas kernels for 2%

profile of v10, /device:TPU:6, one launch (start us, length us, event | category | flops | bytes accessed | tf_op | source)
XLA Modules:
  0.0 251.8 jit_solution(14797362620452324221)
XLA Ops:
  0.0 0.1 add_add_fusion
  0.1 0.7 broadcast_add_fusion
  0.8 0.8 iota_compare_fusion
  1.5 1.0 convert_reduce_fusion
  2.5 0.1 fusion.14
  2.6 0.7 copy.13
  3.3 9.2 %all-to-all-start = ((s32[16,2,2]{1,2,0:T(2,128)}), s32[16,2,2]{1,2,0:T(2,128)S(1)}, u32[]{:S(2)}, u32[]{:S(2)}) async-start(s32[16,2,2]{1,2,0:T(2,128)} %copy.13), calls=%async_computation | async-start | bytes 32768 | tf_op jit(solution)/shard_map/all_to_all | solution.py:173
  12.5 0.8 slice_reduce_fusion.1
  13.3 0.1 stack_reshape_squeeze.6
  13.3 0.1 stack_reshape_squeeze.7
  13.4 0.1 copy.16
  13.5 0.7 reshape.85.source_ref
  14.2 0.6 add_clamp_fusion.1.block_ref
  14.8 5.6 %shard_map.64 = f32[64,128,128]{2,1,0:T(8,128)} custom-call(s32[64]{0:T(128)} %reshape.85.source_ref, s32[2,16]{1,0:T(2,128)} %add_clamp_fusion.1.block_ref, f32[2,512,256]{2,1,0:T(8,128)} %bitcast.40, f32[8,128,128]{2,1,0:T(8,128)} %bank_ref.1), custom_call_target="tpu_custom_call" | custom-call | tf_op jit(solution)/shard_map/pallas_call | solution.py:99
  20.4 0.0 all-to-all-done
  20.4 7.2 %all-to-all-start.1 = ((f32[16,2,2,128,128]{4,3,2,1,0:T(8,128)}), f32[16,2,2,128,128]{4,3,2,1,0:T(8,128)}, u32[]{:S(2)}, u32[]{:S(2)}) async-start(f32[16,2,2,128,128]{4,3,2,1,0:T(8,128)} %bitcast.39), calls=%async_computation.1 | async-start | bytes 8388608 | tf_op jit(solution)/shard_map/all_to_all | solution.py:171
  27.6 0.1 copy.14
  27.7 0.1 copy.15
  27.8 0.7 min.20.label_ref
  28.5 48.7 %all-to-all-done.1 = f32[16,2,2,128,128]{4,3,2,1,0:T(8,128)} async-done(((f32[16,2,2,128,128]{4,3,2,1,0:T(8,128)}), f32[16,2,2,128,128]{4,3,2,1,0:T(8,128)}, u32[]{:S(2)}, u32[]{:S(2)}) %all-to-all-start.1) | async-done | bytes 4194336 | tf_op jit(solution)/shard_map/all_to_all | solution.py:171
  77.1 3.7 %shard_map.65 = f32[2,512,256]{2,1,0:T(8,128)} custom-call(s32[64]{0:T(128)} %min.20.label_ref, f32[64,128,128]{2,1,0:T(8,128)} %bitcast.7.recv_ref), custom_call_target="tpu_custom_call" | custom-call | tf_op jit(solution)/shard_map/pallas_call | solution.py:125
  80.9 1.3 slice_bitcast_fusion.1
  82.2 1.3 collective-permute-start
  83.5 1.3 collective-permute-start.1
  84.8 0.2 collective-permute-done
  85.0 10.3 %collective-permute-done.1 = f32[512,256]{1,0:T(8,128)S(1)} collective-permute-done((f32[512,256]{1,0:T(8,128)S(1)}, f32[512,256]{1,0:T(8,128)S(1)}, u32[]{:S(2)}, u32[]{:S(2)}) %collective-permute-start.1) | collective-permute-done | bytes 524320 | tf_op jit(solution)/shard_map/ppermute | solution.py:186
  95.3 6.6 %collective-permute-start.2 = (f32[2,1,256]{2,1,0:T(1,128)S(1)}, f32[2,1,256]{2,1,0:T(1,128)S(1)}, u32[]{:S(2)}, u32[]{:S(2)}) collective-permute-start(f32[2,1,256]{2,1,0:T(1,128)S(1)} %pad_maximum_fusion.1), channel_id=1, source_target_pairs={{1,0},{2,1},{3,2},{4,3},{5,4},{6,5},{7,6},{8,7},{9,8},{10,9},{11,1... | collective-permute-start | bytes 6152 | tf_op jit(solution)/shard_map/ppermute | solution.py:192
  101.9 0.0 copy-start
  101.9 2.1 collective-permute-start.3
  103.9 0.1 fusion.18
  104.0 0.2 fusion.17
  104.2 0.1 fusion.16
  104.3 0.2 fusion.15
  104.5 0.0 collective-permute-done.2
  104.5 5.1 %collective-permute-done.3 = f32[2,1,256]{2,1,0:T(1,128)S(1)} collective-permute-done((f32[2,1,256]{2,1,0:T(1,128)S(1)}, f32[2,1,256]{2,1,0:T(1,128)S(1)}, u32[]{:S(2)}, u32[]{:S(2)}) %collective-permute-start.3) | collective-permute-done | bytes 2080 | tf_op jit(solution)/shard_map/ppermute | solution.py:191
  109.6 0.0 copy-done
  109.6 0.5 fusion.5
  110.1 0.1 pad_maximum_fusion
  110.2 77.6 %all_to_all.20.rhs_ref = f32[32,2,16,256]{3,2,1,0:T(8,128)} all-to-all(f32[32,2,16,256]{3,2,1,0:T(8,128)S(1)} %pad_maximum_fusion), channel_id=1, replica_groups=mesh['par'=32,'perp'=16] {'par'}, dimensions={0} | all-to-all | bytes 2097152 | tf_op jit(solution)/shard_map/all_to_all | solution.py:202
  187.8 2.6 %shard_map.66 = f32[32,2,16,256]{3,2,1,0:T(8,128)} custom-call(f32[2,32]{1,0:T(2,128)} %band_ref.1, f32[32,2,16,256]{3,2,1,0:T(8,128)} %all_to_all.20.rhs_ref), custom_call_target="tpu_custom_call" | custom-call | tf_op jit(solution)/shard_map/pallas_call | solution.py:64
  190.3 60.4 %all_to_all.21 = f32[32,2,16,256]{3,2,1,0:T(8,128)S(1)} all-to-all(f32[32,2,16,256]{3,2,1,0:T(8,128)} %shard_map.66), channel_id=1, replica_groups=mesh['par'=32,'perp'=16] {'par'}, dimensions={0} | all-to-all | bytes 2097152 | tf_op jit(solution)/shard_map/all_to_all | solution.py:204
  250.7 1.1 copy.17
  (12 shorter events, 0.1 us)
Async XLA Ops:
  3.3 17.1 %all-to-all-start = ((s32[16,2,2]{1,2,0:T(2,128)}), s32[16,2,2]{1,2,0:T(2,128)S(1)}, u32[]{:S(2)}, u32[]{:S(2)}) async-start(s32[16,2,2]{1,2,0:T(2,128)} %copy.13), calls=%async_computation | async-start | bytes 32768 | tf_op jit(solution)/shard_map/all_to_all | solution.py:173
  20.4 56.7 %all-to-all-start.1 = ((f32[16,2,2,128,128]{4,3,2,1,0:T(8,128)}), f32[16,2,2,128,128]{4,3,2,1,0:T(8,128)}, u32[]{:S(2)}, u32[]{:S(2)}) async-start(f32[16,2,2,128,128]{4,3,2,1,0:T(8,128)} %bitcast.39), calls=%async_computation.1 | async-start | bytes 8388608 | tf_op jit(solution)/shard_map/all_to_all | solution.py:171
  82.2 2.8 %collective-permute-start = (f32[512,256]{1,0:T(8,128)S(1)}, f32[512,256]{1,0:T(8,128)S(1)}, u32[]{:S(2)}, u32[]{:S(2)}) collective-permute-start(f32[512,256]{1,0:T(8,128)S(1)} %get-tuple-element.11), channel_id=1, source_target_pairs={{0,16},{16,32},{32,48},{48,64},{64,80},{80,96},{96,112},{112,128},... | collective-permute-start | bytes 1572872 | tf_op jit(solution)/shard_map/ppermute | solution.py:185
  83.5 11.8 %collective-permute-start.1 = (f32[512,256]{1,0:T(8,128)S(1)}, f32[512,256]{1,0:T(8,128)S(1)}, u32[]{:S(2)}, u32[]{:S(2)}) collective-permute-start(f32[512,256]{1,0:T(8,128)S(1)} %get-tuple-element.12), channel_id=1, source_target_pairs={{16,0},{32,16},{48,32},{64,48},{80,64},{96,80},{112,96},{128,112},... | collective-permute-start | bytes 1572872 | tf_op jit(solution)/shard_map/ppermute | solution.py:186
  95.3 9.2 %collective-permute-start.2 = (f32[2,1,256]{2,1,0:T(1,128)S(1)}, f32[2,1,256]{2,1,0:T(1,128)S(1)}, u32[]{:S(2)}, u32[]{:S(2)}) collective-permute-start(f32[2,1,256]{2,1,0:T(1,128)S(1)} %pad_maximum_fusion.1), channel_id=1, source_target_pairs={{1,0},{2,1},{3,2},{4,3},{5,4},{6,5},{7,6},{8,7},{9,8},{10,9},{11,1... | collective-permute-start | bytes 6152 | tf_op jit(solution)/shard_map/ppermute | solution.py:192
  101.9 7.7 %copy-start = (f32[2,1,512,256]{3,2,1,0:T(8,128)S(1)}, f32[2,1,512,256]{3,2,1,0:T(8,128)}, u32[]{:S(2)}) copy-start(f32[2,1,512,256]{3,2,1,0:T(8,128)} %param.6) | copy-start | bytes 3145732
  101.9 7.7 %collective-permute-start.3 = (f32[2,1,256]{2,1,0:T(1,128)S(1)}, f32[2,1,256]{2,1,0:T(1,128)S(1)}, u32[]{:S(2)}, u32[]{:S(2)}) collective-permute-start(f32[2,1,256]{2,1,0:T(1,128)S(1)} %pad_maximum_fusion.2), channel_id=1, source_target_pairs={{0,1},{1,2},{2,3},{3,4},{4,5},{5,6},{6,7},{7,8},{8,9},{9,10},{10,1... | collective-permute-start | bytes 6152 | tf_op jit(solution)/shard_map/ppermute | solution.py:191

commit v11 on v10

--- a/solution.py
+++ b/solution.py
@@ -105,9 +105,10 @@
     )(source_ids, blocks, planes, weight_bank)
 
 
-def landing_kernel(label_ref, recv_ref, out_ref, acc_ref):
-    field_count = out_ref.shape[0]
-    tiles_across = out_ref.shape[2] // TILE
+def landing_kernel(label_ref, recv_ref, *refs):
+    out_refs, acc_ref = refs[:-1], refs[-1]
+    field_count = len(out_refs)
+    tiles_across = out_refs[0].shape[1] // TILE
     acc_ref[...] = jnp.zeros(acc_ref.shape, jnp.float32)
     for k in range(recv_ref.shape[0]):
         field = k % field_count
@@ -116,7 +117,7 @@
     for field in range(field_count):
         for t in range(acc_ref.shape[1] - 1):
             a, b = divmod(t, tiles_across)
-            out_ref[field, a * TILE:(a + 1) * TILE, b * TILE:(b + 1) * TILE] = acc_ref[field, t + 1]
+            out_refs[field][a * TILE:(a + 1) * TILE, b * TILE:(b + 1) * TILE] = acc_ref[field, t + 1]
 
 
 def land(labels, received, field_count, tile_count, row_count, col_count):
@@ -124,9 +125,11 @@
     whole = pl.BlockSpec(memory_space=pltpu.VMEM)
     return pl.pallas_call(
         landing_kernel,
-        out_shape=jax.ShapeDtypeStruct((field_count, row_count, col_count), received.dtype),
+        out_shape=tuple(
+            jax.ShapeDtypeStruct((row_count, col_count), received.dtype) for _ in range(field_count)
+        ),
         in_specs=[scalar, whole],
-        out_specs=whole,
+        out_specs=tuple(whole for _ in range(field_count)),
         scratch_shapes=[pltpu.VMEM((field_count, tile_count + 1, TILE, TILE), jnp.float32)],
     )(labels, received)
 

time: 252 us -> 251 us (level)
  no operation moved by 1% of the time
where the time goes in v11:
time: 251 us
  blocking collectives  138 us (55%)
  waiting for transfers between devices  64.4 us (26%)
  starting transfers between devices  27.6 us (11%)
  Pallas kernels  11.9 us (5%)
  local copies, waits for them, and re-layouts  4.85 us (2%)
  other arithmetic  3.79 us (2%)
    all_to_all x1, blocking collectives, local(): lax.all_to_all(right_side, 'par', split_axis=0, concat_axis=0, tiled=True)  77.7 us
    all_to_all x1, blocking collectives, local(): lax.all_to_all(solved, 'par', split_axis=0, concat_axis=0, tiled=True)  60.4 us
    all_to_all x1, waiting for transfers between devices, local(): lax.all_to_all(packed, 'perp', split_axis=0, concat_axis=0, tiled=True)  48.7 us
    ppermute x1, waiting for transfers between devices, local(): lax.ppermute(deposit[1], 'par', downward)  10.3 us
    all_to_all x1, starting transfers between devices, local(): lax.all_to_all(slot_target.transpose(1, 2, 0), 'perp', split_axis=0, conc...  9.18 us
    all_to_all x1, starting transfers between devices, local(): lax.all_to_all(packed, 'perp', split_axis=0, concat_axis=0, tiled=True)  7.21 us
    ppermute x1, starting transfers between devices, local(): lax.ppermute(jnp.stack([m[:1] for m in mapped]), 'perp', backward)  6.56 us
    pallas_call x1, Pallas kernels, move_and_pack(): pl.pallas_call(moving_kernel, out_shape=jax.ShapeDtypeStruct((slot_count,...  5.65 us
  transfers between devices with their start and end apart: 6, of which 4 were waited for; matrix products, arithmetic and copies ran while one was open for 1% of the time, Pallas kernels for 2%

profile of v11, /device:TPU:6, one launch (start us, length us, event | category | flops | bytes accessed | tf_op | source)
XLA Modules:
  0.0 250.8 jit_solution(12269080983265781130)
XLA Ops:
  0.0 0.1 add_add_fusion
  0.1 0.7 broadcast_add_fusion
  0.8 0.8 iota_compare_fusion
  1.5 1.0 convert_reduce_fusion
  2.5 0.1 fusion.14
  2.6 0.7 copy.13
  3.3 9.2 %all-to-all-start = ((s32[16,2,2]{1,2,0:T(2,128)}), s32[16,2,2]{1,2,0:T(2,128)S(1)}, u32[]{:S(2)}, u32[]{:S(2)}) async-start(s32[16,2,2]{1,2,0:T(2,128)} %copy.13), calls=%async_computation | async-start | bytes 32768 | tf_op jit(solution)/shard_map/all_to_all | solution.py:176
  12.5 0.8 slice_reduce_fusion.1
  13.3 0.1 stack_reshape_squeeze.6
  13.3 0.1 stack_reshape_squeeze.7
  13.4 0.1 copy.16
  13.5 0.7 reshape.85.source_ref
  14.2 0.6 add_clamp_fusion.1.block_ref
  14.8 5.6 %shard_map.64 = f32[64,128,128]{2,1,0:T(8,128)} custom-call(s32[64]{0:T(128)} %reshape.85.source_ref, s32[2,16]{1,0:T(2,128)} %add_clamp_fusion.1.block_ref, f32[2,512,256]{2,1,0:T(8,128)} %bitcast.36, f32[8,128,128]{2,1,0:T(8,128)} %bank_ref.1), custom_call_target="tpu_custom_call" | custom-call | tf_op jit(solution)/shard_map/pallas_call | solution.py:99
  20.4 0.0 all-to-all-done
  20.4 7.2 %all-to-all-start.1 = ((f32[16,2,2,128,128]{4,3,2,1,0:T(8,128)}), f32[16,2,2,128,128]{4,3,2,1,0:T(8,128)}, u32[]{:S(2)}, u32[]{:S(2)}) async-start(f32[16,2,2,128,128]{4,3,2,1,0:T(8,128)} %bitcast.35), calls=%async_computation.1 | async-start | bytes 8388608 | tf_op jit(solution)/shard_map/all_to_all | solution.py:174
  27.6 0.1 copy.14
  27.7 0.1 copy.15
  27.8 0.7 min.20.label_ref
  28.5 48.7 %all-to-all-done.1 = f32[16,2,2,128,128]{4,3,2,1,0:T(8,128)} async-done(((f32[16,2,2,128,128]{4,3,2,1,0:T(8,128)}), f32[16,2,2,128,128]{4,3,2,1,0:T(8,128)}, u32[]{:S(2)}, u32[]{:S(2)}) %all-to-all-start.1) | async-done | bytes 4194336 | tf_op jit(solution)/shard_map/all_to_all | solution.py:174
  77.1 3.7 %shard_map.65 = (f32[512,256]{1,0:T(8,128)}, f32[512,256]{1,0:T(8,128)}) custom-call(s32[64]{0:T(128)} %min.20.label_ref, f32[64,128,128]{2,1,0:T(8,128)} %bitcast.7.recv_ref), custom_call_target="tpu_custom_call" | custom-call | tf_op jit(solution)/shard_map/pallas_call | solution.py:126
  80.8 1.3 collective-permute-start
  82.2 1.3 collective-permute-start.1
  83.5 0.4 collective-permute-done
  83.9 10.3 %collective-permute-done.1 = f32[512,256]{1,0:T(8,128)S(1)} collective-permute-done((f32[512,256]{1,0:T(8,128)}, f32[512,256]{1,0:T(8,128)S(1)}, u32[]{:S(2)}, u32[]{:S(2)}) %collective-permute-start.1) | collective-permute-done | bytes 524320 | tf_op jit(solution)/shard_map/ppermute | solution.py:189
  94.2 6.6 %collective-permute-start.2 = (f32[2,1,256]{2,1,0:T(1,128)S(1)}, f32[2,1,256]{2,1,0:T(1,128)S(1)}, u32[]{:S(2)}, u32[]{:S(2)}) collective-permute-start(f32[2,1,256]{2,1,0:T(1,128)S(1)} %pad_maximum_fusion.1), channel_id=1, source_target_pairs={{1,0},{2,1},{3,2},{4,3},{5,4},{6,5},{7,6},{8,7},{9,8},{10,9},{11,1... | collective-permute-start | bytes 6152 | tf_op jit(solution)/shard_map/ppermute | solution.py:195
  100.7 0.0 copy-start
  100.8 2.1 collective-permute-start.3
  102.8 0.1 fusion.18
  102.9 0.2 fusion.17
  103.1 0.1 fusion.16
  103.2 0.2 fusion.15
  103.4 0.0 collective-permute-done.2
  103.4 5.1 %collective-permute-done.3 = f32[2,1,256]{2,1,0:T(1,128)S(1)} collective-permute-done((f32[2,1,256]{2,1,0:T(1,128)S(1)}, f32[2,1,256]{2,1,0:T(1,128)S(1)}, u32[]{:S(2)}, u32[]{:S(2)}) %collective-permute-start.3) | collective-permute-done | bytes 2080 | tf_op jit(solution)/shard_map/ppermute | solution.py:194
  108.5 0.0 copy-done
  108.5 0.5 fusion.5
  109.0 0.1 pad_maximum_fusion
  109.1 77.7 %all_to_all.20.rhs_ref = f32[32,2,16,256]{3,2,1,0:T(8,128)} all-to-all(f32[32,2,16,256]{3,2,1,0:T(8,128)S(1)} %pad_maximum_fusion), channel_id=1, replica_groups=mesh['par'=32,'perp'=16] {'par'}, dimensions={0} | all-to-all | bytes 2097152 | tf_op jit(solution)/shard_map/all_to_all | solution.py:205
  186.8 2.6 %shard_map.66 = f32[32,2,16,256]{3,2,1,0:T(8,128)} custom-call(f32[2,32]{1,0:T(2,128)} %band_ref.1, f32[32,2,16,256]{3,2,1,0:T(8,128)} %all_to_all.20.rhs_ref), custom_call_target="tpu_custom_call" | custom-call | tf_op jit(solution)/shard_map/pallas_call | solution.py:64
  189.3 60.4 %all_to_all.21 = f32[32,2,16,256]{3,2,1,0:T(8,128)S(1)} all-to-all(f32[32,2,16,256]{3,2,1,0:T(8,128)} %shard_map.66), channel_id=1, replica_groups=mesh['par'=32,'perp'=16] {'par'}, dimensions={0} | all-to-all | bytes 2097152 | tf_op jit(solution)/shard_map/all_to_all | solution.py:207
  249.7 1.1 copy.17
  (12 shorter events, 0.1 us)
Async XLA Ops:
  3.3 17.1 %all-to-all-start = ((s32[16,2,2]{1,2,0:T(2,128)}), s32[16,2,2]{1,2,0:T(2,128)S(1)}, u32[]{:S(2)}, u32[]{:S(2)}) async-start(s32[16,2,2]{1,2,0:T(2,128)} %copy.13), calls=%async_computation | async-start | bytes 32768 | tf_op jit(solution)/shard_map/all_to_all | solution.py:176
  20.4 56.7 %all-to-all-start.1 = ((f32[16,2,2,128,128]{4,3,2,1,0:T(8,128)}), f32[16,2,2,128,128]{4,3,2,1,0:T(8,128)}, u32[]{:S(2)}, u32[]{:S(2)}) async-start(f32[16,2,2,128,128]{4,3,2,1,0:T(8,128)} %bitcast.35), calls=%async_computation.1 | async-start | bytes 8388608 | tf_op jit(solution)/shard_map/all_to_all | solution.py:174
  80.8 3.0 %collective-permute-start = (f32[512,256]{1,0:T(8,128)}, f32[512,256]{1,0:T(8,128)S(1)}, u32[]{:S(2)}, u32[]{:S(2)}) collective-permute-start(f32[512,256]{1,0:T(8,128)} %get-tuple-element.7), channel_id=1, source_target_pairs={{0,16},{16,32},{32,48},{48,64},{64,80},{80,96},{96,112},{112,128},... | collective-permute-start | bytes 1572872 | tf_op jit(solution)/shard_map/ppermute | solution.py:188
  82.2 12.0 %collective-permute-start.1 = (f32[512,256]{1,0:T(8,128)}, f32[512,256]{1,0:T(8,128)S(1)}, u32[]{:S(2)}, u32[]{:S(2)}) collective-permute-start(f32[512,256]{1,0:T(8,128)} %get-tuple-element.8), channel_id=1, source_target_pairs={{16,0},{32,16},{48,32},{64,48},{80,64},{96,80},{112,96},{128,112},... | collective-permute-start | bytes 1572872 | tf_op jit(solution)/shard_map/ppermute | solution.py:189
  94.2 9.2 %collective-permute-start.2 = (f32[2,1,256]{2,1,0:T(1,128)S(1)}, f32[2,1,256]{2,1,0:T(1,128)S(1)}, u32[]{:S(2)}, u32[]{:S(2)}) collective-permute-start(f32[2,1,256]{2,1,0:T(1,128)S(1)} %pad_maximum_fusion.1), channel_id=1, source_target_pairs={{1,0},{2,1},{3,2},{4,3},{5,4},{6,5},{7,6},{8,7},{9,8},{10,9},{11,1... | collective-permute-start | bytes 6152 | tf_op jit(solution)/shard_map/ppermute | solution.py:195
  100.7 7.7 %copy-start = (f32[2,1,512,256]{3,2,1,0:T(8,128)S(1)}, f32[2,1,512,256]{3,2,1,0:T(8,128)}, u32[]{:S(2)}) copy-start(f32[2,1,512,256]{3,2,1,0:T(8,128)} %param.6) | copy-start | bytes 3145732
  100.8 7.7 %collective-permute-start.3 = (f32[2,1,256]{2,1,0:T(1,128)S(1)}, f32[2,1,256]{2,1,0:T(1,128)S(1)}, u32[]{:S(2)}, u32[]{:S(2)}) collective-permute-start(f32[2,1,256]{2,1,0:T(1,128)S(1)} %pad_maximum_fusion.2), channel_id=1, source_target_pairs={{0,1},{1,2},{2,3},{3,4},{4,5},{5,6},{6,7},{7,8},{8,9},{9,10},{10,1... | collective-permute-start | bytes 6152 | tf_op jit(solution)/shard_map/ppermute | solution.py:194

commit v12 on v11

--- a/solution.py
+++ b/solution.py
@@ -70,12 +70,11 @@
     )(band_terms, rhs)
 
 
-def moving_kernel(source_ref, block_ref, plane_ref, bank_ref, out_ref, moved_ref):
+def moving_kernel(slot_ref, block_ref, plane_ref, bank_ref, out_ref):
     field_count = plane_ref.shape[0]
     tiles_across = plane_ref.shape[2] // TILE
     tile_count = (plane_ref.shape[1] // TILE) * tiles_across
-    blank = field_count * tile_count
-    moved_ref[blank] = jnp.zeros((TILE, TILE), jnp.float32)
+    out_ref[...] = jnp.zeros(out_ref.shape, jnp.float32)
     for field in range(field_count):
         for s in range(tile_count):
             a, b = divmod(s, tiles_across)
@@ -83,26 +82,21 @@
             left = bank_ref[block_ref[0, field * tile_count + s]]
             right = bank_ref[block_ref[1, field * tile_count + s]]
             shifted = jnp.dot(left, tile, precision=THREE_PASS, preferred_element_type=jnp.float32)
-            moved_ref[field * tile_count + s] = lax.dot_general(
+            out_ref[slot_ref[field * tile_count + s]] = lax.dot_general(
                 shifted, right, (((1,), (1,)), ((), ())),
                 precision=THREE_PASS, preferred_element_type=jnp.float32,
             )
-    for k in range(out_ref.shape[0]):
-        out_ref[k] = moved_ref[source_ref[k]]
-
-
-def move_and_pack(source_ids, blocks, planes, weight_bank, slot_count):
+
+
+def move_and_pack(slot_ids, blocks, planes, weight_bank, slot_count):
     scalar = pl.BlockSpec(memory_space=pltpu.SMEM)
     whole = pl.BlockSpec(memory_space=pltpu.VMEM)
-    field_count, row_count, col_count = planes.shape
-    tile_total = field_count * (row_count // TILE) * (col_count // TILE)
     return pl.pallas_call(
         moving_kernel,
         out_shape=jax.ShapeDtypeStruct((slot_count, TILE, TILE), planes.dtype),
         in_specs=[scalar, scalar, whole, whole],
         out_specs=whole,
-        scratch_shapes=[pltpu.VMEM((tile_total + 1, TILE, TILE), jnp.float32)],
-    )(source_ids, blocks, planes, weight_bank)
+    )(slot_ids, blocks, planes, weight_bank)
 
 
 def landing_kernel(label_ref, recv_ref, *refs):
@@ -158,19 +152,17 @@
     right_index = tile_blocks[:, 0, :, 1]
 
     chosen = slot_labels(dest_slabs, peer_count, capacity)
-    tile_ids = (
-        jnp.arange(field_count, dtype=jnp.int32)[:, None] * tile_count
-        + jnp.arange(tile_count, dtype=jnp.int32)[None, :]
-    )
-    source_id = jnp.sum(chosen.astype(jnp.int32) * (tile_ids[:, None, None, :] + 1), axis=3) - 1
-    source_id = jnp.where(source_id < 0, field_count * tile_count, source_id)
+    slot_ids = jnp.arange(peer_count * capacity, dtype=jnp.int32).reshape(peer_count, capacity)
+    slot_ids = slot_ids[None] * field_count + jnp.arange(field_count, dtype=jnp.int32)[:, None, None]
+    tile_slot = jnp.sum(chosen.astype(jnp.int32) * slot_ids[..., None], axis=(1, 2))
+    slot_count = peer_count * capacity * field_count
+    tile_slot = jnp.clip(tile_slot, 0, slot_count - 1)
     blocks = jnp.clip(
         jnp.stack((left_index.reshape(-1), right_index.reshape(-1))), 0, weight_bank.shape[0] - 1
     )
-    slot_sources = source_id.transpose(1, 2, 0)
     packed = move_and_pack(
-        slot_sources.reshape(-1), blocks, local_pair, weight_bank, slot_sources.size
-    ).reshape(slot_sources.shape + (TILE, TILE))
+        tile_slot.reshape(-1), blocks, local_pair, weight_bank, slot_count
+    ).reshape(peer_count, capacity, field_count, TILE, TILE)
     moved_tiles = lax.all_to_all(packed, "perp", split_axis=0, concat_axis=0, tiled=True)
     slot_target = jnp.sum(chosen.astype(jnp.int32) * (target[:, None, None, :] + 1), axis=3) - 1
     arrived_target = lax.all_to_all(

time: 251 us -> 251 us (level)
  no operation moved by 1% of the time
where the time goes in v12:
time: 251 us
  blocking collectives  138 us (55%)
  waiting for transfers between devices  64.4 us (26%)
  starting transfers between devices  27.6 us (11%)
  Pallas kernels  11.9 us (5%)
  local copies, waits for them, and re-layouts  4.72 us (2%)
  other arithmetic  3.82 us (2%)
    all_to_all x1, blocking collectives, local(): lax.all_to_all(right_side, 'par', split_axis=0, concat_axis=0, tiled=True)  77.7 us
    all_to_all x1, blocking collectives, local(): lax.all_to_all(solved, 'par', split_axis=0, concat_axis=0, tiled=True)  60.4 us
    all_to_all x1, waiting for transfers between devices, local(): lax.all_to_all(packed, 'perp', split_axis=0, concat_axis=0, tiled=True)  48.7 us
    ppermute x1, waiting for transfers between devices, local(): lax.ppermute(deposit[1], 'par', downward)  10.3 us
    all_to_all x1, starting transfers between devices, local(): lax.all_to_all(slot_target.transpose(1, 2, 0), 'perp', split_axis=0, conc...  9.18 us
    all_to_all x1, starting transfers between devices, local(): lax.all_to_all(packed, 'perp', split_axis=0, concat_axis=0, tiled=True)  7.21 us
    ppermute x1, starting transfers between devices, local(): lax.ppermute(jnp.stack([m[:1] for m in mapped]), 'perp', backward)  6.56 us
    pallas_call x1, Pallas kernels, move_and_pack(): pl.pallas_call(moving_kernel, out_shape=jax.ShapeDtypeStruct((slot_count,...  5.66 us
  transfers between devices with their start and end apart: 6, of which 4 were waited for; matrix products, arithmetic and copies ran while one was open for 1% of the time, Pallas kernels for 2%

profile of v12, /device:TPU:6, one launch (start us, length us, event | category | flops | bytes accessed | tf_op | source)
XLA Modules:
  0.0 250.7 jit_solution(6899517173720575980)
XLA Ops:
  0.0 0.7 broadcast_add_fusion
  0.7 0.8 iota_compare_fusion
  1.5 1.0 convert_reduce_fusion
  2.4 0.2 fusion.14
  2.6 0.7 copy.16
  3.3 9.2 %all-to-all-start = ((s32[16,2,2]{1,2,0:T(2,128)}), s32[16,2,2]{1,2,0:T(2,128)S(1)}, u32[]{:S(2)}, u32[]{:S(2)}) async-start(s32[16,2,2]{1,2,0:T(2,128)} %copy.16), calls=%async_computation | async-start | bytes 32768 | tf_op jit(solution)/shard_map/all_to_all | solution.py:168
  12.5 0.6 min.33.slot_ref
  13.1 0.8 slice_reduce_fusion.1
  13.9 0.1 stack_reshape_squeeze.6
  14.0 0.1 stack_reshape_squeeze.7
  14.1 0.6 add_clamp_fusion.1.block_ref
  14.7 5.7 %shard_map.64 = f32[64,128,128]{2,1,0:T(8,128)} custom-call(s32[16]{0:T(128)} %min.33.slot_ref, s32[2,16]{1,0:T(2,128)} %add_clamp_fusion.1.block_ref, f32[2,512,256]{2,1,0:T(8,128)} %bitcast.34, f32[8,128,128]{2,1,0:T(8,128)} %bank_ref.1), custom_call_target="tpu_custom_call" | custom-call | tf_op jit(solution)/shard_map/pallas_call | solution.py:94
  20.3 0.0 all-to-all-done
  20.3 7.2 %all-to-all-start.1 = ((f32[16,2,2,128,128]{4,3,2,1,0:T(8,128)}), f32[16,2,2,128,128]{4,3,2,1,0:T(8,128)}, u32[]{:S(2)}, u32[]{:S(2)}) async-start(f32[16,2,2,128,128]{4,3,2,1,0:T(8,128)} %bitcast.33), calls=%async_computation.1 | async-start | bytes 8388608 | tf_op jit(solution)/shard_map/all_to_all | solution.py:166
  27.5 0.1 copy.17
  27.6 0.1 copy.18
  27.7 0.7 min.30.label_ref
  28.4 48.7 %all-to-all-done.1 = f32[16,2,2,128,128]{4,3,2,1,0:T(8,128)} async-done(((f32[16,2,2,128,128]{4,3,2,1,0:T(8,128)}), f32[16,2,2,128,128]{4,3,2,1,0:T(8,128)}, u32[]{:S(2)}, u32[]{:S(2)}) %all-to-all-start.1) | async-done | bytes 4194336 | tf_op jit(solution)/shard_map/all_to_all | solution.py:166
  77.0 3.7 %shard_map.65 = (f32[512,256]{1,0:T(8,128)}, f32[512,256]{1,0:T(8,128)}) custom-call(s32[64]{0:T(128)} %min.30.label_ref, f32[64,128,128]{2,1,0:T(8,128)} %bitcast.6.recv_ref), custom_call_target="tpu_custom_call" | custom-call | tf_op jit(solution)/shard_map/pallas_call | solution.py:120
  80.8 1.3 collective-permute-start
  82.1 1.3 collective-permute-start.1
  83.4 0.4 collective-permute-done
  83.8 10.3 %collective-permute-done.1 = f32[512,256]{1,0:T(8,128)S(1)} collective-permute-done((f32[512,256]{1,0:T(8,128)}, f32[512,256]{1,0:T(8,128)S(1)}, u32[]{:S(2)}, u32[]{:S(2)}) %collective-permute-start.1) | collective-permute-done | bytes 524320 | tf_op jit(solution)/shard_map/ppermute | solution.py:181
  94.1 6.6 %collective-permute-start.2 = (f32[2,1,256]{2,1,0:T(1,128)S(1)}, f32[2,1,256]{2,1,0:T(1,128)S(1)}, u32[]{:S(2)}, u32[]{:S(2)}) collective-permute-start(f32[2,1,256]{2,1,0:T(1,128)S(1)} %pad_maximum_fusion.1), channel_id=1, source_target_pairs={{1,0},{2,1},{3,2},{4,3},{5,4},{6,5},{7,6},{8,7},{9,8},{10,9},{11,1... | collective-permute-start | bytes 6152 | tf_op jit(solution)/shard_map/ppermute | solution.py:187
  100.7 0.0 copy-start
  100.7 2.1 collective-permute-start.3
  102.7 0.1 fusion.18
  102.8 0.2 fusion.17
  103.0 0.1 fusion.16
  103.1 0.2 fusion.15
  103.3 0.0 collective-permute-done.2
  103.3 5.1 %collective-permute-done.3 = f32[2,1,256]{2,1,0:T(1,128)S(1)} collective-permute-done((f32[2,1,256]{2,1,0:T(1,128)S(1)}, f32[2,1,256]{2,1,0:T(1,128)S(1)}, u32[]{:S(2)}, u32[]{:S(2)}) %collective-permute-start.3) | collective-permute-done | bytes 2080 | tf_op jit(solution)/shard_map/ppermute | solution.py:186
  108.4 0.0 copy-done
  108.4 0.5 fusion.5
  108.9 0.1 pad_maximum_fusion
  109.0 77.7 %all_to_all.20.rhs_ref = f32[32,2,16,256]{3,2,1,0:T(8,128)} all-to-all(f32[32,2,16,256]{3,2,1,0:T(8,128)S(1)} %pad_maximum_fusion), channel_id=1, replica_groups=mesh['par'=32,'perp'=16] {'par'}, dimensions={0} | all-to-all | bytes 2097152 | tf_op jit(solution)/shard_map/all_to_all | solution.py:197
  186.7 2.6 %shard_map.66 = f32[32,2,16,256]{3,2,1,0:T(8,128)} custom-call(f32[2,32]{1,0:T(2,128)} %band_ref.1, f32[32,2,16,256]{3,2,1,0:T(8,128)} %all_to_all.20.rhs_ref), custom_call_target="tpu_custom_call" | custom-call | tf_op jit(solution)/shard_map/pallas_call | solution.py:64
  189.2 60.4 %all_to_all.21 = f32[32,2,16,256]{3,2,1,0:T(8,128)S(1)} all-to-all(f32[32,2,16,256]{3,2,1,0:T(8,128)} %shard_map.66), channel_id=1, replica_groups=mesh['par'=32,'perp'=16] {'par'}, dimensions={0} | all-to-all | bytes 2097152 | tf_op jit(solution)/shard_map/all_to_all | solution.py:199
  249.6 1.1 copy.19
  (13 shorter events, 0.1 us)
Async XLA Ops:
  3.3 17.0 %all-to-all-start = ((s32[16,2,2]{1,2,0:T(2,128)}), s32[16,2,2]{1,2,0:T(2,128)S(1)}, u32[]{:S(2)}, u32[]{:S(2)}) async-start(s32[16,2,2]{1,2,0:T(2,128)} %copy.16), calls=%async_computation | async-start | bytes 32768 | tf_op jit(solution)/shard_map/all_to_all | solution.py:168
  20.3 56.7 %all-to-all-start.1 = ((f32[16,2,2,128,128]{4,3,2,1,0:T(8,128)}), f32[16,2,2,128,128]{4,3,2,1,0:T(8,128)}, u32[]{:S(2)}, u32[]{:S(2)}) async-start(f32[16,2,2,128,128]{4,3,2,1,0:T(8,128)} %bitcast.33), calls=%async_computation.1 | async-start | bytes 8388608 | tf_op jit(solution)/shard_map/all_to_all | solution.py:166
  80.8 3.0 %collective-permute-start = (f32[512,256]{1,0:T(8,128)}, f32[512,256]{1,0:T(8,128)S(1)}, u32[]{:S(2)}, u32[]{:S(2)}) collective-permute-start(f32[512,256]{1,0:T(8,128)} %get-tuple-element.7), channel_id=1, source_target_pairs={{0,16},{16,32},{32,48},{48,64},{64,80},{80,96},{96,112},{112,128},... | collective-permute-start | bytes 1572872 | tf_op jit(solution)/shard_map/ppermute | solution.py:180
  82.1 12.0 %collective-permute-start.1 = (f32[512,256]{1,0:T(8,128)}, f32[512,256]{1,0:T(8,128)S(1)}, u32[]{:S(2)}, u32[]{:S(2)}) collective-permute-start(f32[512,256]{1,0:T(8,128)} %get-tuple-element.8), channel_id=1, source_target_pairs={{16,0},{32,16},{48,32},{64,48},{80,64},{96,80},{112,96},{128,112},... | collective-permute-start | bytes 1572872 | tf_op jit(solution)/shard_map/ppermute | solution.py:181
  94.1 9.2 %collective-permute-start.2 = (f32[2,1,256]{2,1,0:T(1,128)S(1)}, f32[2,1,256]{2,1,0:T(1,128)S(1)}, u32[]{:S(2)}, u32[]{:S(2)}) collective-permute-start(f32[2,1,256]{2,1,0:T(1,128)S(1)} %pad_maximum_fusion.1), channel_id=1, source_target_pairs={{1,0},{2,1},{3,2},{4,3},{5,4},{6,5},{7,6},{8,7},{9,8},{10,9},{11,1... | collective-permute-start | bytes 6152 | tf_op jit(solution)/shard_map/ppermute | solution.py:187
  100.7 7.7 %copy-start = (f32[2,1,512,256]{3,2,1,0:T(8,128)S(1)}, f32[2,1,512,256]{3,2,1,0:T(8,128)}, u32[]{:S(2)}) copy-start(f32[2,1,512,256]{3,2,1,0:T(8,128)} %param.6) | copy-start | bytes 3145732
  100.7 7.7 %collective-permute-start.3 = (f32[2,1,256]{2,1,0:T(1,128)S(1)}, f32[2,1,256]{2,1,0:T(1,128)S(1)}, u32[]{:S(2)}, u32[]{:S(2)}) collective-permute-start(f32[2,1,256]{2,1,0:T(1,128)S(1)} %pad_maximum_fusion.2), channel_id=1, source_target_pairs={{0,1},{1,2},{2,3},{3,4},{4,5},{5,6},{6,7},{7,8},{8,9},{9,10},{10,1... | collective-permute-start | bytes 6152 | tf_op jit(solution)/shard_map/ppermute | solution.py:186
